TPU v7x, 32 devices: a whole 2x2x4 slice. The times are simulated.
32 devices in a mesh: dp: 32 (over z, y, x, core), mp: 1.
Axes of the slice: x: 2, y: 2, z: 4, core: 2. Of those that a mesh axis runs over, the one named last changes fastest.
Arguments:
- pre_tokens: bfloat16 [16384, 1024], P(('dp', 'mp')), may hold values from -6 to 6
- dec_tokens: bfloat16 [128, 1024], P(('dp', 'mp')), may hold values from -6 to 6
- deal_slots: int32 [128], replicated, may hold values from 0 to 127, as said below
- dec_lengths: int32 [128], P('dp'), may hold values from 1 to 256, as said below
- pre_offsets: int32 [32], P('dp'), may hold values from 0 to 1024, as said below
- dec_cache: bfloat16 [8, 128, 256, 128], P('mp', 'dp'), may hold values from -420 to 420, as said below
- prior_cache: bfloat16 [8, 32, 1024, 128], P('mp', 'dp'), may hold values from -420 to 420, as said below
- attn_gain: float32 [1024], replicated, may hold values from 0.5 to 2
- moe_gain: float32 [1024], replicated, may hold values from 0.5 to 2
- qkv_weight: bfloat16 [1024, 2048], P('dp', 'mp'), may hold values from -0.1875 to 0.1875
- out_weight: bfloat16 [1024, 1024], P('mp', 'dp'), may hold values from -0.1875 to 0.1875
- gate_up: bfloat16 [32, 1024, 1024], P(None, 'dp', 'mp'), may hold values from -0.1875 to 0.1875
- down_weight: bfloat16 [32, 512, 1024], P(None, 'dp', 'mp'), may hold values from -0.25 to 0.25
- routes: int32 [16512, 8], P(('dp', 'mp')), may hold values from 0 to 31, all different within a row; in each aligned block of 516 rows (0 to 515, 516 to 1031, ...) at most 172 rows name the same one
- route_gates: bfloat16 [16512, 8], P(('dp', 'mp')), may hold values from 0.019897461 to 0.29882812
Outputs:
- hidden: bfloat16 [16512, 1024], P(('dp', 'mp'))
Inputs may be any that keep to these rules, and one draw needn't show every extreme that they name: deal_slots is a permutation of the decode slots; a request keeps its index in mp and its position among the 4 requests of a device; the positions of one device form aligned blocks of 1 that go to one group each, different blocks to different groups. `dec_lengths`: in every draw some slot has exactly 256 cached positions. `pre_offsets`: in every draw some group has exactly 1024 cached positions before its prefill tokens. `dec_cache`: keys hold the first 64 entries of the last dimension, values the rest. `prior_cache`: keys hold the first 64 entries of the last dimension, values the rest. `routes`: each row names 8 different experts; within the 516 rows of one device no expert is named by more than 172 rows, a bound that some block reaches.
All inputs are finite; a program needn't handle non-finite values.
Results may differ from a plain program's by a relative error of at most 0.019.
Values may be sent and summed in bfloat16 or wider, within the bound.
No kernel may reach another device: no remote copies, remote signals or barrier semaphores. Data moves between devices by JAX's collectives and lax.ppermute only.
A program may use at most 128 MiB of HBM per device.

v0:
```python
import jax
import jax.numpy as jnp
from jax import lax
from jax.sharding import PartitionSpec as P

EPSILON = 1e-06
ROTARY_BASE = 10000.0
SCORE_SCALE = 0.015625


def root_norm(values, gain):
    mean_square = jnp.mean(values * values, axis=-1, keepdims=True)
    return values * lax.rsqrt(mean_square + EPSILON) * gain


def rotary(vectors, positions):
    halfway = vectors.shape[-1] // 2
    freq_table = ROTARY_BASE ** (-jnp.arange(halfway).astype(jnp.float32) / halfway)
    angles = positions[..., None] * freq_table
    cosine = jnp.cos(angles)
    sine_part = jnp.sin(angles)
    leading = vectors[..., :halfway]
    trailing = vectors[..., halfway:]
    return jnp.concatenate(
        [leading * cosine - trailing * sine_part, trailing * cosine + leading * sine_part], axis=-1
    )


def split_heads(projected, positions, head_dim):
    per_group = projected.shape[-1] // head_dim - 2
    row_count = projected.shape[0]
    group_count = projected.shape[1]
    queries = projected[..., : per_group * head_dim].reshape(
        row_count, group_count, per_group, head_dim
    )
    key_rows = projected[..., per_group * head_dim : (per_group + 1) * head_dim]
    value_rows = projected[..., (per_group + 1) * head_dim :]
    queries = rotary(queries, positions[:, None, None]).astype(jnp.bfloat16)
    key_rows = rotary(key_rows, positions[:, None]).astype(jnp.bfloat16)
    return (queries, key_rows, value_rows.astype(jnp.bfloat16))


def prefill_attention(queries, key_rows, value_rows, prior, offset):
    head_dim = queries.shape[-1]
    row_count = queries.shape[0]
    span = prior.shape[1]
    all_keys = jnp.concatenate([prior[:, :, :head_dim], jnp.swapaxes(key_rows, 0, 1)], axis=1)
    all_values = jnp.concatenate([prior[:, :, head_dim:], jnp.swapaxes(value_rows, 0, 1)], axis=1)
    scores = (
        jnp.einsum("cgph,gkh->gpck", queries, all_keys, preferred_element_type=jnp.float32)
        * SCORE_SCALE
    )
    column = jnp.arange(span + row_count)
    row_ids = jnp.arange(row_count)
    allowed = jnp.where(
        column[None, :] < span, column[None, :] < offset, column[None, :] - span <= row_ids[:, None]
    )
    scores = jnp.where(allowed, scores, -jnp.inf)
    highest = jnp.max(scores, axis=-1, keepdims=True)
    expo = jnp.exp(scores - highest)
    weights = (expo / jnp.sum(expo, axis=-1, keepdims=True)).astype(jnp.bfloat16)
    mixed = jnp.einsum("gpck,gkh->cgph", weights, all_values, preferred_element_type=jnp.float32)
    return mixed.astype(jnp.bfloat16)


def decode_attention(queries, key_rows, value_rows, cache, lengths):
    head_dim = queries.shape[-1]
    cached = (
        jnp.einsum(
            "sgph,gslh->sgpl", queries, cache[..., :head_dim], preferred_element_type=jnp.float32
        )
        * SCORE_SCALE
    )
    own_score = (
        jnp.einsum("sgph,sgh->sgp", queries, key_rows, preferred_element_type=jnp.float32)
        * SCORE_SCALE
    )
    valid = jnp.arange(cache.shape[2])[None, :] < lengths[:, None]
    cached = jnp.where(valid[:, None, None, :], cached, -jnp.inf)
    highest = jnp.maximum(jnp.max(cached, axis=-1), own_score)
    expo = jnp.exp(cached - highest[..., None])
    own_expo = jnp.exp(own_score - highest)
    total = jnp.sum(expo, axis=-1) + own_expo
    weights = (expo / total[..., None]).astype(jnp.bfloat16)
    own_weight = (own_expo / total).astype(jnp.bfloat16)
    mixed = jnp.einsum(
        "sgpl,gslh->sgph", weights, cache[..., head_dim:], preferred_element_type=jnp.float32
    )
    mixed = (
        mixed
        + own_weight.astype(jnp.float32)[..., None] * value_rows.astype(jnp.float32)[:, :, None, :]
    )
    return mixed.astype(jnp.bfloat16)


def group_attention(projected, prior, cache, lengths, offset, pre_rows, head_dim):
    part_count = projected.shape[0]
    pre_part = projected[:, :pre_rows].reshape((-1,) + projected.shape[2:])
    dec_part = projected[:, pre_rows:].reshape((-1,) + projected.shape[2:])
    pre_pos = (offset + jnp.arange(pre_part.shape[0], dtype=jnp.int32)).astype(jnp.float32)
    dec_pos = lengths.astype(jnp.float32)
    queries, key_rows, value_rows = split_heads(pre_part, pre_pos, head_dim)
    pre_out = prefill_attention(queries, key_rows, value_rows, prior, offset)
    queries, key_rows, value_rows = split_heads(dec_part, dec_pos, head_dim)
    dec_out = decode_attention(queries, key_rows, value_rows, cache, lengths)
    columns = pre_out.shape[1] * pre_out.shape[2] * pre_out.shape[3]
    pre_out = pre_out.reshape(part_count, pre_rows, columns)
    dec_out = dec_out.reshape(part_count, -1, columns)
    return jnp.concatenate([pre_out, dec_out], axis=1).reshape(-1, columns)


def local(
    pre_tokens,
    dec_tokens,
    deal_slots,
    dec_lengths,
    pre_offsets,
    dec_cache,
    prior_cache,
    attn_gain,
    moe_gain,
    qkv_weight,
    out_weight,
    gate_up,
    down_weight,
    routes,
    route_gates,
):
    group_count = lax.axis_size("dp")
    part_count = lax.axis_size("mp")
    group_index = lax.axis_index("dp")
    part_index = lax.axis_index("mp")
    pre_rows = pre_tokens.shape[0]
    width = pre_tokens.shape[1]
    dec_rows = dec_tokens.shape[0]
    head_dim = dec_cache.shape[-1] // 2
    bundle = max(1, dec_rows // group_count)
    device = group_index * part_count + part_index
    position = jnp.arange(dec_rows, dtype=jnp.int32)
    own_deal = lax.dynamic_slice_in_dim(deal_slots, device * dec_rows, dec_rows, 0)
    target = own_deal // (part_count * dec_rows)
    group_ids = jnp.arange(group_count, dtype=jnp.int32)
    lane_ids = jnp.arange(bundle, dtype=jnp.int32)
    send_table = (
        (target[None, None, :] == group_ids[:, None, None])
        & (position[None, None, :] % bundle == lane_ids[None, :, None])
    ).astype(jnp.bfloat16)
    outgoing = jnp.einsum(
        "jbi,id->jbd", send_table, dec_tokens, preferred_element_type=jnp.float32
    ).astype(jnp.bfloat16)
    incoming = lax.all_to_all(outgoing, "dp", split_axis=0, concat_axis=0, tiled=True)
    slot_ids = device * dec_rows + position
    request_ids = jnp.arange(deal_slots.shape[0], dtype=jnp.int32)
    request = jnp.sum(
        jnp.where(deal_slots[None, :] == slot_ids[:, None], request_ids[None, :], 0), axis=1
    )
    source = request // (part_count * dec_rows)
    lane = request % dec_rows % bundle
    take_table = (
        (source[:, None, None] == group_ids[None, :, None])
        & (lane[:, None, None] == lane_ids[None, None, :])
    ).astype(jnp.bfloat16)
    slot_rows = jnp.einsum(
        "ijb,jbd->id", take_table, incoming, preferred_element_type=jnp.float32
    ).astype(jnp.bfloat16)
    layer_input = jnp.concatenate([pre_tokens, slot_rows], axis=0)
    rows_dev = layer_input.shape[0]
    normed = root_norm(layer_input.astype(jnp.float32), attn_gain).astype(jnp.bfloat16)
    group_rows = lax.all_gather(normed, "mp", axis=0, tiled=True)
    local_width = qkv_weight.shape[1]
    projected = jnp.dot(
        group_rows,
        lax.all_gather(qkv_weight, "dp", axis=0, tiled=True),
        preferred_element_type=jnp.float32,
    )
    local_groups = dec_cache.shape[0]
    projected = projected.reshape(part_count, rows_dev, local_groups, local_width // local_groups)
    attn_out = group_attention(
        projected, prior_cache[:, 0], dec_cache, dec_lengths, pre_offsets[0], pre_rows, head_dim
    )
    partial_sums = jnp.dot(
        attn_out,
        lax.all_gather(out_weight, "dp", axis=1, tiled=True),
        preferred_element_type=jnp.float32,
    )
    attn_sum = lax.psum_scatter(
        partial_sums.astype(jnp.bfloat16), "mp", scatter_dimension=0, tiled=True
    ).astype(jnp.float32)
    residual = layer_input.astype(jnp.float32) + attn_sum
    normed_moe = root_norm(residual, moe_gain).astype(jnp.bfloat16)
    expert_count = gate_up.shape[0]
    local_experts = max(1, expert_count // group_count)
    copies = max(1, group_count // expert_count)
    sent_gu = jnp.repeat(gate_up, copies, axis=0).reshape(
        (group_count, local_experts) + gate_up.shape[1:]
    )
    sent_dn = jnp.repeat(down_weight, copies, axis=0).reshape(
        (group_count, local_experts) + down_weight.shape[1:]
    )
    owned_gu, owned_dn = (
        lax.all_to_all(sent_gu, "dp", split_axis=0, concat_axis=2, tiled=True),
        lax.all_to_all(sent_dn, "dp", split_axis=0, concat_axis=2, tiled=True),
    )
    full_gu, full_dn = (
        lax.all_gather(owned_gu, "mp", axis=3, tiled=True),
        lax.all_gather(owned_dn, "mp", axis=3, tiled=True),
    )
    full_gu = full_gu[0]
    full_dn = full_dn[0]
    topk = routes.shape[1]
    capacity = 4 * ((rows_dev * topk + 3 * expert_count - 1) // (3 * expert_count))
    expert_ids = jnp.arange(expert_count, dtype=jnp.int32)
    hits = routes[:, :, None] == expert_ids[None, None, :]
    chosen = jnp.any(hits, axis=1)
    weight = jnp.sum(jnp.where(hits, route_gates.astype(jnp.float32)[:, :, None], 0.0), axis=1)
    rank = jnp.cumsum(chosen.astype(jnp.int32), axis=0) - 1
    slot_range = jnp.arange(capacity, dtype=jnp.int32)
    placed = chosen.T[:, None, :] & (rank.T[:, None, :] == slot_range[None, :, None])
    dispatch_table = placed.astype(jnp.bfloat16)
    outbound = jnp.einsum(
        "ecr,rd->ecd", dispatch_table, normed_moe, preferred_element_type=jnp.float32
    ).astype(jnp.bfloat16)
    per_owner = expert_count * capacity // group_count
    outbound = outbound.reshape(group_count, local_experts, per_owner // local_experts, width)
    both = jnp.einsum(
        "slnd,ldf->slnf",
        lax.all_to_all(outbound, "dp", split_axis=0, concat_axis=0, tiled=True),
        full_gu,
        preferred_element_type=jnp.float32,
    )
    halfway = both.shape[-1] // 2
    activation = (jax.nn.silu(both[..., :halfway]) * both[..., halfway:]).astype(jnp.bfloat16)
    expert_out = jnp.einsum(
        "slnf,lfd->slnd", activation, full_dn, preferred_element_type=jnp.float32
    ).astype(jnp.bfloat16)
    returned = lax.all_to_all(expert_out, "dp", split_axis=0, concat_axis=0, tiled=True)
    returned = returned.reshape(expert_count, capacity, width)
    combine_table = (placed.astype(jnp.float32) * weight.T[:, None, :]).astype(jnp.bfloat16)
    moe_sum = jnp.einsum("ecr,ecd->rd", combine_table, returned, preferred_element_type=jnp.float32)
    return (residual + moe_sum).astype(jnp.bfloat16)


def solution(mesh):
    return jax.shard_map(
        local,
        mesh=mesh,
        in_specs=(
            P(("dp", "mp"), None),
            P(("dp", "mp"), None),
            P(),
            P("dp"),
            P("dp"),
            P("mp", "dp", None, None),
            P("mp", "dp", None, None),
            P(),
            P(),
            P("dp", "mp"),
            P("mp", "dp"),
            P(None, "dp", "mp"),
            P(None, "dp", "mp"),
            P(("dp", "mp"), None),
            P(("dp", "mp"), None),
        ),
        out_specs=P(("dp", "mp"), None),
        check_vma=False,
    )
```

profile of v0, /device:TPU:23, one launch (start us, length us, event | category | flops | bytes accessed | tf_op | source)
XLA Modules:
  0.0 748.8 jit_solution(776319263484663891)
XLA Ops:
  10.0 6.2 all-to-all-start
  23.6 2.9 copy.61
  28.8 2.9 fusion.93
  31.7 2.3 fusion.29
  34.1 6.2 all-to-all-start.2
  40.9 44.1 %all-gather.3.cloned.1.call-done = bf16[1024,2048]{1,0:T(8,128)(2,1)} async-done(((bf16[32,2048]{1,0:T(8,128)(2,1)}), bf16[1024,2048]{1,0:T(8,128)(2,1)}) %all-gather.3.cloned.1.call-update) | async-done | bytes 4194320 | tf_op jit(solution)/shard_map/all_gather | solution.py:173
  85.0 4.7 fusion.60
  92.0 2.0 copy-done.2
  94.0 2.2 slice.101
  96.2 5.3 copy.78
  101.5 2.1 fusion.68
  109.0 24.1 %fusion.95 = (f32[8,2,512]{2,1,0:T(2,128)S(1)}, f32[8,2,512,1536]{2,3,1,0:T(8,128)}) fusion(pred[512,1536]{0,1:T(8,128)(4,1)} %fusion.29, bf16[8,512,64]{1,2,0:T(8,128)(2,1)} %maximum_bitcast_fusion.13, bf16[8,1024,64]{1,2,0:T(8,128)(2,1)} %get-tuple-element.10, bf16[512,8,2,32]{0,3,2,1:T(8,128)(2,1)} %get-tuple-element.8, ...), kind=kOutput, calls=%fused_computation.149 | convolution fusion | flops 1666188800 | bytes 53772288 | tf_op jit(solution)/shard_map/sub | solution.py:60
  133.1 19.6 %fusion.42 = bf16[8,64,2,512]{3,1,2,0:T(8,128)(2,1)} fusion(f32[8,2,512,1536]{2,3,1,0:T(8,128)} %get-tuple-element.26, f32[8,2,512]{2,1,0:T(2,128)S(1)} %get-tuple-element.25, bf16[8,512,64]{1,2,0:T(8,128)(2,1)} %fusion.68, bf16[8,1024,64]{1,2,0:T(8,128)(2,1)} %get-tuple-element.9), kind=kOutput, calls=%fused_computation.52 | convolution fusion | flops 1639448576 | bytes 52985856 | tf_op jit(solution)/shard_map/gpck,gkh->cgph/dot_general | solution.py:62
  154.0 2.5 fusion.94
  157.6 3.6 multiply_reduce_fusion
  162.2 12.3 %convert_bitcast_fusion.1 = bf16[32,1,172,1024]{3,2,1,0:T(8,128)(2,1)} fusion(s32[32,516]{1,0:T(8,128)S(1)} %copy-done.7, pred[32,516]{1,0:T(8,128)(4,1)S(1)} %bitcast.145, bf16[516,1024]{1,0:T(8,128)(2,1)S(1)} %get-tuple-element.28, f32[1024]{0:T(1024)S(1)} %copy-done.10, f32[516]{0:T(1024)S(1)} %add_rsqrt_fusion, ...), kind=kOutput, calls=%fused_computation.20 | convolution fusion | flops 5832522752 | bytes 13474448 | tf_op jit(solution)/shard_map/ecr,rd->ecd/dot_general | solution.py:220
  174.5 256.4 %all_to_all.33 = bf16[32,1,172,1024]{3,2,1,0:T(8,128)(2,1)} all-to-all(bf16[32,1,172,1024]{3,2,1,0:T(8,128)(2,1)} %convert_bitcast_fusion.1), channel_id=1, replica_groups=mesh['dp'=32,'mp'=1] {'dp'}, dimensions={0} | all-to-all | bytes 22544384 | tf_op jit(solution)/shard_map/all_to_all | solution.py:227
  430.9 7.9 %all-to-all-start.3 = ((bf16[32,1,16,1024]{3,2,1,0:T(8,128)(2,1)}), bf16[32,1,16,1024]{3,2,1,0:T(8,128)(2,1)}, u32[]{:S(2)}, u32[]{:S(2)}) async-start(bf16[32,1,16,1024]{3,2,1,0:T(8,128)(2,1)} %bitcast.37), calls=%async_computation.3 | async-start | bytes 2097152 | tf_op jit(solution)/shard_map/all_to_all | solution.py:202
  438.8 19.3 %fusion.14 = f32[32,1,172,1024]{3,2,0,1:T(8,128)} fusion(bf16[1024,1024,1]{1,0,2:T(8,128)(2,1)S(1)} %bitcast.142, bf16[32,1,172,1024]{3,2,1,0:T(8,128)(2,1)} %all_to_all.33), kind=kOutput, calls=%fused_computation.21 | convolution fusion | flops 11542724608 | bytes 35913728 | tf_op jit(solution)/shard_map/slnd,ldf->slnf/dot_general | solution.py:225
  458.1 3.2 all-to-all-done.3
  461.3 13.8 %convert_bitcast_fusion = bf16[32,1,172,1024]{3,2,1,0:T(8,128)(2,1)} fusion(bf16[512,1024,1]{1,0,2:T(8,128)(2,1)} %bitcast.39, f32[32,1,172,1024]{3,2,0,1:T(8,128)} %fusion.14), kind=kOutput, calls=%fused_computation.19 | convolution fusion | flops 5793906688 | bytes 34865152 | tf_op jit(solution)/shard_map/slnf,lfd->slnd/dot_general | solution.py:233
  475.1 7.8 %all-to-all-start.4 = ((bf16[32,1,172,1024]{3,2,1,0:T(8,128)(2,1)}), bf16[32,1,172,1024]{3,2,1,0:T(8,128)(2,1)}, u32[]{:S(2)}, u32[]{:S(2)}) async-start(bf16[32,1,172,1024]{3,2,1,0:T(8,128)(2,1)} %convert_bitcast_fusion), calls=%async_computation.4 | async-start | bytes 23068672 | tf_op jit(solution)/shard_map/all_to_all | solution.py:236
  483.0 248.7 %all-to-all-done.4 = bf16[32,1,172,1024]{3,2,1,0:T(8,128)(2,1)} async-done(((bf16[32,1,172,1024]{3,2,1,0:T(8,128)(2,1)}), bf16[32,1,172,1024]{3,2,1,0:T(8,128)(2,1)}, u32[]{:S(2)}, u32[]{:S(2)}) %all-to-all-start.4) | async-done | bytes 11272224 | tf_op jit(solution)/shard_map/all_to_all | solution.py:236
  731.8 10.0 %fusion.33 = bf16[516,1024]{1,0:T(8,128)(2,1)} fusion(bf16[516,1024]{1,0:T(8,128)(2,1)S(1)} %copy-done.12, bf16[32,1,172,1024]{3,2,1,0:T(8,128)(2,1)} %all-to-all-done.4, bf16[32,516]{1,0:T(8,128)(2,1)S(1)} %bitcast.149, s32[32,516]{1,0:T(8,128)S(1)} %copy-done.7, pred[32,516]{1,0:T(8,128)(4,1)S(1)} %bitcast.146, ...), kind=kOutput, calls=%fused_computation.40 | convolution fusion | flops 5829198336 | bytes 14558080 | tf_op jit(solution)/shard_map/ecr,ecd->rd/dot_general | solution.py:239
  (82 shorter events, 24.1 us)
Async XLA Ops:
  6.5 1.5 copy-start
  6.5 78.4 %all-gather.3.cloned.1.call-start = ((), (), s32[]{:S(2)}) async-start(), calls=%async_computation.5 | async-start | bytes 4325376 | tf_op jit(solution)/shard_map/all_gather | solution.py:173
  10.0 24.1 %all-to-all-start = ((bf16[32,2,512]{2,1,0:T(2,128)(2,1)}), bf16[32,2,512]{2,1,0:T(2,128)(2,1)S(1)}, u32[]{:S(2)}, u32[]{:S(2)}) async-start(bf16[32,2,512]{2,1,0:T(2,128)(2,1)} %reshape.492), calls=%async_computation | async-start | bytes 131072 | tf_op jit(solution)/shard_map/all_to_all | solution.py:151
  16.2 141.4 %all-gather.5.cloned.1.call-start = ((), (), s32[]{:S(2)}) async-start(), calls=%async_computation.6 | async-start | bytes 2162688 | tf_op jit(solution)/shard_map/all_gather | solution.py:183
  26.4 2.4 copy-start.3
  34.0 6.5 copy-start.5
  34.1 50.9 %copy-start.9 = (f32[1024]{0:T(1024)S(1)}, f32[1024]{0:T(1024)}, u32[]{:S(2)}) copy-start(f32[1024]{0:T(1024)} %param.22) | copy-start | bytes 12292
  34.1 140.4 %all-to-all-start.2 = ((bf16[32,1,32,1024]{3,2,1,0:T(8,128)(2,1)}), bf16[32,1,32,1024]{3,2,1,0:T(8,128)(2,1)S(1)}, u32[]{:S(2)}, u32[]{:S(2)}) async-start(bf16[32,1,32,1024]{3,2,1,0:T(8,128)(2,1)} %bitcast.28), calls=%async_computation.2 | async-start | bytes 4194304 | tf_op jit(solution)/shard_map/all_to_all | solution.py:201
  92.0 2.0 copy-start.2
  153.5 3.3 copy-start.4
  157.6 4.6 copy-start.7
  157.6 4.6 copy-start.10
  161.2 1.0 copy-start.11
  430.9 30.3 %all-to-all-start.3 = ((bf16[32,1,16,1024]{3,2,1,0:T(8,128)(2,1)}), bf16[32,1,16,1024]{3,2,1,0:T(8,128)(2,1)}, u32[]{:S(2)}, u32[]{:S(2)}) async-start(bf16[32,1,16,1024]{3,2,1,0:T(8,128)(2,1)} %bitcast.37), calls=%async_computation.3 | async-start | bytes 2097152 | tf_op jit(solution)/shard_map/all_to_all | solution.py:202
  475.1 7.8 %copy-start.8 = (bf16[516,8]{0,1:T(8,128)(2,1)S(1)}, bf16[516,8]{0,1:T(8,128)(2,1)}, u32[]{:S(2)}) copy-start(bf16[516,8]{0,1:T(8,128)(2,1)} %param.29) | copy-start | bytes 24772
  475.1 7.9 %copy-start.6 = (s32[516,8]{0,1:T(8,128)S(1)}, s32[516,8]{0,1:T(8,128)}, u32[]{:S(2)}) copy-start(s32[516,8]{0,1:T(8,128)} %param.28) | copy-start | bytes 49540
  475.1 256.7 %copy-start.12 = (bf16[516,1024]{1,0:T(8,128)(2,1)S(1)}, bf16[516,1024]{1,0:T(8,128)(2,1)}, u32[]{:S(2)}) copy-start(bf16[516,1024]{1,0:T(8,128)(2,1)} %copy-done.11) | copy-start | bytes 3170308
  475.1 256.7 %all-to-all-start.4 = ((bf16[32,1,172,1024]{3,2,1,0:T(8,128)(2,1)}), bf16[32,1,172,1024]{3,2,1,0:T(8,128)(2,1)}, u32[]{:S(2)}, u32[]{:S(2)}) async-start(bf16[32,1,172,1024]{3,2,1,0:T(8,128)(2,1)} %convert_bitcast_fusion), calls=%async_computation.4 | async-start | bytes 23068672 | tf_op jit(solution)/shard_map/all_to_all | solution.py:236
  731.8 10.0 %copy-start.1 = (bf16[4,1024]{1,0:T(4,128)(2,1)S(1)}, bf16[4,1024]{1,0:T(4,128)(2,1)}, u32[]{:S(2)}) copy-start(bf16[4,1024]{1,0:T(4,128)(2,1)} %param.16) | copy-start | bytes 24580
Sparse Core Ops, SparseCore 0:
  10.2 74.7 all-gather.2
  87.8 58.0 all-gather.4
where the time goes:
time: 760 us; the launch traced here: 749 us
  waiting for transfers between devices  297 us (39%)
  blocking collectives  256 us (34%)
  matrix products  111 us (15%)
  starting transfers between devices  28.1 us (4%)
  local copies, waits for them, and re-layouts  27.4 us (4%)
  between operations  14.6 us (2%)
  other arithmetic  14 us (2%)
    all_to_all x1, blocking collectives, local(): lax.all_to_all(outbound, 'dp', split_axis=0, concat_axis=0, tiled=True)  256 us
    all_to_all x1, waiting for transfers between devices, local(): lax.all_to_all(expert_out, 'dp', split_axis=0, concat_axis=0, tiled=True)  249 us
    all_gather x1, waiting for transfers between devices, local(): lax.all_gather(qkv_weight, 'dp', axis=0, tiled=True)  44.1 us
    sub x1, matrix products, prefill_attention(): expo = jnp.exp(scores - highest)  24.1 us
    dot_general x1, matrix products, prefill_attention(): jnp.einsum('gpck,gkh->cgph', weights, all_values, preferred_element_type=...  19.6 us
    dot_general x1, matrix products, local(): jnp.einsum('slnd,ldf->slnf', lax.all_to_all(outbound, 'dp', split_axis=0,...  19.3 us
  transfers between devices with their start and end apart: 6, of which 3 were waited for; matrix products, arithmetic and copies ran while one was open for 17% of the time, Pallas kernels for 0%

commit v1 on v0

--- a/solution.py
+++ b/solution.py
@@ -126,9 +126,12 @@
     routes,
     route_gates,
 ):
-    group_count = lax.axis_size("dp")
+    dp = ("zh", "dl")
+    halves = lax.axis_size("zh")
+    half_size = lax.axis_size("dl")
+    group_count = halves * half_size
     part_count = lax.axis_size("mp")
-    group_index = lax.axis_index("dp")
+    group_index = lax.axis_index("zh") * half_size + lax.axis_index("dl")
     part_index = lax.axis_index("mp")
     pre_rows = pre_tokens.shape[0]
     width = pre_tokens.shape[1]
@@ -148,7 +151,7 @@
     outgoing = jnp.einsum(
         "jbi,id->jbd", send_table, dec_tokens, preferred_element_type=jnp.float32
     ).astype(jnp.bfloat16)
-    incoming = lax.all_to_all(outgoing, "dp", split_axis=0, concat_axis=0, tiled=True)
+    incoming = lax.all_to_all(outgoing, dp, split_axis=0, concat_axis=0, tiled=True)
     slot_ids = device * dec_rows + position
     request_ids = jnp.arange(deal_slots.shape[0], dtype=jnp.int32)
     request = jnp.sum(
@@ -168,38 +171,38 @@
     normed = root_norm(layer_input.astype(jnp.float32), attn_gain).astype(jnp.bfloat16)
     group_rows = lax.all_gather(normed, "mp", axis=0, tiled=True)
     local_width = qkv_weight.shape[1]
-    projected = jnp.dot(
-        group_rows,
-        lax.all_gather(qkv_weight, "dp", axis=0, tiled=True),
-        preferred_element_type=jnp.float32,
-    )
+    qkv_pair = lax.all_gather(qkv_weight, "zh", axis=0, tiled=False)
+    qkv_full = lax.all_gather(qkv_pair, "dl", axis=0, tiled=False)
+    qkv_full = jnp.swapaxes(qkv_full, 0, 1).reshape(-1, local_width)
+    projected = jnp.dot(group_rows, qkv_full, preferred_element_type=jnp.float32)
     local_groups = dec_cache.shape[0]
     projected = projected.reshape(part_count, rows_dev, local_groups, local_width // local_groups)
     attn_out = group_attention(
         projected, prior_cache[:, 0], dec_cache, dec_lengths, pre_offsets[0], pre_rows, head_dim
     )
-    partial_sums = jnp.dot(
-        attn_out,
-        lax.all_gather(out_weight, "dp", axis=1, tiled=True),
-        preferred_element_type=jnp.float32,
-    )
+    out_pair = lax.all_gather(out_weight, "zh", axis=1, tiled=False)
+    out_full = lax.all_gather(out_pair, "dl", axis=1, tiled=False)
+    out_full = jnp.swapaxes(out_full, 1, 2).reshape(out_weight.shape[0], -1)
+    partial_sums = jnp.dot(attn_out, out_full, preferred_element_type=jnp.float32)
     attn_sum = lax.psum_scatter(
         partial_sums.astype(jnp.bfloat16), "mp", scatter_dimension=0, tiled=True
     ).astype(jnp.float32)
     residual = layer_input.astype(jnp.float32) + attn_sum
     normed_moe = root_norm(residual, moe_gain).astype(jnp.bfloat16)
     expert_count = gate_up.shape[0]
-    local_experts = max(1, expert_count // group_count)
-    copies = max(1, group_count // expert_count)
-    sent_gu = jnp.repeat(gate_up, copies, axis=0).reshape(
-        (group_count, local_experts) + gate_up.shape[1:]
-    )
-    sent_dn = jnp.repeat(down_weight, copies, axis=0).reshape(
-        (group_count, local_experts) + down_weight.shape[1:]
-    )
+    local_experts = max(1, expert_count // half_size)
+    copies = max(1, half_size // expert_count)
+
+    def owner_major(weights):
+        per_half = jnp.repeat(weights, copies, axis=0).reshape(
+            (half_size, local_experts) + weights.shape[1:]
+        )
+        both = jnp.broadcast_to(per_half[None], (halves,) + per_half.shape)
+        return both.reshape((group_count, local_experts) + weights.shape[1:])
+
     owned_gu, owned_dn = (
-        lax.all_to_all(sent_gu, "dp", split_axis=0, concat_axis=2, tiled=True),
-        lax.all_to_all(sent_dn, "dp", split_axis=0, concat_axis=2, tiled=True),
+        lax.all_to_all(owner_major(gate_up), dp, split_axis=0, concat_axis=2, tiled=True),
+        lax.all_to_all(owner_major(down_weight), dp, split_axis=0, concat_axis=2, tiled=True),
     )
     full_gu, full_dn = (
         lax.all_gather(owned_gu, "mp", axis=3, tiled=True),
@@ -220,11 +223,11 @@
     outbound = jnp.einsum(
         "ecr,rd->ecd", dispatch_table, normed_moe, preferred_element_type=jnp.float32
     ).astype(jnp.bfloat16)
-    per_owner = expert_count * capacity // group_count
-    outbound = outbound.reshape(group_count, local_experts, per_owner // local_experts, width)
+    per_owner = expert_count * capacity // half_size
+    outbound = outbound.reshape(half_size, local_experts, per_owner // local_experts, width)
     both = jnp.einsum(
         "slnd,ldf->slnf",
-        lax.all_to_all(outbound, "dp", split_axis=0, concat_axis=0, tiled=True),
+        lax.all_to_all(outbound, "dl", split_axis=0, concat_axis=0, tiled=True),
         full_gu,
         preferred_element_type=jnp.float32,
     )
@@ -233,7 +236,7 @@
     expert_out = jnp.einsum(
         "slnf,lfd->slnd", activation, full_dn, preferred_element_type=jnp.float32
     ).astype(jnp.bfloat16)
-    returned = lax.all_to_all(expert_out, "dp", split_axis=0, concat_axis=0, tiled=True)
+    returned = lax.all_to_all(expert_out, "dl", split_axis=0, concat_axis=0, tiled=True)
     returned = returned.reshape(expert_count, capacity, width)
     combine_table = (placed.astype(jnp.float32) * weight.T[:, None, :]).astype(jnp.bfloat16)
     moe_sum = jnp.einsum("ecr,ecd->rd", combine_table, returned, preferred_element_type=jnp.float32)
@@ -241,26 +244,31 @@
 
 
 def solution(mesh):
+    groups = mesh.shape["dp"]
+    halves = 2 if groups % 2 == 0 else 1
+    devices = mesh.devices.reshape(halves, groups // halves, mesh.shape["mp"])
+    split_mesh = jax.sharding.Mesh(devices, ("zh", "dl", "mp"))
+    dp = ("zh", "dl")
     return jax.shard_map(
         local,
-        mesh=mesh,
+        mesh=split_mesh,
         in_specs=(
-            P(("dp", "mp"), None),
-            P(("dp", "mp"), None),
+            P((*dp, "mp"), None),
+            P((*dp, "mp"), None),
             P(),
-            P("dp"),
-            P("dp"),
-            P("mp", "dp", None, None),
-            P("mp", "dp", None, None),
+            P(dp),
+            P(dp),
+            P("mp", dp, None, None),
+            P("mp", dp, None, None),
             P(),
             P(),
-            P("dp", "mp"),
-            P("mp", "dp"),
-            P(None, "dp", "mp"),
-            P(None, "dp", "mp"),
-            P(("dp", "mp"), None),
-            P(("dp", "mp"), None),
+            P(dp, "mp"),
+            P("mp", dp),
+            P(None, dp, "mp"),
+            P(None, dp, "mp"),
+            P((*dp, "mp"), None),
+            P((*dp, "mp"), None),
         ),
-        out_specs=P(("dp", "mp"), None),
+        out_specs=P((*dp, "mp"), None),
         check_vma=False,
     )

time: 760 us -> 715 us (0.941)
  blocking collectives: 256 us -> 11.4 us
  waiting for transfers between devices: 297 us -> 416 us
  local copies, waits for them, and re-layouts: 27.4 us -> 110 us
    all_to_all x1 -> x0, blocking collectives: 256 us -> none  [local(): lax.all_to_all(outbound, 'dp', split_axis=0, concat_axis=0, tiled=True)]
    all_to_all x4 -> x5, waiting for transfers between devices: 252 us -> 367 us  [the longest x1 175 us: local(): lax.all_to_all(expert_out, 'dl', split_axis=0, concat_axis=0, tiled=True)]
    reshape x1 -> x2, local copies, waits for them, and re-layouts: 0.27 us -> 32.9 us  [the longest x1 30.6 us: local(): outbound.reshape(half_size, local_experts, per_owner // local_experts, wi...]
    convert_element_type x0 -> x1, local copies, waits for them, and re-layouts: none -> 22.1 us  [local(): expert_out = jnp.einsum('slnf,lfd->slnd', activation, full_dn, preferred_...]
    all_to_all x0 -> x3, local copies, waits for them, and re-layouts: none -> 15.1 us  [the longest x1 8.22 us: local(): lax.all_to_all(expert_out, 'dl', split_axis=0, concat_axis=0, tiled=True)]
    all_gather x0 -> x2, blocking collectives: none -> 11.4 us  [the longest x1 6.27 us: local(): qkv_pair = lax.all_gather(qkv_weight, 'zh', axis=0, tiled=False)]
    transpose x0 -> x3, local copies, waits for them, and re-layouts: none -> 9.58 us  [the longest x1 4.79 us: local(): qkv_full = jnp.swapaxes(qkv_full, 0, 1).reshape(-1, local_width)]
    dot_general x0 -> x2, local copies, waits for them, and re-layouts: none -> 7.77 us  [local(): jnp.dot(group_rows, qkv_full, preferred_element_type=jnp.float32)]
  transfers between devices with their start and end apart: 6 -> 7, of which waited for: 3 -> 4; matrix products, arithmetic and copies ran while one was open for 17% -> 22% of each run, Pallas kernels for 0% -> 0%
where the time goes in v1:
time: 715 us; the launch traced here: 709 us
  waiting for transfers between devices  416 us (58%)
  local copies, waits for them, and re-layouts  110 us (15%)
  matrix products  107 us (15%)
  starting transfers between devices  34.2 us (5%)
  other arithmetic  15.2 us (2%)
  between operations  14.9 us (2%)
  blocking collectives  11.4 us (2%)
    all_to_all x1, waiting for transfers between devices, local(): lax.all_to_all(expert_out, 'dl', split_axis=0, concat_axis=0, tiled=True)  175 us
    all_to_all x1, waiting for transfers between devices, local(): lax.all_to_all(outbound, 'dl', split_axis=0, concat_axis=0, tiled=True)  169 us
    all_gather x1, waiting for transfers between devices, local(): qkv_full = lax.all_gather(qkv_pair, 'dl', axis=0, tiled=False)  48.8 us
    reshape x1, local copies, waits for them, and re-layouts, local(): outbound.reshape(half_size, local_experts, per_owner // local_experts, wi...  30.6 us
    sub x1, matrix products, prefill_attention(): expo = jnp.exp(scores - highest)  24.5 us
    all_to_all x1, waiting for transfers between devices, local(): lax.all_to_all(owner_major(gate_up), dp, split_axis=0, concat_axis=2, til...  24 us
    dot_general x1, matrix products, local(): jnp.einsum('slnd,ldf->slnf', lax.all_to_all(outbound, 'dl', split_axis=0,...  22.6 us
    convert_element_type x1, local copies, waits for them, and re-layouts, local(): expert_out = jnp.einsum('slnf,lfd->slnd', activation, full_dn, preferred_...  22.1 us
  transfers between devices with their start and end apart: 7, of which 4 were waited for; matrix products, arithmetic and copies ran while one was open for 22% of the time, Pallas kernels for 0%

profile of v1, /device:TPU:23, one launch (start us, length us, event | category | flops | bytes accessed | tf_op | source)
XLA Modules:
  0.0 708.9 jit_solution(10691843231036386536)
XLA Ops:
  6.5 5.2 all-gather.2
  11.8 6.3 all-gather
  20.8 10.3 %all-to-all-start = ((bf16[32,2,512]{2,1,0:T(2,128)(2,1)}), bf16[32,2,512]{2,1,0:T(2,128)(2,1)}, u32[]{:S(2)}, u32[]{:S(2)}) async-start(bf16[32,2,512]{2,1,0:T(2,128)(2,1)} %reshape.604), calls=%async_computation | async-start | bytes 131072 | tf_op jit(solution)/shard_map/all_to_all | solution.py:154
  49.3 6.3 all-to-all-start.3
  63.0 48.8 %all-gather.7.cloned.1.call-done = bf16[32,32,2048]{2,1,0:T(8,128)(2,1)} async-done(((bf16[2,32,2048]{2,1,0:T(8,128)(2,1)}), bf16[32,32,2048]{2,1,0:T(8,128)(2,1)}) %all-gather.7.cloned.1.call-update) | async-done | bytes 4194320 | tf_op jit(solution)/shard_map/all_gather | solution.py:175
  111.8 4.8 copy.163
  116.6 6.4 copy.164
  123.0 4.7 fusion.54
  142.5 24.5 %fusion.95 = (f32[8,2,512]{2,1,0:T(2,128)S(1)}, f32[8,2,512,1536]{2,3,1,0:T(8,128)}) fusion(pred[512,1536]{0,1:T(8,128)(4,1)} %fusion.28, bf16[8,512,64]{1,2,0:T(8,128)(2,1)} %copy.169, bf16[8,1024,64]{1,2,0:T(8,128)(2,1)S(1)} %copy-done.11, bf16[512,8,2,32]{0,3,2,1:T(8,128)(2,1)} %get-tuple-element.8, bf16[512,8,2,32]{0,3,2,1:T(8,128)(2,1)} %get-tuple-element.7), kind=kOutput, calls=%fused_computation.151 | convolution fusion | flops 1666188800 | bytes 53772288 | tf_op jit(solution)/shard_map/sub | solution.py:60
  169.5 5.1 all-to-all-start.2
  179.7 17.7 %fusion.37 = bf16[8,64,2,512]{3,1,2,0:T(8,128)(2,1)S(1)} fusion(f32[8,2,512,1536]{2,3,1,0:T(8,128)} %get-tuple-element.26, f32[8,2,512]{2,1,0:T(2,128)S(1)} %get-tuple-element.25, bf16[8,512,64]{1,2,0:T(8,128)(2,1)} %copy.166, bf16[8,1024,64]{1,2,0:T(8,128)(2,1)S(1)} %copy-done.10), kind=kOutput, calls=%fused_computation.52 | convolution fusion | flops 1639448576 | bytes 52985856 | tf_op jit(solution)/shard_map/gpck,gkh->cgph/dot_general | solution.py:62
  199.2 11.2 %fusion.22 = bf16[32,172,1024]{2,1,0:T(8,128)(2,1)S(1)} fusion(s32[32,516]{1,0:T(8,128)S(1)} %copy-done.16, pred[32,516]{1,0:T(8,128)(4,1)S(1)} %bitcast.163, bf16[516,1024]{1,0:T(8,128)(2,1)S(1)} %get-tuple-element.28, f32[1024]{0:T(1024)S(1)} %copy-done.29, f32[516]{0:T(1024)S(1)} %add_rsqrt_fusion, bf16[4,1024]{1,0:T(4,128)(2,1)S(1)} %copy-done.28, ...), kind=kOutput, calls=%fused_computation.26 | convolution fusion | flops 5832522752 | bytes 13474448 | tf_op jit(solution)/shard_map/ecr,rd->ecd/dot_general | solution.py:223
  210.4 30.6 %copy.178 = bf16[16,2,172,1024]{3,1,2,0:T(2,128)(2,1)} copy(bf16[16,2,172,1024]{3,2,1,0:T(8,128)(2,1)S(1)} %bitcast.147) | data formatting | bytes 22544384 | tf_op jit(solution)/shard_map/reshape | solution.py:227
  241.0 24.0 %all-to-all-done.2 = bf16[32,2,32,1024]{3,2,1,0:T(8,128)(2,1)} async-done(((bf16[32,2,32,1024]{3,2,1,0:T(8,128)(2,1)}), bf16[32,2,32,1024]{3,2,1,0:T(8,128)(2,1)}, u32[]{:S(2)}, u32[]{:S(2)}) %all-to-all-start.2) | async-done | bytes 4194336 | tf_op jit(solution)/shard_map/all_to_all | solution.py:204
  264.9 7.3 %all-to-all-start.1 = ((bf16[16,2,172,1024]{3,1,2,0:T(2,128)(2,1)}), bf16[16,2,172,1024]{3,1,2,0:T(2,128)(2,1)}, u32[]{:S(2)}, u32[]{:S(2)}) async-start(bf16[16,2,172,1024]{3,1,2,0:T(2,128)(2,1)} %copy.178), calls=%async_computation.1 | async-start | bytes 22544384 | tf_op jit(solution)/shard_map/all_to_all | solution.py:230
  274.0 5.1 copy.179
  279.0 168.7 %all-to-all-done.1 = bf16[16,2,172,1024]{3,1,2,0:T(2,128)(2,1)} async-done(((bf16[16,2,172,1024]{3,1,2,0:T(2,128)(2,1)}), bf16[16,2,172,1024]{3,1,2,0:T(2,128)(2,1)}, u32[]{:S(2)}, u32[]{:S(2)}) %all-to-all-start.1) | async-done | bytes 11272224 | tf_op jit(solution)/shard_map/all_to_all | solution.py:230
  447.7 22.6 %fusion.12 = f32[16,2,172,1024]{3,2,0,1:T(8,128)} fusion(bf16[2,1024,1024,1]{2,1,3,0:T(8,128)(2,1)} %bitcast.151, bf16[16,2,172,1024]{3,1,2,0:T(2,128)(2,1)} %all-to-all-done.1), kind=kOutput, calls=%fused_computation.18 | convolution fusion | flops 11542724608 | bytes 38010880 | tf_op jit(solution)/shard_map/slnd,ldf->slnf/dot_general | solution.py:228
  470.3 13.7 %convert_bitcast_fusion = bf16[16,2,172,1024]{3,2,0,1:T(8,128)(2,1)} fusion(bf16[2,512,1024,1]{2,1,3,0:T(8,128)(2,1)S(1)} %bitcast.156, f32[16,2,172,1024]{3,2,0,1:T(8,128)} %fusion.12), kind=kOutput, calls=%fused_computation.17 | convolution fusion | flops 5793906688 | bytes 35913728 | tf_op jit(solution)/shard_map/slnf,lfd->slnd/dot_general | solution.py:236
  484.1 22.1 %copy.182 = bf16[16,2,172,1024]{3,1,2,0:T(2,128)(2,1)} copy(bf16[16,2,172,1024]{3,2,0,1:T(8,128)(2,1)} %convert_bitcast_fusion) | data formatting | bytes 22544384 | tf_op jit(solution)/shard_map/convert_element_type | solution.py:238
  506.2 5.1 all-to-all-start.4
  511.4 174.8 %all-to-all-done.4 = bf16[16,2,172,1024]{3,1,2,0:T(2,128)(2,1)} async-done(((bf16[16,2,172,1024]{3,1,2,0:T(2,128)(2,1)}), bf16[16,2,172,1024]{3,1,2,0:T(2,128)(2,1)}, u32[]{:S(2)}, u32[]{:S(2)}) %all-to-all-start.4) | async-done | bytes 11272224 | tf_op jit(solution)/shard_map/all_to_all | solution.py:239
  686.2 8.2 %copy.183 = bf16[16,2,172,1024]{3,2,1,0:T(8,128)(2,1)S(1)} copy(bf16[16,2,172,1024]{3,1,2,0:T(2,128)(2,1)} %all-to-all-done.4) | data formatting | bytes 22544384 | tf_op jit(solution)/shard_map/all_to_all | solution.py:239
  694.4 7.4 %fusion.30 = bf16[516,1024]{1,0:T(8,128)(2,1)} fusion(bf16[516,1024]{1,0:T(8,128)(2,1)S(1)} %copy-done.34, bf16[32,172,1024]{2,1,0:T(8,128)(2,1)S(1)} %bitcast.146, bf16[32,516]{1,0:T(8,128)(2,1)S(1)} %bitcast.167, s32[32,516]{1,0:T(8,128)S(1)} %copy-done.16, pred[32,516]{1,0:T(8,128)(4,1)S(1)} %bitcast.164, bf16[4,1024]{1,0:T(4,128)(2,1)S(1)} %copy-done.28, ...), kind=kOutput, calls=%fused_computation.36 | convolution fusion | flops 5829198336 | bytes 14558080 | tf_op jit(solution)/shard_map/ecr,ecd->rd/dot_general | solution.py:242
  (143 shorter events, 53.3 us)
Async XLA Ops:
  6.5 12.3 %copy-start = (bf16[4,1024]{1,0:T(4,128)(2,1)S(1)}, bf16[4,1024]{1,0:T(4,128)(2,1)}, u32[]{:S(2)}) copy-start(bf16[4,1024]{1,0:T(4,128)(2,1)} %param.16) | copy-start | bytes 24580
  6.5 53.2 %all-gather.9.cloned.1.call-start = ((), (), s32[]{:S(2)}) async-start(), calls=%async_computation.6 | async-start | bytes 2228224 | tf_op jit(solution)/shard_map/all_gather | solution.py:184
  11.7 100.1 %all-gather.7.cloned.1.call-start = ((), (), s32[]{:S(2)}) async-start(), calls=%async_computation.5 | async-start | bytes 4456448 | tf_op jit(solution)/shard_map/all_gather | solution.py:175
  20.8 26.9 %all-to-all-start = ((bf16[32,2,512]{2,1,0:T(2,128)(2,1)}), bf16[32,2,512]{2,1,0:T(2,128)(2,1)}, u32[]{:S(2)}, u32[]{:S(2)}) async-start(bf16[32,2,512]{2,1,0:T(2,128)(2,1)} %reshape.604), calls=%async_computation | async-start | bytes 131072 | tf_op jit(solution)/shard_map/all_to_all | solution.py:154
  33.8 5.4 copy-start.30
  33.8 5.6 copy-start.31
  43.2 4.5 copy-start.7
  49.3 9.6 %copy-start.8 = (bf16[512,1024]{1,0:T(8,128)(2,1)S(1)}, bf16[512,1024]{1,0:T(8,128)(2,1)}, u32[]{:S(2)}) copy-start(bf16[512,1024]{1,0:T(8,128)(2,1)} %param.15) | copy-start | bytes 3145732
  49.3 117.7 %all-to-all-start.3 = ((bf16[32,2,16,1024]{3,2,1,0:T(8,128)(2,1)}), bf16[32,2,16,1024]{3,2,1,0:T(8,128)(2,1)}, u32[]{:S(2)}, u32[]{:S(2)}) async-start(bf16[32,2,16,1024]{3,2,1,0:T(8,128)(2,1)} %bitcast.50), calls=%async_computation.3 | async-start | bytes 4194304 | tf_op jit(solution)/shard_map/all_to_all | solution.py:205
  116.6 6.4 copy-start.27
  142.5 24.5 %copy-start.4 = (bf16[32,32,1024]{2,1,0:T(8,128)(2,1)S(1)}, bf16[32,32,1024]{2,1,0:T(8,128)(2,1)}, u32[]{:S(2)}) copy-start(bf16[32,32,1024]{2,1,0:T(8,128)(2,1)} %param.26) | copy-start | bytes 6291460
  169.5 5.9 copy-start.6
  169.5 95.4 %all-to-all-start.2 = ((bf16[32,2,32,1024]{3,2,1,0:T(8,128)(2,1)}), bf16[32,2,32,1024]{3,2,1,0:T(8,128)(2,1)}, u32[]{:S(2)}, u32[]{:S(2)}) async-start(bf16[32,2,32,1024]{3,2,1,0:T(8,128)(2,1)} %bitcast.144), calls=%async_computation.2 | async-start | bytes 8388608 | tf_op jit(solution)/shard_map/all_to_all | solution.py:204
  175.9 3.8 copy-start.10
  179.7 17.7 %copy-start.5 = (bf16[1024,2,16,32]{0,3,2,1:T(8,128)(2,1)S(1)}, bf16[1024,2,16,32]{0,3,2,1:T(8,128)(2,1)}, u32[]{:S(2)}) copy-start(bf16[1024,2,16,32]{0,3,2,1:T(8,128)(2,1)} %copy.175) | copy-start | bytes 6291460
  179.7 17.7 %copy-start.9 = (bf16[512,1024]{1,0:T(8,128)(2,1)S(1)}, bf16[512,1024]{1,0:T(8,128)(2,1)}, u32[]{:S(2)}) copy-start(bf16[512,1024]{1,0:T(8,128)(2,1)} %param.15) | copy-start | bytes 3145732
  179.7 17.7 %copy-start.28 = (bf16[4,1024]{1,0:T(4,128)(2,1)S(1)}, bf16[4,1024]{1,0:T(4,128)(2,1)}, u32[]{:S(2)}) copy-start(bf16[4,1024]{1,0:T(4,128)(2,1)} %copy-done.26) | copy-start | bytes 24580
  199.1 11.3 %copy-start.33 = (bf16[516,1024]{1,0:T(8,128)(2,1)}, bf16[516,1024]{1,0:T(8,128)(2,1)S(1)}, u32[]{:S(2)}) copy-start(bf16[516,1024]{1,0:T(8,128)(2,1)S(1)} %get-tuple-element.28) | copy-start | bytes 3170308
  264.9 182.8 %all-to-all-start.1 = ((bf16[16,2,172,1024]{3,1,2,0:T(2,128)(2,1)}), bf16[16,2,172,1024]{3,1,2,0:T(2,128)(2,1)}, u32[]{:S(2)}, u32[]{:S(2)}) async-start(bf16[16,2,172,1024]{3,1,2,0:T(2,128)(2,1)} %copy.178), calls=%async_computation.1 | async-start | bytes 22544384 | tf_op jit(solution)/shard_map/all_to_all | solution.py:230
  506.2 5.1 copy-start.25
  506.2 5.2 copy-start.15
  506.2 180.0 %all-to-all-start.4 = ((bf16[16,2,172,1024]{3,1,2,0:T(2,128)(2,1)}), bf16[16,2,172,1024]{3,1,2,0:T(2,128)(2,1)}, u32[]{:S(2)}, u32[]{:S(2)}) async-start(bf16[16,2,172,1024]{3,1,2,0:T(2,128)(2,1)} %copy.182), calls=%async_computation.4 | async-start | bytes 22544384 | tf_op jit(solution)/shard_map/all_to_all | solution.py:239
  511.4 183.0 %copy-start.34 = (bf16[516,1024]{1,0:T(8,128)(2,1)S(1)}, bf16[516,1024]{1,0:T(8,128)(2,1)}, u32[]{:S(2)}) copy-start(bf16[516,1024]{1,0:T(8,128)(2,1)} %copy-done.33) | copy-start | bytes 3170308
  694.4 7.4 %copy-start.1 = (bf16[4,1024]{1,0:T(4,128)(2,1)S(1)}, bf16[4,1024]{1,0:T(4,128)(2,1)}, u32[]{:S(2)}) copy-start(bf16[4,1024]{1,0:T(4,128)(2,1)} %param.16) | copy-start | bytes 24580
  (19 other events, 38.0 us)
Sparse Core Ops, SparseCore 0:
  11.9 34.1 all-gather.8
  47.7 64.0 all-gather.6

commit v2 on v1

--- a/solution.py
+++ b/solution.py
@@ -219,27 +219,32 @@
     rank = jnp.cumsum(chosen.astype(jnp.int32), axis=0) - 1
     slot_range = jnp.arange(capacity, dtype=jnp.int32)
     placed = chosen.T[:, None, :] & (rank.T[:, None, :] == slot_range[None, :, None])
-    dispatch_table = placed.astype(jnp.bfloat16)
-    outbound = jnp.einsum(
-        "ecr,rd->ecd", dispatch_table, normed_moe, preferred_element_type=jnp.float32
-    ).astype(jnp.bfloat16)
-    per_owner = expert_count * capacity // half_size
-    outbound = outbound.reshape(half_size, local_experts, per_owner // local_experts, width)
-    both = jnp.einsum(
-        "slnd,ldf->slnf",
-        lax.all_to_all(outbound, "dl", split_axis=0, concat_axis=0, tiled=True),
-        full_gu,
-        preferred_element_type=jnp.float32,
-    )
-    halfway = both.shape[-1] // 2
-    activation = (jax.nn.silu(both[..., :halfway]) * both[..., halfway:]).astype(jnp.bfloat16)
-    expert_out = jnp.einsum(
-        "slnf,lfd->slnd", activation, full_dn, preferred_element_type=jnp.float32
-    ).astype(jnp.bfloat16)
-    returned = lax.all_to_all(expert_out, "dl", split_axis=0, concat_axis=0, tiled=True)
-    returned = returned.reshape(expert_count, capacity, width)
     combine_table = (placed.astype(jnp.float32) * weight.T[:, None, :]).astype(jnp.bfloat16)
-    moe_sum = jnp.einsum("ecr,ecd->rd", combine_table, returned, preferred_element_type=jnp.float32)
+    halfway = full_gu.shape[-1] // 2
+    if copies > 1:
+        chunks = [(slice(None), 0)]
+    else:
+        chunks = [(slice(l, None, local_experts), l) for l in range(local_experts)]
+    moe_sum = jnp.zeros((rows_dev, width), jnp.float32)
+    for picked, l in chunks:
+        table = placed[picked].astype(jnp.bfloat16)
+        outbound = jnp.einsum(
+            "ecr,rd->ecd", table, normed_moe, preferred_element_type=jnp.float32
+        ).astype(jnp.bfloat16)
+        outbound = outbound.reshape(half_size, -1, width)
+        arrived = lax.all_to_all(outbound, "dl", split_axis=0, concat_axis=0, tiled=True)
+        both = jnp.einsum(
+            "snd,df->snf", arrived, full_gu[l], preferred_element_type=jnp.float32
+        )
+        activation = (jax.nn.silu(both[..., :halfway]) * both[..., halfway:]).astype(jnp.bfloat16)
+        expert_out = jnp.einsum(
+            "snf,fd->snd", activation, full_dn[l], preferred_element_type=jnp.float32
+        ).astype(jnp.bfloat16)
+        returned = lax.all_to_all(expert_out, "dl", split_axis=0, concat_axis=0, tiled=True)
+        returned = returned.reshape(-1, capacity, width)
+        moe_sum = moe_sum + jnp.einsum(
+            "ecr,ecd->rd", combine_table[picked], returned, preferred_element_type=jnp.float32
+        )
     return (residual + moe_sum).astype(jnp.bfloat16)
 
 

time: 715 us -> 663 us (0.927)
  local copies, waits for them, and re-layouts: 110 us -> 46.1 us
  starting transfers between devices: 34.2 us -> 43.3 us
  waiting for transfers between devices: 416 us -> 407 us
    all_to_all x1, waiting for transfers between devices: 24 us -> 61.7 us  [local(): lax.all_to_all(owner_major(gate_up), dp, split_axis=0, concat_axis=2, til...]
    reshape x1 -> x0, local copies, waits for them, and re-layouts: 30.6 us -> none  [local(): outbound.reshape(half_size, local_experts, per_owner // local_experts, wi...]
    all_to_all x1 -> x2, waiting for transfers between devices: 175 us -> 146 us  [local(): lax.all_to_all(expert_out, 'dl', split_axis=0, concat_axis=0, tiled=True)]
    convert_element_type x1 -> x0, local copies, waits for them, and re-layouts: 22.1 us -> none  [local(): expert_out = jnp.einsum('slnf,lfd->slnd', activation, full_dn, preferred_...]
    all_to_all x1 -> x2, waiting for transfers between devices: 169 us -> 149 us  [local(): lax.all_to_all(outbound, 'dl', split_axis=0, concat_axis=0, tiled=True)]
    all_to_all x1 -> x0, local copies, waits for them, and re-layouts: 8.22 us -> none  [local(): lax.all_to_all(expert_out, 'dl', split_axis=0, concat_axis=0, tiled=True)]
    dot_general x4 -> x8, matrix products: 55 us -> 60 us  [the longest x2 18.7 us: local(): jnp.einsum('snd,df->snf', arrived, full_gu[l], preferred_element_type=jnp...]
  transfers between devices with their start and end apart: 7 -> 9, of which waited for: 4 -> 6; matrix products, arithmetic and copies ran while one was open for 22% -> 25% of each run, Pallas kernels for 0% -> 0%
where the time goes in v2:
time: 663 us; the launch traced here: 656 us
  waiting for transfers between devices  407 us (61%)
  matrix products  112 us (17%)
  local copies, waits for them, and re-layouts  46.1 us (7%)
  starting transfers between devices  43.3 us (7%)
  other arithmetic  20.2 us (3%)
  between operations  15.1 us (2%)
  blocking collectives  11.5 us (2%)
    all_to_all x2, waiting for transfers between devices, local(): lax.all_to_all(outbound, 'dl', split_axis=0, concat_axis=0, tiled=True)  149 us
    all_to_all x2, waiting for transfers between devices, local(): lax.all_to_all(expert_out, 'dl', split_axis=0, concat_axis=0, tiled=True)  146 us
    all_to_all x1, waiting for transfers between devices, local(): lax.all_to_all(owner_major(gate_up), dp, split_axis=0, concat_axis=2, til...  61.7 us
    all_gather x1, waiting for transfers between devices, local(): qkv_full = lax.all_gather(qkv_pair, 'dl', axis=0, tiled=False)  50.3 us
    sub x1, matrix products, prefill_attention(): expo = jnp.exp(scores - highest)  24.3 us
    dot_general x2, matrix products, local(): jnp.einsum('snd,df->snf', arrived, full_gu[l], preferred_element_type=jnp...  18.7 us
    dot_general x1, matrix products, prefill_attention(): jnp.einsum('gpck,gkh->cgph', weights, all_values, preferred_element_type=...  17.9 us
    dot_general x2, matrix products, local(): jnp.einsum('ecr,ecd->rd', combine_table[picked], returned, preferred_elem...  16.1 us
  transfers between devices with their start and end apart: 9, of which 6 were waited for; matrix products, arithmetic and copies ran while one was open for 25% of the time, Pallas kernels for 0%

profile of v2, /device:TPU:23, one launch (start us, length us, event | category | flops | bytes accessed | tf_op | source)
XLA Modules:
  0.0 655.7 jit_solution(1917915357618407907)
XLA Ops:
  6.5 5.2 all-gather.2
  11.8 6.3 all-gather
  20.8 10.3 %all-to-all-start = ((bf16[32,2,512]{2,1,0:T(2,128)(2,1)}), bf16[32,2,512]{2,1,0:T(2,128)(2,1)S(1)}, u32[]{:S(2)}, u32[]{:S(2)}) async-start(bf16[32,2,512]{2,1,0:T(2,128)(2,1)} %reshape.605), calls=%async_computation | async-start | bytes 131072 | tf_op jit(solution)/shard_map/all_to_all | solution.py:154
  51.8 6.6 %all-to-all-start.3 = ((bf16[32,2,16,1024]{3,2,1,0:T(8,128)(2,1)}), bf16[32,2,16,1024]{3,2,1,0:T(8,128)(2,1)}, u32[]{:S(2)}, u32[]{:S(2)}) async-start(bf16[32,2,16,1024]{3,2,1,0:T(8,128)(2,1)} %bitcast.48), calls=%async_computation.3 | async-start | bytes 4194304 | tf_op jit(solution)/shard_map/all_to_all | solution.py:205
  62.2 50.3 %all-gather.7.cloned.1.call-done = bf16[32,32,2048]{2,1,0:T(8,128)(2,1)} async-done(((bf16[2,32,2048]{2,1,0:T(8,128)(2,1)}), bf16[32,32,2048]{2,1,0:T(8,128)(2,1)}) %all-gather.7.cloned.1.call-update) | async-done | bytes 4194320 | tf_op jit(solution)/shard_map/all_gather | solution.py:175
  117.3 6.4 copy.146
  143.2 24.3 %fusion.98 = (f32[8,2,512]{2,1,0:T(2,128)S(1)}, f32[8,2,512,1536]{2,3,1,0:T(8,128)}) fusion(pred[512,1536]{0,1:T(8,128)(4,1)} %fusion.25, bf16[8,512,64]{1,2,0:T(8,128)(2,1)} %copy.151, bf16[8,1024,64]{1,2,0:T(8,128)(2,1)S(1)} %copy-done.15, bf16[512,8,2,32]{0,3,2,1:T(8,128)(2,1)} %get-tuple-element.8, bf16[512,8,2,32]{0,3,2,1:T(8,128)(2,1)} %get-tuple-element.7), kind=kOutput, calls=%fused_computation.157 | convolution fusion | flops 1666188800 | bytes 53772288 | tf_op jit(solution)/shard_map/sub | solution.py:60
  170.1 5.3 all-to-all-start.2
  176.5 17.9 %fusion.41 = bf16[8,64,2,512]{3,1,2,0:T(8,128)(2,1)S(1)} fusion(f32[8,2,512,1536]{2,3,1,0:T(8,128)} %get-tuple-element.26, f32[8,2,512]{2,1,0:T(2,128)S(1)} %get-tuple-element.25, bf16[8,512,64]{1,2,0:T(8,128)(2,1)} %copy.148, bf16[8,1024,64]{1,2,0:T(8,128)(2,1)} %get-tuple-element.9), kind=kOutput, calls=%fused_computation.58 | convolution fusion | flops 1639448576 | bytes 52985856 | tf_op jit(solution)/shard_map/gpck,gkh->cgph/dot_general | solution.py:62
  197.1 6.8 %fusion.22 = bf16[16,172,1024]{2,1,0:T(8,128)(2,1)} fusion(pred[32,172,516]{2,1,0:T(8,128)(4,1)S(1)} %copy-done.8, bf16[516,1024]{1,0:T(8,128)(2,1)S(1)} %get-tuple-element.28, f32[1024]{0:T(1024)S(1)} %copy-done.24, f32[516]{0:T(1024)S(1)} %add_rsqrt_fusion, bf16[4,1024]{1,0:T(4,128)(2,1)S(1)} %convolution_convert_fusion.4, ...), kind=kOutput, calls=%fused_computation.28 | convolution fusion | flops 2915799040 | bytes 9568256 | tf_op jit(solution)/shard_map/ecr,rd->ecd/dot_general | solution.py:231
  204.0 61.7 %all-to-all-done.2 = bf16[32,2,32,1024]{3,2,1,0:T(8,128)(2,1)} async-done(((bf16[32,2,32,1024]{3,2,1,0:T(8,128)(2,1)}), bf16[32,2,32,1024]{3,2,1,0:T(8,128)(2,1)}, u32[]{:S(2)}, u32[]{:S(2)}) %all-to-all-start.2) | async-done | bytes 4194336 | tf_op jit(solution)/shard_map/all_to_all | solution.py:204
  265.7 7.3 %all-to-all-start.5 = ((bf16[16,172,1024]{2,1,0:T(8,128)(2,1)}), bf16[16,172,1024]{2,1,0:T(8,128)(2,1)}, u32[]{:S(2)}, u32[]{:S(2)}) async-start(bf16[16,172,1024]{2,1,0:T(8,128)(2,1)} %fusion.22), calls=%async_computation.5 | async-start | bytes 11534336 | tf_op jit(solution)/shard_map/all_to_all | solution.py:235
  273.0 8.2 %fusion.19 = bf16[16,172,1024]{2,1,0:T(8,128)(2,1)} fusion(pred[32,172,516]{2,1,0:T(8,128)(4,1)} %fusion.6, bf16[516,1024]{1,0:T(8,128)(2,1)S(1)} %copy-done.28, f32[1024]{0:T(1024)S(1)} %copy-done.24, f32[516]{0:T(1024)S(1)} %add_rsqrt_fusion, bf16[4,1024]{1,0:T(4,128)(2,1)S(1)} %convolution_convert_fusion.4, bf16[512,1024]{1,0:T(8,128)(2,1)S(1)} %copy-done.14), kind=kOutput, calls=%fused_computation.27 | convolution fusion | flops 2915799040 | bytes 9558032 | tf_op jit(solution)/shard_map/ecr,rd->ecd/dot_general | solution.py:231
  281.2 80.3 %all-to-all-done.5 = bf16[16,172,1024]{2,1,0:T(8,128)(2,1)} async-done(((bf16[16,172,1024]{2,1,0:T(8,128)(2,1)}), bf16[16,172,1024]{2,1,0:T(8,128)(2,1)}, u32[]{:S(2)}, u32[]{:S(2)}) %all-to-all-start.5) | async-done | bytes 5636128 | tf_op jit(solution)/shard_map/all_to_all | solution.py:235
  370.4 9.8 %fusion.31 = f32[16,172,1024]{2,1,0:T(8,128)S(1)} fusion(bf16[16,172,1024]{2,1,0:T(8,128)(2,1)} %all-to-all-done.5, bf16[1,2,1024,1024]{3,2,1,0:T(8,128)(2,1)S(1)} %bitcast.162), kind=kOutput, calls=%fused_computation.43 | convolution fusion | flops 5771362304 | bytes 19005440 | tf_op jit(solution)/shard_map/snd,df->snf/dot_general | solution.py:236
  380.2 5.1 convolution_convert_fusion
  385.4 68.8 %all-to-all-done.1 = bf16[16,172,1024]{2,1,0:T(8,128)(2,1)} async-done(((bf16[16,172,1024]{2,1,0:T(8,128)(2,1)}), bf16[16,172,1024]{2,1,0:T(8,128)(2,1)}, u32[]{:S(2)}, u32[]{:S(2)}) %all-to-all-start.1) | async-done | bytes 5636128 | tf_op jit(solution)/shard_map/all_to_all | solution.py:235
  458.7 8.9 %fusion.32 = f32[16,172,1024]{2,1,0:T(8,128)S(1)} fusion(bf16[16,172,1024]{2,1,0:T(8,128)(2,1)} %all-to-all-done.1, bf16[1,2,1024,1024]{3,2,1,0:T(8,128)(2,1)} %bitcast.163), kind=kOutput, calls=%fused_computation.45 | convolution fusion | flops 5771362304 | bytes 19136512 | tf_op jit(solution)/shard_map/snd,df->snf/dot_general | solution.py:236
  467.6 5.1 convolution_convert_fusion.1
  472.7 74.1 %all-to-all-done.6 = bf16[16,172,1024]{2,1,0:T(8,128)(2,1)} async-done(((bf16[16,172,1024]{2,1,0:T(8,128)(2,1)}), bf16[16,172,1024]{2,1,0:T(8,128)(2,1)}, u32[]{:S(2)}, u32[]{:S(2)}) %all-to-all-start.6) | async-done | bytes 5636128 | tf_op jit(solution)/shard_map/all_to_all | solution.py:243
  551.8 5.5 select_convert_fusion
  560.2 7.4 %fusion.15 = f32[516,1024,1]{1,0,2:T(8,128)} fusion(bf16[16,172,1024]{2,1,0:T(8,128)(2,1)} %all-to-all-done.6, bf16[32,172,516]{2,1,0:T(8,128)(2,1)S(1)} %select_convert_fusion), kind=kOutput, calls=%fused_computation.23 | convolution fusion | flops 2908225536 | bytes 11354112 | tf_op jit(solution)/shard_map/ecr,ecd->rd/dot_general | solution.py:245
  567.5 72.2 %all-to-all-done.4 = bf16[16,172,1024]{2,1,0:T(8,128)(2,1)} async-done(((bf16[16,172,1024]{2,1,0:T(8,128)(2,1)}), bf16[16,172,1024]{2,1,0:T(8,128)(2,1)}, u32[]{:S(2)}, u32[]{:S(2)}) %all-to-all-start.4) | async-done | bytes 5636128 | tf_op jit(solution)/shard_map/all_to_all | solution.py:243
  639.7 8.7 %fusion.30 = bf16[516,1024]{1,0:T(8,128)(2,1)} fusion(f32[516,1024,1]{1,0,2:T(8,128)} %fusion.15, bf16[516,1024]{1,0:T(8,128)(2,1)S(1)} %copy-done.29, bf16[16,172,1024]{2,1,0:T(8,128)(2,1)} %all-to-all-done.4, bf16[32,172,516]{2,1,0:T(8,128)(2,1)} %copy-done.5, bf16[4,1024]{1,0:T(4,128)(2,1)S(1)} %convolution_convert_fusion.4, ...), kind=kOutput, calls=%fused_computation.38 | convolution fusion | flops 2912980992 | bytes 14671872 | tf_op jit(solution)/shard_map/ecr,ecd->rd/dot_general | solution.py:245
  (140 shorter events, 78.1 us)
Async XLA Ops:
  6.5 12.3 %copy-start = (bf16[4,1024]{1,0:T(4,128)(2,1)S(1)}, bf16[4,1024]{1,0:T(4,128)(2,1)}, u32[]{:S(2)}) copy-start(bf16[4,1024]{1,0:T(4,128)(2,1)} %param.16) | copy-start | bytes 24580
  6.5 52.4 %all-gather.9.cloned.1.call-start = ((), (), s32[]{:S(2)}) async-start(), calls=%async_computation.8 | async-start | bytes 2228224 | tf_op jit(solution)/shard_map/all_gather | solution.py:184
  11.7 100.7 %all-gather.7.cloned.1.call-start = ((), (), s32[]{:S(2)}) async-start(), calls=%async_computation.7 | async-start | bytes 4456448 | tf_op jit(solution)/shard_map/all_gather | solution.py:175
  20.8 29.4 %all-to-all-start = ((bf16[32,2,512]{2,1,0:T(2,128)(2,1)}), bf16[32,2,512]{2,1,0:T(2,128)(2,1)S(1)}, u32[]{:S(2)}, u32[]{:S(2)}) async-start(bf16[32,2,512]{2,1,0:T(2,128)(2,1)} %reshape.605), calls=%async_computation | async-start | bytes 131072 | tf_op jit(solution)/shard_map/all_to_all | solution.py:154
  35.4 10.0 %copy-start.18 = (pred[516,32]{0,1:T(8,128)(4,1)}, pred[516,32]{0,1:T(8,128)(4,1)S(1)}, u32[]{:S(2)}) copy-start(pred[516,32]{0,1:T(8,128)(4,1)S(1)} %fusion.68) | copy-start | bytes 49540
  37.6 7.7 %copy-start.16 = (s32[32,516]{1,0:T(8,128)}, s32[32,516]{1,0:T(8,128)S(1)}, u32[]{:S(2)}) copy-start(s32[32,516]{1,0:T(8,128)S(1)} %fusion.69) | copy-start | bytes 198148
  43.0 7.2 %copy-start.12 = (bf16[32,16,1024]{2,1,0:T(8,128)(2,1)S(1)}, bf16[32,16,1024]{2,1,0:T(8,128)(2,1)}, u32[]{:S(2)}) copy-start(bf16[32,16,1024]{2,1,0:T(8,128)(2,1)} %param.27) | copy-start | bytes 3145732
  51.8 115.7 %all-to-all-start.3 = ((bf16[32,2,16,1024]{3,2,1,0:T(8,128)(2,1)}), bf16[32,2,16,1024]{3,2,1,0:T(8,128)(2,1)}, u32[]{:S(2)}, u32[]{:S(2)}) async-start(bf16[32,2,16,1024]{3,2,1,0:T(8,128)(2,1)} %bitcast.48), calls=%async_computation.3 | async-start | bytes 4194304 | tf_op jit(solution)/shard_map/all_to_all | solution.py:205
  143.2 24.3 %copy-start.9 = (bf16[32,32,1024]{2,1,0:T(8,128)(2,1)S(1)}, bf16[32,32,1024]{2,1,0:T(8,128)(2,1)}, u32[]{:S(2)}) copy-start(bf16[32,32,1024]{2,1,0:T(8,128)(2,1)} %param.26) | copy-start | bytes 6291460
  170.1 95.6 %all-to-all-start.2 = ((bf16[32,2,32,1024]{3,2,1,0:T(8,128)(2,1)}), bf16[32,2,32,1024]{3,2,1,0:T(8,128)(2,1)}, u32[]{:S(2)}, u32[]{:S(2)}) async-start(bf16[32,2,32,1024]{3,2,1,0:T(8,128)(2,1)} %bitcast.157), calls=%async_computation.2 | async-start | bytes 8388608 | tf_op jit(solution)/shard_map/all_to_all | solution.py:204
  176.4 18.0 %copy-start.10 = (bf16[1024,2,16,32]{0,3,2,1:T(8,128)(2,1)S(1)}, bf16[1024,2,16,32]{0,3,2,1:T(8,128)(2,1)}, u32[]{:S(2)}) copy-start(bf16[1024,2,16,32]{0,3,2,1:T(8,128)(2,1)} %copy.157) | copy-start | bytes 6291460
  176.4 18.0 %copy-start.14 = (bf16[512,1024]{1,0:T(8,128)(2,1)S(1)}, bf16[512,1024]{1,0:T(8,128)(2,1)}, u32[]{:S(2)}) copy-start(bf16[512,1024]{1,0:T(8,128)(2,1)} %param.15) | copy-start | bytes 3145732
  204.0 69.1 %copy-start.28 = (bf16[516,1024]{1,0:T(8,128)(2,1)S(1)}, bf16[516,1024]{1,0:T(8,128)(2,1)}, u32[]{:S(2)}) copy-start(bf16[516,1024]{1,0:T(8,128)(2,1)} %copy-done.27) | copy-start | bytes 3170308
  265.7 95.8 %all-to-all-start.5 = ((bf16[16,172,1024]{2,1,0:T(8,128)(2,1)}), bf16[16,172,1024]{2,1,0:T(8,128)(2,1)}, u32[]{:S(2)}, u32[]{:S(2)}) async-start(bf16[16,172,1024]{2,1,0:T(8,128)(2,1)} %fusion.22), calls=%async_computation.5 | async-start | bytes 11534336 | tf_op jit(solution)/shard_map/all_to_all | solution.py:235
  361.5 92.7 %all-to-all-start.1 = ((bf16[16,172,1024]{2,1,0:T(8,128)(2,1)}), bf16[16,172,1024]{2,1,0:T(8,128)(2,1)}, u32[]{:S(2)}, u32[]{:S(2)}) async-start(bf16[16,172,1024]{2,1,0:T(8,128)(2,1)} %fusion.19), calls=%async_computation.1 | async-start | bytes 11534336 | tf_op jit(solution)/shard_map/all_to_all | solution.py:235
  370.4 9.8 %copy-start.6 = (bf16[1,2,32,32,1024]{4,3,2,1,0:T(8,128)(2,1)}, bf16[1,2,32,32,1024]{4,3,2,1,0:T(8,128)(2,1)S(1)}, u32[]{:S(2)}) copy-start(bf16[1,2,32,32,1024]{4,3,2,1,0:T(8,128)(2,1)S(1)} %copy.160) | copy-start | bytes 12582916
  454.2 92.7 %all-to-all-start.6 = ((bf16[16,172,1024]{2,1,0:T(8,128)(2,1)}), bf16[16,172,1024]{2,1,0:T(8,128)(2,1)}, u32[]{:S(2)}, u32[]{:S(2)}) async-start(bf16[16,172,1024]{2,1,0:T(8,128)(2,1)} %convolution_convert_fusion), calls=%async_computation.6 | async-start | bytes 11534336 | tf_op jit(solution)/shard_map/all_to_all | solution.py:243
  472.7 78.9 %copy-start.22 = (bf16[516,8]{0,1:T(8,128)(2,1)S(1)}, bf16[516,8]{0,1:T(8,128)(2,1)}, u32[]{:S(2)}) copy-start(bf16[516,8]{0,1:T(8,128)(2,1)} %param.29) | copy-start | bytes 24772
  472.7 78.9 %copy-start.21 = (s32[516,8]{0,1:T(8,128)S(1)}, s32[516,8]{0,1:T(8,128)}, u32[]{:S(2)}) copy-start(s32[516,8]{0,1:T(8,128)} %param.28) | copy-start | bytes 49540
  472.7 79.0 %copy-start.17 = (s32[32,516]{1,0:T(8,128)S(1)}, s32[32,516]{1,0:T(8,128)}, u32[]{:S(2)}) copy-start(s32[32,516]{1,0:T(8,128)} %copy-done.16) | copy-start | bytes 198148
  472.7 79.0 %copy-start.19 = (pred[516,32]{0,1:T(8,128)(4,1)S(1)}, pred[516,32]{0,1:T(8,128)(4,1)}, u32[]{:S(2)}) copy-start(pred[516,32]{0,1:T(8,128)(4,1)} %copy-done.18) | copy-start | bytes 49540
  546.8 92.9 %all-to-all-start.4 = ((bf16[16,172,1024]{2,1,0:T(8,128)(2,1)}), bf16[16,172,1024]{2,1,0:T(8,128)(2,1)}, u32[]{:S(2)}, u32[]{:S(2)}) async-start(bf16[16,172,1024]{2,1,0:T(8,128)(2,1)} %convolution_convert_fusion.1), calls=%async_computation.4 | async-start | bytes 11534336 | tf_op jit(solution)/shard_map/all_to_all | solution.py:243
  560.2 79.6 %copy-start.29 = (bf16[516,1024]{1,0:T(8,128)(2,1)S(1)}, bf16[516,1024]{1,0:T(8,128)(2,1)}, u32[]{:S(2)}) copy-start(bf16[516,1024]{1,0:T(8,128)(2,1)} %copy-done.27) | copy-start | bytes 3170308
  639.7 8.7 %copy-start.1 = (bf16[4,1024]{1,0:T(4,128)(2,1)S(1)}, bf16[4,1024]{1,0:T(4,128)(2,1)}, u32[]{:S(2)}) copy-start(bf16[4,1024]{1,0:T(4,128)(2,1)} %param.16) | copy-start | bytes 24580
  (16 other events, 53.5 us)
Sparse Core Ops, SparseCore 0:
  11.9 34.1 all-gather.8
  47.7 64.7 all-gather.6

commit v3 on v2

--- a/solution.py
+++ b/solution.py
@@ -107,6 +107,15 @@
     pre_out = pre_out.reshape(part_count, pre_rows, columns)
     dec_out = dec_out.reshape(part_count, -1, columns)
     return jnp.concatenate([pre_out, dec_out], axis=1).reshape(-1, columns)
+
+
+def across_halves(shard):
+    halves = lax.axis_size("zh")
+    if halves == 1:
+        return shard[None]
+    other = lax.ppermute(shard, "zh", [(0, 1), (1, 0)])
+    first = lax.axis_index("zh") == 0
+    return jnp.stack([jnp.where(first, shard, other), jnp.where(first, other, shard)])
 
 
 def local(
@@ -171,16 +180,17 @@
     normed = root_norm(layer_input.astype(jnp.float32), attn_gain).astype(jnp.bfloat16)
     group_rows = lax.all_gather(normed, "mp", axis=0, tiled=True)
     local_width = qkv_weight.shape[1]
-    qkv_pair = lax.all_gather(qkv_weight, "zh", axis=0, tiled=False)
+    qkv_pair = across_halves(qkv_weight)
     qkv_full = lax.all_gather(qkv_pair, "dl", axis=0, tiled=False)
     qkv_full = jnp.swapaxes(qkv_full, 0, 1).reshape(-1, local_width)
+    qkv_full, out_source = lax.optimization_barrier((qkv_full, out_weight))
     projected = jnp.dot(group_rows, qkv_full, preferred_element_type=jnp.float32)
     local_groups = dec_cache.shape[0]
     projected = projected.reshape(part_count, rows_dev, local_groups, local_width // local_groups)
     attn_out = group_attention(
         projected, prior_cache[:, 0], dec_cache, dec_lengths, pre_offsets[0], pre_rows, head_dim
     )
-    out_pair = lax.all_gather(out_weight, "zh", axis=1, tiled=False)
+    out_pair = jnp.moveaxis(across_halves(out_source), 0, 1)
     out_full = lax.all_gather(out_pair, "dl", axis=1, tiled=False)
     out_full = jnp.swapaxes(out_full, 1, 2).reshape(out_weight.shape[0], -1)
     partial_sums = jnp.dot(attn_out, out_full, preferred_element_type=jnp.float32)
@@ -200,9 +210,16 @@
         both = jnp.broadcast_to(per_half[None], (halves,) + per_half.shape)
         return both.reshape((group_count, local_experts) + weights.shape[1:])
 
-    owned_gu, owned_dn = (
-        lax.all_to_all(owner_major(gate_up), dp, split_axis=0, concat_axis=2, tiled=True),
-        lax.all_to_all(owner_major(down_weight), dp, split_axis=0, concat_axis=2, tiled=True),
+    gu_rows = gate_up.shape[1]
+    owned = lax.all_to_all(
+        jnp.concatenate([owner_major(gate_up), owner_major(down_weight)], axis=2),
+        dp, split_axis=0, concat_axis=0, tiled=True,
+    )
+    owned_gu = jnp.moveaxis(owned[:, :, :gu_rows], 0, 1).reshape(
+        (1, local_experts, -1) + gate_up.shape[2:]
+    )
+    owned_dn = jnp.moveaxis(owned[:, :, gu_rows:], 0, 1).reshape(
+        (1, local_experts, -1) + down_weight.shape[2:]
     )
     full_gu, full_dn = (
         lax.all_gather(owned_gu, "mp", axis=3, tiled=True),

time: 663 us -> 636 us (0.959)
  blocking collectives: 11.5 us -> 0 us
  starting transfers between devices: 43.3 us -> 36.1 us
    ppermute x0 -> x2, waiting for transfers between devices: none -> 93 us  [across_halves(): other = lax.ppermute(shard, 'zh', [(0, 1), (1, 0)])]
    all_to_all x2 -> x1, waiting for transfers between devices: 61.7 us -> 0.01 us  [local(): lax.all_to_all(jnp.concatenate([owner_major(gate_up), owner_major(down_we...]
    all_gather x1, waiting for transfers between devices: 50.3 us -> 0.02 us  [local(): qkv_full = lax.all_gather(qkv_pair, 'dl', axis=0, tiled=False)]
    all_gather x1, waiting for transfers between devices: 0.02 us -> 14.5 us  [local(): out_full = lax.all_gather(out_pair, 'dl', axis=1, tiled=False)]
    all_gather x2 -> x0, blocking collectives: 11.5 us -> none  [the longest x1 6.28 us: local(): qkv_pair = lax.all_gather(qkv_weight, 'zh', axis=0, tiled=False)]
    dot_general x2 -> x0, local copies, waits for them, and re-layouts: 7.76 us -> none  [local(): jnp.dot(group_rows, qkv_full, preferred_element_type=jnp.float32)]
    unnamed x63 -> x61, local copies, waits for them, and re-layouts: 9.02 us -> 16.5 us
  transfers between devices with their start and end apart: 9 -> 10, of which waited for: 6 -> 7; matrix products, arithmetic and copies ran while one was open for 25% -> 25% of each run, Pallas kernels for 0% -> 0%
where the time goes in v3:
time: 636 us; the launch traced here: 629 us
  waiting for transfers between devices  402 us (63%)
  matrix products  108 us (17%)
  local copies, waits for them, and re-layouts  41.7 us (7%)
  starting transfers between devices  36.1 us (6%)
  other arithmetic  26.7 us (4%)
  between operations  14.8 us (2%)
    all_to_all x2, waiting for transfers between devices, local(): lax.all_to_all(outbound, 'dl', split_axis=0, concat_axis=0, tiled=True)  148 us
    all_to_all x2, waiting for transfers between devices, local(): lax.all_to_all(expert_out, 'dl', split_axis=0, concat_axis=0, tiled=True)  146 us
    ppermute x2, waiting for transfers between devices, across_halves(): other = lax.ppermute(shard, 'zh', [(0, 1), (1, 0)])  93 us
    sub x1, matrix products, prefill_attention(): expo = jnp.exp(scores - highest)  24 us
    dot_general x1, matrix products, prefill_attention(): jnp.einsum('gpck,gkh->cgph', weights, all_values, preferred_element_type=...  18.5 us
    dot_general x2, matrix products, local(): jnp.einsum('snd,df->snf', arrived, full_gu[l], preferred_element_type=jnp...  17.2 us
    unnamed x61, local copies, waits for them, and re-layouts  16.5 us
    dot_general x2, matrix products, local(): jnp.einsum('ecr,ecd->rd', combine_table[picked], returned, preferred_elem...  16.1 us
  transfers between devices with their start and end apart: 10, of which 7 were waited for; matrix products, arithmetic and copies ran while one was open for 25% of the time, Pallas kernels for 0%

profile of v3, /device:TPU:23, one launch (start us, length us, event | category | flops | bytes accessed | tf_op | source)
XLA Modules:
  0.0 628.9 jit_solution(2825508665208615183)
XLA Ops:
  6.6 5.4 collective-permute-done
  16.5 9.7 %all-to-all-start = ((bf16[32,2,512]{2,1,0:T(2,128)(2,1)}), bf16[32,2,512]{2,1,0:T(2,128)(2,1)S(1)}, u32[]{:S(2)}, u32[]{:S(2)}) async-start(bf16[32,2,512]{2,1,0:T(2,128)(2,1)} %reshape.494), calls=%async_computation | async-start | bytes 131072 | tf_op jit(solution)/shard_map/all_to_all | solution.py:163
  46.1 4.8 fusion.6
  51.0 5.8 all-to-all-start.2
  67.5 5.5 copy.102
  81.9 24.0 %fusion.95 = (f32[8,2,512]{2,1,0:T(2,128)S(1)}, f32[8,2,512,1536]{2,3,1,0:T(8,128)}) fusion(pred[512,1536]{0,1:T(8,128)(4,1)} %fusion.25, bf16[8,512,64]{1,2,0:T(8,128)(2,1)} %maximum_bitcast_fusion.13, bf16[8,1024,64]{1,2,0:T(8,128)(2,1)S(1)} %copy-done.11, bf16[512,8,2,32]{0,3,2,1:T(8,128)(2,1)} %get-tuple-element.12, ...), kind=kOutput, calls=%fused_computation.162 | convolution fusion | flops 1666188800 | bytes 53772288 | tf_op jit(solution)/shard_map/sub | solution.py:60
  107.4 87.6 %collective-permute-done.1 = bf16[1024,32]{0,1:T(8,128)(2,1)S(1)} collective-permute-done((bf16[1024,32]{0,1:T(8,128)(2,1)S(1)}, bf16[1024,32]{0,1:T(8,128)(2,1)S(1)}, u32[]{:S(2)}, u32[]{:S(2)}) %collective-permute-start.1) | collective-permute-done | bytes 65568 | tf_op jit(solution)/shard_map/ppermute | solution.py:116
  195.7 18.5 %fusion.43 = bf16[8,64,2,512]{3,1,2,0:T(8,128)(2,1)} fusion(f32[8,2,512,1536]{2,3,1,0:T(8,128)} %get-tuple-element.34, f32[8,2,512]{2,1,0:T(2,128)S(1)} %get-tuple-element.33, bf16[8,512,64]{1,2,0:T(8,128)(2,1)S(1)} %fusion.66, bf16[8,1024,64]{1,2,0:T(8,128)(2,1)S(1)} %copy-done.10), kind=kOutput, calls=%fused_computation.59 | convolution fusion | flops 1639448576 | bytes 52985856 | tf_op jit(solution)/shard_map/gpck,gkh->cgph/dot_general | solution.py:62
  214.2 14.5 %all-gather.7.cloned.1.call-done = bf16[1024,32,32]{0,2,1:T(8,128)(2,1)} async-done(((bf16[1024,2,32]{0,2,1:T(8,128)(2,1)}), bf16[1024,32,32]{0,2,1:T(8,128)(2,1)}) %all-gather.7.cloned.1.call-update) | async-done | bytes 2097168 | tf_op jit(solution)/shard_map/all_gather | solution.py:194
  233.2 7.3 %fusion.22 = bf16[16,172,1024]{2,1,0:T(8,128)(2,1)} fusion(pred[32,172,516]{2,1,0:T(8,128)(4,1)S(1)} %copy-done.5, bf16[516,1024]{1,0:T(8,128)(2,1)S(1)} %get-tuple-element.36, f32[1024]{0:T(1024)S(1)} %copy-done.21, f32[516]{0:T(1024)S(1)} %add_rsqrt_fusion, bf16[4,1024]{1,0:T(4,128)(2,1)S(1)} %convolution_convert_fusion.4, bf16[512,1024]{1,0:T(8,128)(2,1)S(1)} %copy-done.9), kind=kOutput, calls=%fused_computation.29 | convolution fusion | flops 2915799040 | bytes 9568256 | tf_op jit(solution)/shard_map/ecr,rd->ecd/dot_general | solution.py:248
  240.5 5.9 all-to-all-start.4
  246.4 8.2 %fusion.19 = bf16[16,172,1024]{2,1,0:T(8,128)(2,1)} fusion(pred[32,172,516]{2,1,0:T(8,128)(4,1)} %fusion.6, bf16[516,1024]{1,0:T(8,128)(2,1)S(1)} %copy-done.26, f32[1024]{0:T(1024)S(1)} %copy-done.21, f32[516]{0:T(1024)S(1)} %add_rsqrt_fusion, bf16[4,1024]{1,0:T(4,128)(2,1)S(1)} %convolution_convert_fusion.4, bf16[512,1024]{1,0:T(8,128)(2,1)S(1)} %copy-done.9), kind=kOutput, calls=%fused_computation.28 | convolution fusion | flops 2915799040 | bytes 9558032 | tf_op jit(solution)/shard_map/ecr,rd->ecd/dot_general | solution.py:248
  254.6 80.6 %all-to-all-done.4 = bf16[16,172,1024]{2,1,0:T(8,128)(2,1)} async-done(((bf16[16,172,1024]{2,1,0:T(8,128)(2,1)}), bf16[16,172,1024]{2,1,0:T(8,128)(2,1)}, u32[]{:S(2)}, u32[]{:S(2)}) %all-to-all-start.4) | async-done | bytes 5636128 | tf_op jit(solution)/shard_map/all_to_all | solution.py:252
  346.6 8.3 %fusion.33 = f32[16,172,1024]{2,1,0:T(8,128)S(1)} fusion(bf16[16,172,1024]{2,1,0:T(8,128)(2,1)} %all-to-all-done.4, bf16[1,2,1024,1024]{3,2,1,0:T(8,128)(2,1)S(1)} %bitcast.161), kind=kOutput, calls=%fused_computation.46 | convolution fusion | flops 5771362304 | bytes 19005440 | tf_op jit(solution)/shard_map/snd,df->snf/dot_general | solution.py:253
  354.9 5.1 convolution_convert_fusion
  360.0 67.7 %all-to-all-done.1 = bf16[16,172,1024]{2,1,0:T(8,128)(2,1)} async-done(((bf16[16,172,1024]{2,1,0:T(8,128)(2,1)}), bf16[16,172,1024]{2,1,0:T(8,128)(2,1)}, u32[]{:S(2)}, u32[]{:S(2)}) %all-to-all-start.1) | async-done | bytes 5636128 | tf_op jit(solution)/shard_map/all_to_all | solution.py:252
  427.7 4.7 all-to-all-start.5
  432.4 8.9 %fusion.34 = f32[16,172,1024]{2,1,0:T(8,128)S(1)} fusion(bf16[16,172,1024]{2,1,0:T(8,128)(2,1)} %all-to-all-done.1, bf16[1,2,1024,1024]{3,2,1,0:T(8,128)(2,1)} %bitcast.162), kind=kOutput, calls=%fused_computation.49 | convolution fusion | flops 5771362304 | bytes 19136512 | tf_op jit(solution)/shard_map/snd,df->snf/dot_general | solution.py:253
  441.3 5.1 convolution_convert_fusion.1
  446.5 74.1 %all-to-all-done.5 = bf16[16,172,1024]{2,1,0:T(8,128)(2,1)} async-done(((bf16[16,172,1024]{2,1,0:T(8,128)(2,1)}), bf16[16,172,1024]{2,1,0:T(8,128)(2,1)}, u32[]{:S(2)}, u32[]{:S(2)}) %all-to-all-start.5) | async-done | bytes 5636128 | tf_op jit(solution)/shard_map/all_to_all | solution.py:260
  525.2 5.5 select_convert_fusion
  533.6 7.4 %fusion.15 = f32[516,1024,1]{1,0,2:T(8,128)} fusion(bf16[16,172,1024]{2,1,0:T(8,128)(2,1)} %all-to-all-done.5, bf16[32,172,516]{2,1,0:T(8,128)(2,1)S(1)} %select_convert_fusion), kind=kOutput, calls=%fused_computation.24 | convolution fusion | flops 2908225536 | bytes 11354112 | tf_op jit(solution)/shard_map/ecr,ecd->rd/dot_general | solution.py:262
  541.1 72.1 %all-to-all-done.3 = bf16[16,172,1024]{2,1,0:T(8,128)(2,1)} async-done(((bf16[16,172,1024]{2,1,0:T(8,128)(2,1)}), bf16[16,172,1024]{2,1,0:T(8,128)(2,1)}, u32[]{:S(2)}, u32[]{:S(2)}) %all-to-all-start.3) | async-done | bytes 5636128 | tf_op jit(solution)/shard_map/all_to_all | solution.py:260
  613.2 8.7 %fusion.32 = bf16[516,1024]{1,0:T(8,128)(2,1)} fusion(f32[516,1024,1]{1,0,2:T(8,128)} %fusion.15, bf16[516,1024]{1,0:T(8,128)(2,1)S(1)} %copy-done.27, bf16[16,172,1024]{2,1,0:T(8,128)(2,1)} %all-to-all-done.3, bf16[32,172,516]{2,1,0:T(8,128)(2,1)} %copy-done.3, bf16[4,1024]{1,0:T(4,128)(2,1)S(1)} %convolution_convert_fusion.4, ...), kind=kOutput, calls=%fused_computation.42 | convolution fusion | flops 2912980992 | bytes 14671872 | tf_op jit(solution)/shard_map/ecr,ecd->rd/dot_general | solution.py:262
  (138 shorter events, 68.7 us)
Async XLA Ops:
  6.5 8.0 %copy-start = (bf16[4,1024]{1,0:T(4,128)(2,1)S(1)}, bf16[4,1024]{1,0:T(4,128)(2,1)}, u32[]{:S(2)}) copy-start(bf16[4,1024]{1,0:T(4,128)(2,1)} %param.16) | copy-start | bytes 24580
  6.5 51.4 %all-gather.5.cloned.1.call-start = ((), (), s32[]{:S(2)}) async-start(), calls=%async_computation.6 | async-start | bytes 4456448 | tf_op jit(solution)/shard_map/all_gather | solution.py:184
  6.5 5.5 collective-permute-start
  6.6 23.1 %copy-start.23 = (s32[4]{0:T(128)S(1)}, s32[4]{0:T(128)}, u32[]{:S(2)}) copy-start(s32[4]{0:T(128)} %param.18) | copy-start | bytes 52
  6.6 23.2 %copy-start.16 = (s32[516,8]{0,1:T(8,128)S(1)}, s32[516,8]{0,1:T(8,128)}, u32[]{:S(2)}) copy-start(s32[516,8]{0,1:T(8,128)} %param.28) | copy-start | bytes 49540
  13.0 18.7 %copy-start.22 = (s32[128]{0:T(128)S(1)}, s32[128]{0:T(128)}, u32[]{:S(2)}) copy-start(s32[128]{0:T(128)} %param.17) | copy-start | bytes 1540
  16.5 34.5 %all-to-all-start = ((bf16[32,2,512]{2,1,0:T(2,128)(2,1)}), bf16[32,2,512]{2,1,0:T(2,128)(2,1)S(1)}, u32[]{:S(2)}, u32[]{:S(2)}) async-start(bf16[32,2,512]{2,1,0:T(2,128)(2,1)} %reshape.494), calls=%async_computation | async-start | bytes 131072 | tf_op jit(solution)/shard_map/all_to_all | solution.py:163
  29.8 16.3 %copy-start.14 = (pred[516,32]{0,1:T(8,128)(4,1)}, pred[516,32]{0,1:T(8,128)(4,1)S(1)}, u32[]{:S(2)}) copy-start(pred[516,32]{0,1:T(8,128)(4,1)S(1)} %fusion.65) | copy-start | bytes 49540
  32.5 13.7 %copy-start.12 = (s32[32,516]{1,0:T(8,128)}, s32[32,516]{1,0:T(8,128)S(1)}, u32[]{:S(2)}) copy-start(s32[32,516]{1,0:T(8,128)S(1)} %fusion.67) | copy-start | bytes 198148
  51.0 189.5 %all-to-all-start.2 = ((bf16[32,2,48,1024]{3,2,1,0:T(8,128)(2,1)}), bf16[32,2,48,1024]{3,2,1,0:T(8,128)(2,1)}, u32[]{:S(2)}, u32[]{:S(2)}) async-start(bf16[32,2,48,1024]{3,2,1,0:T(8,128)(2,1)} %pad_maximum_fusion), calls=%async_computation.2 | async-start | bytes 12582912 | tf_op jit(solution)/shard_map/all_to_all | solution.py:214
  56.8 171.8 %all-gather.7.cloned.1.call-start = ((), (), s32[]{:S(2)}) async-start(), calls=%async_computation.7 | async-start | bytes 2228224 | tf_op jit(solution)/shard_map/all_gather | solution.py:194
  75.2 119.7 %collective-permute-start.1 = (bf16[1024,32]{0,1:T(8,128)(2,1)S(1)}, bf16[1024,32]{0,1:T(8,128)(2,1)S(1)}, u32[]{:S(2)}, u32[]{:S(2)}) collective-permute-start(bf16[1024,32]{0,1:T(8,128)(2,1)S(1)} %copy-done.18), channel_id=1, source_target_pairs={{0,16},{16,0},{1,17},{17,1},{2,18},{18,2},{3,19},{19,3},{4,20},{20... | collective-permute-start | bytes 196616 | tf_op jit(solution)/shard_map/ppermute | solution.py:116
  81.8 113.8 %copy-start.10 = (bf16[8,1024,64]{1,2,0:T(8,128)(2,1)S(1)}, bf16[8,1024,64]{1,2,0:T(8,128)(2,1)}, u32[]{:S(2)}) copy-start(bf16[8,1024,64]{1,2,0:T(8,128)(2,1)} %get-tuple-element.13) | copy-start | bytes 3145732
  214.2 16.3 %copy-start.24 = (bf16[8,64,2,512]{3,1,2,0:T(8,128)(2,1)S(1)}, bf16[8,64,2,512]{3,1,2,0:T(8,128)(2,1)}, u32[]{:S(2)}) copy-start(bf16[8,64,2,512]{3,1,2,0:T(8,128)(2,1)} %fusion.43) | copy-start | bytes 3145732
  240.5 94.7 %all-to-all-start.4 = ((bf16[16,172,1024]{2,1,0:T(8,128)(2,1)}), bf16[16,172,1024]{2,1,0:T(8,128)(2,1)}, u32[]{:S(2)}, u32[]{:S(2)}) async-start(bf16[16,172,1024]{2,1,0:T(8,128)(2,1)} %fusion.22), calls=%async_computation.4 | async-start | bytes 11534336 | tf_op jit(solution)/shard_map/all_to_all | solution.py:252
  335.1 92.6 %all-to-all-start.1 = ((bf16[16,172,1024]{2,1,0:T(8,128)(2,1)}), bf16[16,172,1024]{2,1,0:T(8,128)(2,1)}, u32[]{:S(2)}, u32[]{:S(2)}) async-start(bf16[16,172,1024]{2,1,0:T(8,128)(2,1)} %fusion.19), calls=%async_computation.1 | async-start | bytes 11534336 | tf_op jit(solution)/shard_map/all_to_all | solution.py:252
  427.7 92.8 %all-to-all-start.5 = ((bf16[16,172,1024]{2,1,0:T(8,128)(2,1)}), bf16[16,172,1024]{2,1,0:T(8,128)(2,1)}, u32[]{:S(2)}, u32[]{:S(2)}) async-start(bf16[16,172,1024]{2,1,0:T(8,128)(2,1)} %convolution_convert_fusion), calls=%async_computation.5 | async-start | bytes 11534336 | tf_op jit(solution)/shard_map/all_to_all | solution.py:260
  446.5 78.6 %copy-start.19 = (bf16[516,8]{0,1:T(8,128)(2,1)S(1)}, bf16[516,8]{0,1:T(8,128)(2,1)}, u32[]{:S(2)}) copy-start(bf16[516,8]{0,1:T(8,128)(2,1)} %param.29) | copy-start | bytes 24772
  446.5 78.6 %copy-start.17 = (s32[516,8]{0,1:T(8,128)S(1)}, s32[516,8]{0,1:T(8,128)}, u32[]{:S(2)}) copy-start(s32[516,8]{0,1:T(8,128)} %param.28) | copy-start | bytes 49540
  446.5 78.7 %copy-start.13 = (s32[32,516]{1,0:T(8,128)S(1)}, s32[32,516]{1,0:T(8,128)}, u32[]{:S(2)}) copy-start(s32[32,516]{1,0:T(8,128)} %copy-done.12) | copy-start | bytes 198148
  446.5 78.7 %copy-start.15 = (pred[516,32]{0,1:T(8,128)(4,1)S(1)}, pred[516,32]{0,1:T(8,128)(4,1)}, u32[]{:S(2)}) copy-start(pred[516,32]{0,1:T(8,128)(4,1)} %copy-done.14) | copy-start | bytes 49540
  520.5 92.7 %all-to-all-start.3 = ((bf16[16,172,1024]{2,1,0:T(8,128)(2,1)}), bf16[16,172,1024]{2,1,0:T(8,128)(2,1)}, u32[]{:S(2)}, u32[]{:S(2)}) async-start(bf16[16,172,1024]{2,1,0:T(8,128)(2,1)} %convolution_convert_fusion.1), calls=%async_computation.3 | async-start | bytes 11534336 | tf_op jit(solution)/shard_map/all_to_all | solution.py:260
  533.6 79.6 %copy-start.27 = (bf16[516,1024]{1,0:T(8,128)(2,1)S(1)}, bf16[516,1024]{1,0:T(8,128)(2,1)}, u32[]{:S(2)}) copy-start(bf16[516,1024]{1,0:T(8,128)(2,1)} %copy-done.25) | copy-start | bytes 3170308
  613.2 8.7 %copy-start.1 = (bf16[4,1024]{1,0:T(4,128)(2,1)S(1)}, bf16[4,1024]{1,0:T(4,128)(2,1)}, u32[]{:S(2)}) copy-start(bf16[4,1024]{1,0:T(4,128)(2,1)} %param.16) | copy-start | bytes 24580
  (14 other events, 41.6 us)
Sparse Core Ops, SparseCore 0:
  13.9 38.7 all-gather.4
  195.8 32.8 all-gather.6

commit v4 on v3

--- a/solution.py
+++ b/solution.py
@@ -181,16 +181,16 @@
     group_rows = lax.all_gather(normed, "mp", axis=0, tiled=True)
     local_width = qkv_weight.shape[1]
     qkv_pair = across_halves(qkv_weight)
+    out_pair = jnp.moveaxis(across_halves(out_weight), 0, 1)
     qkv_full = lax.all_gather(qkv_pair, "dl", axis=0, tiled=False)
     qkv_full = jnp.swapaxes(qkv_full, 0, 1).reshape(-1, local_width)
-    qkv_full, out_source = lax.optimization_barrier((qkv_full, out_weight))
+    qkv_full, out_pair = lax.optimization_barrier((qkv_full, out_pair))
     projected = jnp.dot(group_rows, qkv_full, preferred_element_type=jnp.float32)
     local_groups = dec_cache.shape[0]
     projected = projected.reshape(part_count, rows_dev, local_groups, local_width // local_groups)
     attn_out = group_attention(
         projected, prior_cache[:, 0], dec_cache, dec_lengths, pre_offsets[0], pre_rows, head_dim
     )
-    out_pair = jnp.moveaxis(across_halves(out_source), 0, 1)
     out_full = lax.all_gather(out_pair, "dl", axis=1, tiled=False)
     out_full = jnp.swapaxes(out_full, 1, 2).reshape(out_weight.shape[0], -1)
     partial_sums = jnp.dot(attn_out, out_full, preferred_element_type=jnp.float32)

time: 636 us -> 593 us (0.932)
  waiting for transfers between devices: 402 us -> 352 us
    ppermute x2, waiting for transfers between devices: 93 us -> 5.44 us  [across_halves(): other = lax.ppermute(shard, 'zh', [(0, 1), (1, 0)])]
    all_to_all x1, waiting for transfers between devices: 0.01 us -> 44 us  [local(): lax.all_to_all(jnp.concatenate([owner_major(gate_up), owner_major(down_we...]
    all_gather x1, waiting for transfers between devices: 14.5 us -> 7.92 us  [local(): out_full = lax.all_gather(out_pair, 'dl', axis=1, tiled=False)]
    unnamed x61 -> x59, local copies, waits for them, and re-layouts: 16.5 us -> 15.9 us
  transfers between devices with their start and end apart: 10 -> 10, of which waited for: 7 -> 7; matrix products, arithmetic and copies ran while one was open for 25% -> 28% of each run, Pallas kernels for 0% -> 0%
where the time goes in v4:
time: 593 us; the launch traced here: 583 us
  waiting for transfers between devices  352 us (59%)
  matrix products  110 us (19%)
  local copies, waits for them, and re-layouts  42.6 us (7%)
  starting transfers between devices  37 us (6%)
  other arithmetic  26.7 us (5%)
  between operations  14.8 us (2%)
    all_to_all x2, waiting for transfers between devices, local(): lax.all_to_all(outbound, 'dl', split_axis=0, concat_axis=0, tiled=True)  148 us
    all_to_all x2, waiting for transfers between devices, local(): lax.all_to_all(expert_out, 'dl', split_axis=0, concat_axis=0, tiled=True)  146 us
    all_to_all x1, waiting for transfers between devices, local(): lax.all_to_all(jnp.concatenate([owner_major(gate_up), owner_major(down_we...  44 us
    sub x1, matrix products, prefill_attention(): expo = jnp.exp(scores - highest)  24.1 us
    dot_general x1, matrix products, prefill_attention(): jnp.einsum('gpck,gkh->cgph', weights, all_values, preferred_element_type=...  18.4 us
    dot_general x2, matrix products, local(): jnp.einsum('snd,df->snf', arrived, full_gu[l], preferred_element_type=jnp...  17.2 us
    dot_general x2, matrix products, local(): jnp.einsum('ecr,ecd->rd', combine_table[picked], returned, preferred_elem...  16.1 us
    unnamed x59, local copies, waits for them, and re-layouts  15.9 us
  transfers between devices with their start and end apart: 10, of which 7 were waited for; matrix products, arithmetic and copies ran while one was open for 28% of the time, Pallas kernels for 0%

profile of v4, /device:TPU:23, one launch (start us, length us, event | category | flops | bytes accessed | tf_op | source)
XLA Modules:
  0.0 583.0 jit_solution(8145843682763460705)
XLA Ops:
  6.6 5.4 collective-permute-done
  16.5 9.7 %all-to-all-start = ((bf16[32,2,512]{2,1,0:T(2,128)(2,1)}), bf16[32,2,512]{2,1,0:T(2,128)(2,1)S(1)}, u32[]{:S(2)}, u32[]{:S(2)}) async-start(bf16[32,2,512]{2,1,0:T(2,128)(2,1)} %reshape.494), calls=%async_computation | async-start | bytes 131072 | tf_op jit(solution)/shard_map/all_to_all | solution.py:163
  46.5 4.8 fusion.6
  52.1 6.2 %all-to-all-start.2 = ((bf16[32,2,48,1024]{3,2,1,0:T(8,128)(2,1)}), bf16[32,2,48,1024]{3,2,1,0:T(8,128)(2,1)}, u32[]{:S(2)}, u32[]{:S(2)}) async-start(bf16[32,2,48,1024]{3,2,1,0:T(8,128)(2,1)} %pad_maximum_fusion), calls=%async_computation.2 | async-start | bytes 12582912 | tf_op jit(solution)/shard_map/all_to_all | solution.py:214
  68.8 5.6 copy.102
  87.4 24.1 %fusion.95 = (f32[8,2,512]{2,1,0:T(2,128)S(1)}, f32[8,2,512,1536]{2,3,1,0:T(8,128)}) fusion(pred[512,1536]{0,1:T(8,128)(4,1)} %fusion.25, bf16[8,512,64]{1,2,0:T(8,128)(2,1)} %maximum_bitcast_fusion.13, bf16[8,1024,64]{1,2,0:T(8,128)(2,1)} %get-tuple-element.14, bf16[512,8,2,32]{0,3,2,1:T(8,128)(2,1)} %get-tuple-element.12, ...), kind=kOutput, calls=%fused_computation.162 | convolution fusion | flops 1666188800 | bytes 53772288 | tf_op jit(solution)/shard_map/sub | solution.py:60
  111.5 18.4 %fusion.43 = bf16[8,64,2,512]{3,1,2,0:T(8,128)(2,1)} fusion(f32[8,2,512,1536]{2,3,1,0:T(8,128)} %get-tuple-element.34, f32[8,2,512]{2,1,0:T(2,128)S(1)} %get-tuple-element.33, bf16[8,512,64]{1,2,0:T(8,128)(2,1)S(1)} %copy-done.12, bf16[8,1024,64]{1,2,0:T(8,128)(2,1)S(1)} %copy-done.9), kind=kOutput, calls=%fused_computation.59 | convolution fusion | flops 1639448576 | bytes 52985856 | tf_op jit(solution)/shard_map/gpck,gkh->cgph/dot_general | solution.py:62
  129.9 7.9 %all-gather.7.cloned.1.call-done = bf16[1024,32,32]{0,2,1:T(8,128)(2,1)} async-done(((bf16[1024,2,32]{0,2,1:T(8,128)(2,1)}), bf16[1024,32,32]{0,2,1:T(8,128)(2,1)}) %all-gather.7.cloned.1.call-update) | async-done | bytes 2097168 | tf_op jit(solution)/shard_map/all_gather | solution.py:194
  142.4 7.3 %fusion.22 = bf16[16,172,1024]{2,1,0:T(8,128)(2,1)} fusion(pred[32,172,516]{2,1,0:T(8,128)(4,1)S(1)} %copy-done.5, bf16[516,1024]{1,0:T(8,128)(2,1)S(1)} %get-tuple-element.36, f32[1024]{0:T(1024)S(1)} %copy-done.20, f32[516]{0:T(1024)S(1)} %add_rsqrt_fusion, bf16[4,1024]{1,0:T(4,128)(2,1)S(1)} %convolution_convert_fusion.4, bf16[512,1024]{1,0:T(8,128)(2,1)S(1)} %copy-done.8), kind=kOutput, calls=%fused_computation.29 | convolution fusion | flops 2915799040 | bytes 9568256 | tf_op jit(solution)/shard_map/ecr,rd->ecd/dot_general | solution.py:248
  149.7 44.0 %all-to-all-done.2 = bf16[32,2,48,1024]{3,2,1,0:T(8,128)(2,1)} async-done(((bf16[32,2,48,1024]{3,2,1,0:T(8,128)(2,1)}), bf16[32,2,48,1024]{3,2,1,0:T(8,128)(2,1)}, u32[]{:S(2)}, u32[]{:S(2)}) %all-to-all-start.2) | async-done | bytes 6291488 | tf_op jit(solution)/shard_map/all_to_all | solution.py:214
  193.8 6.7 %all-to-all-start.4 = ((bf16[16,172,1024]{2,1,0:T(8,128)(2,1)}), bf16[16,172,1024]{2,1,0:T(8,128)(2,1)}, u32[]{:S(2)}, u32[]{:S(2)}) async-start(bf16[16,172,1024]{2,1,0:T(8,128)(2,1)} %fusion.22), calls=%async_computation.4 | async-start | bytes 11534336 | tf_op jit(solution)/shard_map/all_to_all | solution.py:252
  200.5 8.2 %fusion.19 = bf16[16,172,1024]{2,1,0:T(8,128)(2,1)} fusion(pred[32,172,516]{2,1,0:T(8,128)(4,1)} %fusion.6, bf16[516,1024]{1,0:T(8,128)(2,1)S(1)} %copy-done.25, f32[1024]{0:T(1024)S(1)} %copy-done.20, f32[516]{0:T(1024)S(1)} %add_rsqrt_fusion, bf16[4,1024]{1,0:T(4,128)(2,1)S(1)} %convolution_convert_fusion.4, bf16[512,1024]{1,0:T(8,128)(2,1)S(1)} %copy-done.8), kind=kOutput, calls=%fused_computation.28 | convolution fusion | flops 2915799040 | bytes 9558032 | tf_op jit(solution)/shard_map/ecr,rd->ecd/dot_general | solution.py:248
  208.7 80.5 %all-to-all-done.4 = bf16[16,172,1024]{2,1,0:T(8,128)(2,1)} async-done(((bf16[16,172,1024]{2,1,0:T(8,128)(2,1)}), bf16[16,172,1024]{2,1,0:T(8,128)(2,1)}, u32[]{:S(2)}, u32[]{:S(2)}) %all-to-all-start.4) | async-done | bytes 5636128 | tf_op jit(solution)/shard_map/all_to_all | solution.py:252
  300.6 8.3 %fusion.33 = f32[16,172,1024]{2,1,0:T(8,128)S(1)} fusion(bf16[16,172,1024]{2,1,0:T(8,128)(2,1)} %all-to-all-done.4, bf16[1,2,1024,1024]{3,2,1,0:T(8,128)(2,1)S(1)} %bitcast.161), kind=kOutput, calls=%fused_computation.46 | convolution fusion | flops 5771362304 | bytes 19005440 | tf_op jit(solution)/shard_map/snd,df->snf/dot_general | solution.py:253
  308.9 5.1 convolution_convert_fusion
  314.0 67.8 %all-to-all-done.1 = bf16[16,172,1024]{2,1,0:T(8,128)(2,1)} async-done(((bf16[16,172,1024]{2,1,0:T(8,128)(2,1)}), bf16[16,172,1024]{2,1,0:T(8,128)(2,1)}, u32[]{:S(2)}, u32[]{:S(2)}) %all-to-all-start.1) | async-done | bytes 5636128 | tf_op jit(solution)/shard_map/all_to_all | solution.py:252
  381.8 4.7 all-to-all-start.5
  386.5 8.9 %fusion.34 = f32[16,172,1024]{2,1,0:T(8,128)S(1)} fusion(bf16[16,172,1024]{2,1,0:T(8,128)(2,1)} %all-to-all-done.1, bf16[1,2,1024,1024]{3,2,1,0:T(8,128)(2,1)} %bitcast.162), kind=kOutput, calls=%fused_computation.49 | convolution fusion | flops 5771362304 | bytes 19136512 | tf_op jit(solution)/shard_map/snd,df->snf/dot_general | solution.py:253
  395.4 5.2 convolution_convert_fusion.1
  400.5 74.0 %all-to-all-done.5 = bf16[16,172,1024]{2,1,0:T(8,128)(2,1)} async-done(((bf16[16,172,1024]{2,1,0:T(8,128)(2,1)}), bf16[16,172,1024]{2,1,0:T(8,128)(2,1)}, u32[]{:S(2)}, u32[]{:S(2)}) %all-to-all-start.5) | async-done | bytes 5636128 | tf_op jit(solution)/shard_map/all_to_all | solution.py:260
  479.3 5.5 select_convert_fusion
  487.7 7.4 %fusion.15 = f32[516,1024,1]{1,0,2:T(8,128)} fusion(bf16[16,172,1024]{2,1,0:T(8,128)(2,1)} %all-to-all-done.5, bf16[32,172,516]{2,1,0:T(8,128)(2,1)S(1)} %select_convert_fusion), kind=kOutput, calls=%fused_computation.24 | convolution fusion | flops 2908225536 | bytes 11354112 | tf_op jit(solution)/shard_map/ecr,ecd->rd/dot_general | solution.py:262
  495.1 72.1 %all-to-all-done.3 = bf16[16,172,1024]{2,1,0:T(8,128)(2,1)} async-done(((bf16[16,172,1024]{2,1,0:T(8,128)(2,1)}), bf16[16,172,1024]{2,1,0:T(8,128)(2,1)}, u32[]{:S(2)}, u32[]{:S(2)}) %all-to-all-start.3) | async-done | bytes 5636128 | tf_op jit(solution)/shard_map/all_to_all | solution.py:260
  567.3 8.7 %fusion.32 = bf16[516,1024]{1,0:T(8,128)(2,1)} fusion(f32[516,1024,1]{1,0,2:T(8,128)} %fusion.15, bf16[516,1024]{1,0:T(8,128)(2,1)S(1)} %copy-done.26, bf16[16,172,1024]{2,1,0:T(8,128)(2,1)} %all-to-all-done.3, bf16[32,172,516]{2,1,0:T(8,128)(2,1)} %copy-done.3, bf16[4,1024]{1,0:T(4,128)(2,1)S(1)} %convolution_convert_fusion.4, ...), kind=kOutput, calls=%fused_computation.42 | convolution fusion | flops 2912980992 | bytes 14671872 | tf_op jit(solution)/shard_map/ecr,ecd->rd/dot_general | solution.py:262
  (136 shorter events, 71.5 us)
Async XLA Ops:
  6.5 52.6 %all-gather.5.cloned.1.call-start = ((), (), s32[]{:S(2)}) async-start(), calls=%async_computation.6 | async-start | bytes 4456448 | tf_op jit(solution)/shard_map/all_gather | solution.py:185
  6.5 5.5 collective-permute-start
  6.6 23.5 %copy-start.22 = (s32[4]{0:T(128)S(1)}, s32[4]{0:T(128)}, u32[]{:S(2)}) copy-start(s32[4]{0:T(128)} %param.18) | copy-start | bytes 52
  6.6 23.5 %copy-start.15 = (s32[516,8]{0,1:T(8,128)S(1)}, s32[516,8]{0,1:T(8,128)}, u32[]{:S(2)}) copy-start(s32[516,8]{0,1:T(8,128)} %param.28) | copy-start | bytes 49540
  13.0 19.0 %copy-start.21 = (s32[128]{0:T(128)S(1)}, s32[128]{0:T(128)}, u32[]{:S(2)}) copy-start(s32[128]{0:T(128)} %param.17) | copy-start | bytes 1540
  16.5 35.6 %all-to-all-start = ((bf16[32,2,512]{2,1,0:T(2,128)(2,1)}), bf16[32,2,512]{2,1,0:T(2,128)(2,1)S(1)}, u32[]{:S(2)}, u32[]{:S(2)}) async-start(bf16[32,2,512]{2,1,0:T(2,128)(2,1)} %reshape.494), calls=%async_computation | async-start | bytes 131072 | tf_op jit(solution)/shard_map/all_to_all | solution.py:163
  26.2 25.1 %collective-permute-start.1 = (bf16[1024,32]{0,1:T(8,128)(2,1)}, bf16[1024,32]{0,1:T(8,128)(2,1)S(1)}, u32[]{:S(2)}, u32[]{:S(2)}) collective-permute-start(bf16[1024,32]{0,1:T(8,128)(2,1)} %param.25), channel_id=1, source_target_pairs={{0,16},{16,0},{1,17},{17,1},{2,18},{18,2},{3,19},{19,3},{4,20},{20... | collective-permute-start | bytes 196616 | tf_op jit(solution)/shard_map/ppermute | solution.py:116
  30.2 16.3 %copy-start.13 = (pred[516,32]{0,1:T(8,128)(4,1)}, pred[516,32]{0,1:T(8,128)(4,1)S(1)}, u32[]{:S(2)}) copy-start(pred[516,32]{0,1:T(8,128)(4,1)S(1)} %fusion.65) | copy-start | bytes 49540
  32.8 13.7 %copy-start.10 = (s32[32,516]{1,0:T(8,128)}, s32[32,516]{1,0:T(8,128)S(1)}, u32[]{:S(2)}) copy-start(s32[32,516]{1,0:T(8,128)S(1)} %fusion.67) | copy-start | bytes 198148
  52.1 141.7 %all-to-all-start.2 = ((bf16[32,2,48,1024]{3,2,1,0:T(8,128)(2,1)}), bf16[32,2,48,1024]{3,2,1,0:T(8,128)(2,1)}, u32[]{:S(2)}, u32[]{:S(2)}) async-start(bf16[32,2,48,1024]{3,2,1,0:T(8,128)(2,1)} %pad_maximum_fusion), calls=%async_computation.2 | async-start | bytes 12582912 | tf_op jit(solution)/shard_map/all_to_all | solution.py:214
  58.3 79.5 %all-gather.7.cloned.1.call-start = ((), (), s32[]{:S(2)}) async-start(), calls=%async_computation.7 | async-start | bytes 2228224 | tf_op jit(solution)/shard_map/all_gather | solution.py:194
  87.4 24.1 %copy-start.9 = (bf16[8,1024,64]{1,2,0:T(8,128)(2,1)S(1)}, bf16[8,1024,64]{1,2,0:T(8,128)(2,1)}, u32[]{:S(2)}) copy-start(bf16[8,1024,64]{1,2,0:T(8,128)(2,1)} %get-tuple-element.13) | copy-start | bytes 3145732
  87.4 24.1 %copy-start.12 = (bf16[8,512,64]{1,2,0:T(8,128)(2,1)S(1)}, bf16[8,512,64]{1,2,0:T(8,128)(2,1)}, u32[]{:S(2)}) copy-start(bf16[8,512,64]{1,2,0:T(8,128)(2,1)} %fusion.66) | copy-start | bytes 1572868
  129.9 9.7 %copy-start.23 = (bf16[8,64,2,512]{3,1,2,0:T(8,128)(2,1)S(1)}, bf16[8,64,2,512]{3,1,2,0:T(8,128)(2,1)}, u32[]{:S(2)}) copy-start(bf16[8,64,2,512]{3,1,2,0:T(8,128)(2,1)} %fusion.43) | copy-start | bytes 3145732
  149.7 50.7 %copy-start.25 = (bf16[516,1024]{1,0:T(8,128)(2,1)S(1)}, bf16[516,1024]{1,0:T(8,128)(2,1)}, u32[]{:S(2)}) copy-start(bf16[516,1024]{1,0:T(8,128)(2,1)} %copy-done.24) | copy-start | bytes 3170308
  193.8 95.4 %all-to-all-start.4 = ((bf16[16,172,1024]{2,1,0:T(8,128)(2,1)}), bf16[16,172,1024]{2,1,0:T(8,128)(2,1)}, u32[]{:S(2)}, u32[]{:S(2)}) async-start(bf16[16,172,1024]{2,1,0:T(8,128)(2,1)} %fusion.22), calls=%async_computation.4 | async-start | bytes 11534336 | tf_op jit(solution)/shard_map/all_to_all | solution.py:252
  289.1 92.7 %all-to-all-start.1 = ((bf16[16,172,1024]{2,1,0:T(8,128)(2,1)}), bf16[16,172,1024]{2,1,0:T(8,128)(2,1)}, u32[]{:S(2)}, u32[]{:S(2)}) async-start(bf16[16,172,1024]{2,1,0:T(8,128)(2,1)} %fusion.19), calls=%async_computation.1 | async-start | bytes 11534336 | tf_op jit(solution)/shard_map/all_to_all | solution.py:252
  381.8 92.8 %all-to-all-start.5 = ((bf16[16,172,1024]{2,1,0:T(8,128)(2,1)}), bf16[16,172,1024]{2,1,0:T(8,128)(2,1)}, u32[]{:S(2)}, u32[]{:S(2)}) async-start(bf16[16,172,1024]{2,1,0:T(8,128)(2,1)} %convolution_convert_fusion), calls=%async_computation.5 | async-start | bytes 11534336 | tf_op jit(solution)/shard_map/all_to_all | solution.py:260
  400.5 78.6 %copy-start.18 = (bf16[516,8]{0,1:T(8,128)(2,1)S(1)}, bf16[516,8]{0,1:T(8,128)(2,1)}, u32[]{:S(2)}) copy-start(bf16[516,8]{0,1:T(8,128)(2,1)} %param.29) | copy-start | bytes 24772
  400.5 78.6 %copy-start.16 = (s32[516,8]{0,1:T(8,128)S(1)}, s32[516,8]{0,1:T(8,128)}, u32[]{:S(2)}) copy-start(s32[516,8]{0,1:T(8,128)} %param.28) | copy-start | bytes 49540
  400.5 78.7 %copy-start.11 = (s32[32,516]{1,0:T(8,128)S(1)}, s32[32,516]{1,0:T(8,128)}, u32[]{:S(2)}) copy-start(s32[32,516]{1,0:T(8,128)} %copy-done.10) | copy-start | bytes 198148
  400.5 78.7 %copy-start.14 = (pred[516,32]{0,1:T(8,128)(4,1)S(1)}, pred[516,32]{0,1:T(8,128)(4,1)}, u32[]{:S(2)}) copy-start(pred[516,32]{0,1:T(8,128)(4,1)} %copy-done.13) | copy-start | bytes 49540
  474.6 92.7 %all-to-all-start.3 = ((bf16[16,172,1024]{2,1,0:T(8,128)(2,1)}), bf16[16,172,1024]{2,1,0:T(8,128)(2,1)}, u32[]{:S(2)}, u32[]{:S(2)}) async-start(bf16[16,172,1024]{2,1,0:T(8,128)(2,1)} %convolution_convert_fusion.1), calls=%async_computation.3 | async-start | bytes 11534336 | tf_op jit(solution)/shard_map/all_to_all | solution.py:260
  487.7 79.6 %copy-start.26 = (bf16[516,1024]{1,0:T(8,128)(2,1)S(1)}, bf16[516,1024]{1,0:T(8,128)(2,1)}, u32[]{:S(2)}) copy-start(bf16[516,1024]{1,0:T(8,128)(2,1)} %copy-done.24) | copy-start | bytes 3170308
  (13 other events, 54.0 us)
Sparse Core Ops, SparseCore 0:
  13.9 39.4 all-gather.4
  81.8 55.9 all-gather.6

commit v5 on v4

--- a/solution.py
+++ b/solution.py
@@ -149,42 +149,24 @@
     bundle = max(1, dec_rows // group_count)
     device = group_index * part_count + part_index
     position = jnp.arange(dec_rows, dtype=jnp.int32)
-    own_deal = lax.dynamic_slice_in_dim(deal_slots, device * dec_rows, dec_rows, 0)
-    target = own_deal // (part_count * dec_rows)
-    group_ids = jnp.arange(group_count, dtype=jnp.int32)
-    lane_ids = jnp.arange(bundle, dtype=jnp.int32)
-    send_table = (
-        (target[None, None, :] == group_ids[:, None, None])
-        & (position[None, None, :] % bundle == lane_ids[None, :, None])
-    ).astype(jnp.bfloat16)
-    outgoing = jnp.einsum(
-        "jbi,id->jbd", send_table, dec_tokens, preferred_element_type=jnp.float32
-    ).astype(jnp.bfloat16)
-    incoming = lax.all_to_all(outgoing, dp, split_axis=0, concat_axis=0, tiled=True)
     slot_ids = device * dec_rows + position
     request_ids = jnp.arange(deal_slots.shape[0], dtype=jnp.int32)
-    request = jnp.sum(
-        jnp.where(deal_slots[None, :] == slot_ids[:, None], request_ids[None, :], 0), axis=1
-    )
-    source = request // (part_count * dec_rows)
-    lane = request % dec_rows % bundle
-    take_table = (
-        (source[:, None, None] == group_ids[None, :, None])
-        & (lane[:, None, None] == lane_ids[None, None, :])
-    ).astype(jnp.bfloat16)
-    slot_rows = jnp.einsum(
-        "ijb,jbd->id", take_table, incoming, preferred_element_type=jnp.float32
+    take_table = (deal_slots[None, :] == slot_ids[:, None]).astype(jnp.bfloat16)
+    local_width = qkv_weight.shape[1]
+    qkv_pair = across_halves(qkv_weight)
+    out_pair = jnp.moveaxis(across_halves(out_weight), 0, 1)
+    qkv_full = lax.all_gather(qkv_pair, "dl", axis=0, tiled=False)
+    qkv_full = jnp.swapaxes(qkv_full, 0, 1).reshape(-1, local_width)
+    qkv_full, dec_tokens = lax.optimization_barrier((qkv_full, dec_tokens))
+    every_request = lax.all_gather(dec_tokens, (*dp, "mp"), axis=0, tiled=True)
+    every_request, out_pair = lax.optimization_barrier((every_request, out_pair))
+    slot_rows = jnp.dot(
+        take_table, every_request, preferred_element_type=jnp.float32
     ).astype(jnp.bfloat16)
     layer_input = jnp.concatenate([pre_tokens, slot_rows], axis=0)
     rows_dev = layer_input.shape[0]
     normed = root_norm(layer_input.astype(jnp.float32), attn_gain).astype(jnp.bfloat16)
     group_rows = lax.all_gather(normed, "mp", axis=0, tiled=True)
-    local_width = qkv_weight.shape[1]
-    qkv_pair = across_halves(qkv_weight)
-    out_pair = jnp.moveaxis(across_halves(out_weight), 0, 1)
-    qkv_full = lax.all_gather(qkv_pair, "dl", axis=0, tiled=False)
-    qkv_full = jnp.swapaxes(qkv_full, 0, 1).reshape(-1, local_width)
-    qkv_full, out_pair = lax.optimization_barrier((qkv_full, out_pair))
     projected = jnp.dot(group_rows, qkv_full, preferred_element_type=jnp.float32)
     local_groups = dec_cache.shape[0]
     projected = projected.reshape(part_count, rows_dev, local_groups, local_width // local_groups)

time: 593 us -> 673 us (1.13)
  blocking collectives: 0 us -> 90.3 us
    all_gather x0 -> x1, blocking collectives: none -> 90.3 us  [local(): every_request = lax.all_gather(dec_tokens, (*dp, 'mp'), axis=0, tiled=True)]
    all_gather x1, waiting for transfers between devices: 0.02 us -> 47.2 us  [local(): qkv_full = lax.all_gather(qkv_pair, 'dl', axis=0, tiled=False)]
    all_to_all x1, waiting for transfers between devices: 44 us -> 0.01 us  [local(): lax.all_to_all(jnp.concatenate([owner_major(gate_up), owner_major(down_we...]
    all_to_all x1 -> x0, starting transfers between devices: 9.71 us -> none  [local(): lax.all_to_all(outgoing, dp, split_axis=0, concat_axis=0, tiled=True)]
    all_gather x1, waiting for transfers between devices: 7.92 us -> 0.01 us  [local(): out_full = lax.all_gather(out_pair, 'dl', axis=1, tiled=False)]
    unnamed x59 -> x61, local copies, waits for them, and re-layouts: 15.9 us -> 14.1 us
  transfers between devices with their start and end apart: 10 -> 9, of which waited for: 7 -> 6; matrix products, arithmetic and copies ran while one was open for 28% -> 25% of each run, Pallas kernels for 0% -> 0%
where the time goes in v5:
time: 673 us; the launch traced here: 666 us
  waiting for transfers between devices  347 us (52%)
  matrix products  111 us (16%)
  blocking collectives  90.3 us (13%)
  local copies, waits for them, and re-layouts  43.5 us (6%)
  starting transfers between devices  33.9 us (5%)
  other arithmetic  24.9 us (4%)
  between operations  14.8 us (2%)
    all_to_all x2, waiting for transfers between devices, local(): lax.all_to_all(outbound, 'dl', split_axis=0, concat_axis=0, tiled=True)  148 us
    all_to_all x2, waiting for transfers between devices, local(): lax.all_to_all(expert_out, 'dl', split_axis=0, concat_axis=0, tiled=True)  146 us
    all_gather x1, blocking collectives, local(): every_request = lax.all_gather(dec_tokens, (*dp, 'mp'), axis=0, tiled=True)  90.3 us
    all_gather x1, waiting for transfers between devices, local(): qkv_full = lax.all_gather(qkv_pair, 'dl', axis=0, tiled=False)  47.2 us
    sub x1, matrix products, prefill_attention(): expo = jnp.exp(scores - highest)  24.1 us
    dot_general x1, matrix products, prefill_attention(): jnp.einsum('gpck,gkh->cgph', weights, all_values, preferred_element_type=...  18.2 us
    dot_general x2, matrix products, local(): jnp.einsum('snd,df->snf', arrived, full_gu[l], preferred_element_type=jnp...  17.2 us
    dot_general x2, matrix products, local(): jnp.einsum('ecr,ecd->rd', combine_table[picked], returned, preferred_elem...  16 us
  transfers between devices with their start and end apart: 9, of which 6 were waited for; matrix products, arithmetic and copies ran while one was open for 25% of the time, Pallas kernels for 0%

profile of v5, /device:TPU:23, one launch (start us, length us, event | category | flops | bytes accessed | tf_op | source)
XLA Modules:
  0.0 665.7 jit_solution(2251703073201833569)
XLA Ops:
  6.6 5.4 collective-permute-done
  22.5 7.4 %all-to-all-start.1 = ((bf16[32,2,48,1024]{3,2,1,0:T(8,128)(2,1)}), bf16[32,2,48,1024]{3,2,1,0:T(8,128)(2,1)}, u32[]{:S(2)}, u32[]{:S(2)}) async-start(bf16[32,2,48,1024]{3,2,1,0:T(8,128)(2,1)} %pad_maximum_fusion), calls=%async_computation.1 | async-start | bytes 12582912 | tf_op jit(solution)/shard_map/all_to_all | solution.py:196
  44.2 4.8 fusion.6
  49.7 47.2 %all-gather.6.cloned.1.call-done = bf16[32,32,2048]{2,1,0:T(8,128)(2,1)} async-done(((bf16[2,32,2048]{2,1,0:T(8,128)(2,1)}), bf16[32,32,2048]{2,1,0:T(8,128)(2,1)}) %all-gather.6.cloned.1.call-update) | async-done | bytes 4194320 | tf_op jit(solution)/shard_map/all_gather | solution.py:158
  96.9 4.9 copy.66
  101.8 90.3 %all-gather.2 = bf16[32,4,1024]{2,1,0:T(4,128)(2,1)S(1)} all-gather(bf16[1,4,1024]{2,1,0:T(4,128)(2,1)S(1)} %bitcast.174), channel_id=1, replica_groups=mesh['zh'=2,'dl'=16,'mp'=1] {'zh','dl','mp'}, dimensions={0}, use_global_device_ids=true | all-gather | bytes 270336 | tf_op jit(solution)/shard_map/all_gather | solution.py:161
  192.7 4.7 fusion.59
  202.0 5.5 copy.84
  219.2 24.1 %fusion.93 = (f32[8,2,512]{2,1,0:T(2,128)S(1)}, f32[8,2,512,1536]{2,3,1,0:T(8,128)}) fusion(pred[512,1536]{0,1:T(8,128)(4,1)} %fusion.25, bf16[8,512,64]{1,2,0:T(8,128)(2,1)} %maximum_bitcast_fusion.13, bf16[8,1024,64]{1,2,0:T(8,128)(2,1)} %get-tuple-element.18, bf16[512,8,2,32]{0,3,2,1:T(8,128)(2,1)} %get-tuple-element.16, ...), kind=kOutput, calls=%fused_computation.148 | convolution fusion | flops 1666188800 | bytes 53772288 | tf_op jit(solution)/shard_map/sub | solution.py:60
  243.3 18.2 %fusion.43 = bf16[8,64,2,512]{3,1,2,0:T(8,128)(2,1)} fusion(f32[8,2,512,1536]{2,3,1,0:T(8,128)} %get-tuple-element.38, f32[8,2,512]{2,1,0:T(2,128)S(1)} %get-tuple-element.37, bf16[8,512,64]{1,2,0:T(8,128)(2,1)S(1)} %copy-done.11, bf16[8,1024,64]{1,2,0:T(8,128)(2,1)S(1)} %copy-done.8), kind=kOutput, calls=%fused_computation.59 | convolution fusion | flops 1639448576 | bytes 52985856 | tf_op jit(solution)/shard_map/gpck,gkh->cgph/dot_general | solution.py:62
  266.1 7.3 %fusion.22 = bf16[16,172,1024]{2,1,0:T(8,128)(2,1)} fusion(pred[32,172,516]{2,1,0:T(8,128)(4,1)S(1)} %copy-done.3, bf16[516,1024]{1,0:T(8,128)(2,1)S(1)} %get-tuple-element.40, f32[1024]{0:T(1024)S(1)} %copy-done.22, f32[516]{0:T(1024)S(1)} %add_rsqrt_fusion, bf16[4,1024]{1,0:T(4,128)(2,1)S(1)} %copy-done.19, bf16[512,1024]{1,0:T(8,128)(2,1)S(1)} %copy-done.7), kind=kOutput, calls=%fused_computation.29 | convolution fusion | flops 2915799040 | bytes 9568256 | tf_op jit(solution)/shard_map/ecr,rd->ecd/dot_general | solution.py:230
  273.4 9.7 %all-to-all-start.3 = ((bf16[16,172,1024]{2,1,0:T(8,128)(2,1)}), bf16[16,172,1024]{2,1,0:T(8,128)(2,1)}, u32[]{:S(2)}, u32[]{:S(2)}) async-start(bf16[16,172,1024]{2,1,0:T(8,128)(2,1)} %fusion.22), calls=%async_computation.3 | async-start | bytes 11534336 | tf_op jit(solution)/shard_map/all_to_all | solution.py:234
  283.1 8.2 %fusion.19 = bf16[16,172,1024]{2,1,0:T(8,128)(2,1)} fusion(pred[32,172,516]{2,1,0:T(8,128)(4,1)} %fusion.6, bf16[516,1024]{1,0:T(8,128)(2,1)S(1)} %copy-done.27, f32[1024]{0:T(1024)S(1)} %copy-done.22, f32[516]{0:T(1024)S(1)} %add_rsqrt_fusion, bf16[4,1024]{1,0:T(4,128)(2,1)S(1)} %copy-done.19, bf16[512,1024]{1,0:T(8,128)(2,1)S(1)} %copy-done.7), kind=kOutput, calls=%fused_computation.28 | convolution fusion | flops 2915799040 | bytes 9558032 | tf_op jit(solution)/shard_map/ecr,rd->ecd/dot_general | solution.py:230
  291.3 80.5 %all-to-all-done.3 = bf16[16,172,1024]{2,1,0:T(8,128)(2,1)} async-done(((bf16[16,172,1024]{2,1,0:T(8,128)(2,1)}), bf16[16,172,1024]{2,1,0:T(8,128)(2,1)}, u32[]{:S(2)}, u32[]{:S(2)}) %all-to-all-start.3) | async-done | bytes 5636128 | tf_op jit(solution)/shard_map/all_to_all | solution.py:234
  383.3 8.3 %fusion.33 = f32[16,172,1024]{2,1,0:T(8,128)S(1)} fusion(bf16[16,172,1024]{2,1,0:T(8,128)(2,1)} %all-to-all-done.3, bf16[1,2,1024,1024]{3,2,1,0:T(8,128)(2,1)S(1)} %bitcast.157), kind=kOutput, calls=%fused_computation.46 | convolution fusion | flops 5771362304 | bytes 19005440 | tf_op jit(solution)/shard_map/snd,df->snf/dot_general | solution.py:235
  391.6 5.1 convolution_convert_fusion
  396.7 67.7 %all-to-all-done = bf16[16,172,1024]{2,1,0:T(8,128)(2,1)} async-done(((bf16[16,172,1024]{2,1,0:T(8,128)(2,1)}), bf16[16,172,1024]{2,1,0:T(8,128)(2,1)}, u32[]{:S(2)}, u32[]{:S(2)}) %all-to-all-start) | async-done | bytes 5636128 | tf_op jit(solution)/shard_map/all_to_all | solution.py:234
  469.2 8.9 %fusion.34 = f32[16,172,1024]{2,1,0:T(8,128)S(1)} fusion(bf16[16,172,1024]{2,1,0:T(8,128)(2,1)} %all-to-all-done, bf16[1,2,1024,1024]{3,2,1,0:T(8,128)(2,1)} %bitcast.158), kind=kOutput, calls=%fused_computation.49 | convolution fusion | flops 5771362304 | bytes 19136512 | tf_op jit(solution)/shard_map/snd,df->snf/dot_general | solution.py:235
  478.1 5.2 convolution_convert_fusion.1
  483.2 74.1 %all-to-all-done.4 = bf16[16,172,1024]{2,1,0:T(8,128)(2,1)} async-done(((bf16[16,172,1024]{2,1,0:T(8,128)(2,1)}), bf16[16,172,1024]{2,1,0:T(8,128)(2,1)}, u32[]{:S(2)}, u32[]{:S(2)}) %all-to-all-start.4) | async-done | bytes 5636128 | tf_op jit(solution)/shard_map/all_to_all | solution.py:242
  561.9 5.5 select_convert_fusion
  570.4 7.4 %fusion.15 = f32[516,1024,1]{1,0,2:T(8,128)} fusion(bf16[16,172,1024]{2,1,0:T(8,128)(2,1)} %all-to-all-done.4, bf16[32,172,516]{2,1,0:T(8,128)(2,1)S(1)} %select_convert_fusion), kind=kOutput, calls=%fused_computation.24 | convolution fusion | flops 2908225536 | bytes 11354112 | tf_op jit(solution)/shard_map/ecr,ecd->rd/dot_general | solution.py:244
  577.7 72.2 %all-to-all-done.2 = bf16[16,172,1024]{2,1,0:T(8,128)(2,1)} async-done(((bf16[16,172,1024]{2,1,0:T(8,128)(2,1)}), bf16[16,172,1024]{2,1,0:T(8,128)(2,1)}, u32[]{:S(2)}, u32[]{:S(2)}) %all-to-all-start.2) | async-done | bytes 5636128 | tf_op jit(solution)/shard_map/all_to_all | solution.py:242
  650.0 8.7 %fusion.32 = bf16[516,1024]{1,0:T(8,128)(2,1)} fusion(f32[516,1024,1]{1,0,2:T(8,128)} %fusion.15, bf16[516,1024]{1,0:T(8,128)(2,1)S(1)} %copy-done.28, bf16[16,172,1024]{2,1,0:T(8,128)(2,1)} %all-to-all-done.2, bf16[32,172,516]{2,1,0:T(8,128)(2,1)} %copy-done.1, bf16[4,1024]{1,0:T(4,128)(2,1)S(1)} %copy-done.19, bf16[512,1024]{1,0:T(8,128)(2,1)S(1)} %copy-done.7), kind=kOutput, calls=%fused_computation.42 | convolution fusion | flops 2912980992 | bytes 14671872 | tf_op jit(solution)/shard_map/ecr,ecd->rd/dot_general | solution.py:244
  (132 shorter events, 69.6 us)
Async XLA Ops:
  6.5 90.3 %all-gather.6.cloned.1.call-start = ((), (), s32[]{:S(2)}) async-start(), calls=%async_computation.5 | async-start | bytes 4456448 | tf_op jit(solution)/shard_map/all_gather | solution.py:158
  6.5 5.5 collective-permute-start
  13.7 35.3 %collective-permute-start.1 = (bf16[1024,32]{0,1:T(8,128)(2,1)}, bf16[1024,32]{0,1:T(8,128)(2,1)S(1)}, u32[]{:S(2)}, u32[]{:S(2)}) collective-permute-start(bf16[1024,32]{0,1:T(8,128)(2,1)} %param.25), channel_id=1, source_target_pairs={{0,16},{16,0},{1,17},{17,1},{2,18},{18,2},{3,19},{19,3},{4,20},{20... | collective-permute-start | bytes 196616 | tf_op jit(solution)/shard_map/ppermute | solution.py:116
  22.5 8.2 %copy-start.4 = (bf16[8,1,1024,128]{3,2,1,0:T(8,128)(2,1)S(1)}, bf16[8,1,1024,128]{3,2,1,0:T(8,128)(2,1)}, u32[]{:S(2)}) copy-start(bf16[8,1,1024,128]{3,2,1,0:T(8,128)(2,1)} %param.21) | copy-start | bytes 6291460
  22.5 250.9 %all-to-all-start.1 = ((bf16[32,2,48,1024]{3,2,1,0:T(8,128)(2,1)}), bf16[32,2,48,1024]{3,2,1,0:T(8,128)(2,1)}, u32[]{:S(2)}, u32[]{:S(2)}) async-start(bf16[32,2,48,1024]{3,2,1,0:T(8,128)(2,1)} %pad_maximum_fusion), calls=%async_computation.1 | async-start | bytes 12582912 | tf_op jit(solution)/shard_map/all_to_all | solution.py:196
  30.0 231.4 %all-gather.8.cloned.1.call-start = ((), (), s32[]{:S(2)}) async-start(), calls=%async_computation.6 | async-start | bytes 2228224 | tf_op jit(solution)/shard_map/all_gather | solution.py:176
  33.4 10.8 %copy-start.12 = (pred[516,32]{0,1:T(8,128)(4,1)}, pred[516,32]{0,1:T(8,128)(4,1)S(1)}, u32[]{:S(2)}) copy-start(pred[516,32]{0,1:T(8,128)(4,1)S(1)} %fusion.64) | copy-start | bytes 49540
  35.8 8.4 %copy-start.9 = (s32[32,516]{1,0:T(8,128)}, s32[32,516]{1,0:T(8,128)S(1)}, u32[]{:S(2)}) copy-start(s32[32,516]{1,0:T(8,128)S(1)} %fusion.66) | copy-start | bytes 198148
  41.9 7.1 %copy-start.16 = (bf16[1024,32]{0,1:T(8,128)(2,1)S(1)}, bf16[1024,32]{0,1:T(8,128)(2,1)}, u32[]{:S(2)}) copy-start(bf16[1024,32]{0,1:T(8,128)(2,1)} %param.25) | copy-start | bytes 196612
  96.9 95.3 %copy-start.24 = (s32[128]{0:T(128)S(1)}, s32[128]{0:T(128)}, u32[]{:S(2)}) copy-start(s32[128]{0:T(128)} %param.17) | copy-start | bytes 1540
  96.9 95.5 %copy-start.7 = (bf16[512,1024]{1,0:T(8,128)(2,1)S(1)}, bf16[512,1024]{1,0:T(8,128)(2,1)}, u32[]{:S(2)}) copy-start(bf16[512,1024]{1,0:T(8,128)(2,1)} %param.15) | copy-start | bytes 3145732
  96.9 95.8 %copy-start.21 = (f32[1024]{0:T(1024)S(1)}, f32[1024]{0:T(1024)}, u32[]{:S(2)}) copy-start(f32[1024]{0:T(1024)} %param.22) | copy-start | bytes 12292
  219.2 24.1 %copy-start.8 = (bf16[8,1024,64]{1,2,0:T(8,128)(2,1)S(1)}, bf16[8,1024,64]{1,2,0:T(8,128)(2,1)}, u32[]{:S(2)}) copy-start(bf16[8,1024,64]{1,2,0:T(8,128)(2,1)} %get-tuple-element.17) | copy-start | bytes 3145732
  219.2 24.1 %copy-start.11 = (bf16[8,512,64]{1,2,0:T(8,128)(2,1)S(1)}, bf16[8,512,64]{1,2,0:T(8,128)(2,1)}, u32[]{:S(2)}) copy-start(bf16[8,512,64]{1,2,0:T(8,128)(2,1)} %fusion.65) | copy-start | bytes 1572868
  273.4 9.7 %copy-start.27 = (bf16[516,1024]{1,0:T(8,128)(2,1)S(1)}, bf16[516,1024]{1,0:T(8,128)(2,1)}, u32[]{:S(2)}) copy-start(bf16[516,1024]{1,0:T(8,128)(2,1)} %copy-done.26) | copy-start | bytes 3170308
  273.4 98.4 %all-to-all-start.3 = ((bf16[16,172,1024]{2,1,0:T(8,128)(2,1)}), bf16[16,172,1024]{2,1,0:T(8,128)(2,1)}, u32[]{:S(2)}, u32[]{:S(2)}) async-start(bf16[16,172,1024]{2,1,0:T(8,128)(2,1)} %fusion.22), calls=%async_computation.3 | async-start | bytes 11534336 | tf_op jit(solution)/shard_map/all_to_all | solution.py:234
  371.9 92.6 %all-to-all-start = ((bf16[16,172,1024]{2,1,0:T(8,128)(2,1)}), bf16[16,172,1024]{2,1,0:T(8,128)(2,1)}, u32[]{:S(2)}, u32[]{:S(2)}) async-start(bf16[16,172,1024]{2,1,0:T(8,128)(2,1)} %fusion.19), calls=%async_computation | async-start | bytes 11534336 | tf_op jit(solution)/shard_map/all_to_all | solution.py:234
  464.5 92.8 %all-to-all-start.4 = ((bf16[16,172,1024]{2,1,0:T(8,128)(2,1)}), bf16[16,172,1024]{2,1,0:T(8,128)(2,1)}, u32[]{:S(2)}, u32[]{:S(2)}) async-start(bf16[16,172,1024]{2,1,0:T(8,128)(2,1)} %convolution_convert_fusion), calls=%async_computation.4 | async-start | bytes 11534336 | tf_op jit(solution)/shard_map/all_to_all | solution.py:242
  483.2 78.6 %copy-start.17 = (bf16[516,8]{0,1:T(8,128)(2,1)S(1)}, bf16[516,8]{0,1:T(8,128)(2,1)}, u32[]{:S(2)}) copy-start(bf16[516,8]{0,1:T(8,128)(2,1)} %param.29) | copy-start | bytes 24772
  483.2 78.6 %copy-start.15 = (s32[516,8]{0,1:T(8,128)S(1)}, s32[516,8]{0,1:T(8,128)}, u32[]{:S(2)}) copy-start(s32[516,8]{0,1:T(8,128)} %param.28) | copy-start | bytes 49540
  483.2 78.7 %copy-start.10 = (s32[32,516]{1,0:T(8,128)S(1)}, s32[32,516]{1,0:T(8,128)}, u32[]{:S(2)}) copy-start(s32[32,516]{1,0:T(8,128)} %copy-done.9) | copy-start | bytes 198148
  483.2 78.7 %copy-start.13 = (pred[516,32]{0,1:T(8,128)(4,1)S(1)}, pred[516,32]{0,1:T(8,128)(4,1)}, u32[]{:S(2)}) copy-start(pred[516,32]{0,1:T(8,128)(4,1)} %copy-done.12) | copy-start | bytes 49540
  557.3 92.7 %all-to-all-start.2 = ((bf16[16,172,1024]{2,1,0:T(8,128)(2,1)}), bf16[16,172,1024]{2,1,0:T(8,128)(2,1)}, u32[]{:S(2)}, u32[]{:S(2)}) async-start(bf16[16,172,1024]{2,1,0:T(8,128)(2,1)} %convolution_convert_fusion.1), calls=%async_computation.2 | async-start | bytes 11534336 | tf_op jit(solution)/shard_map/all_to_all | solution.py:242
  570.4 79.6 %copy-start.28 = (bf16[516,1024]{1,0:T(8,128)(2,1)S(1)}, bf16[516,1024]{1,0:T(8,128)(2,1)}, u32[]{:S(2)}) copy-start(bf16[516,1024]{1,0:T(8,128)(2,1)} %copy-done.26) | copy-start | bytes 3170308
  (14 other events, 44.5 us)
Sparse Core Ops, SparseCore 0:
  13.8 82.9 all-gather.5
  213.7 33.1 all-gather.7

commit v6 on v5

--- a/solution.py
+++ b/solution.py
@@ -153,13 +153,16 @@
     request_ids = jnp.arange(deal_slots.shape[0], dtype=jnp.int32)
     take_table = (deal_slots[None, :] == slot_ids[:, None]).astype(jnp.bfloat16)
     local_width = qkv_weight.shape[1]
-    qkv_pair = across_halves(qkv_weight)
+    weight_rows = qkv_weight.shape[0]
+    riders = jnp.concatenate([qkv_weight, dec_tokens.reshape(-1, local_width)], axis=0)
+    qkv_pair = across_halves(riders)
     out_pair = jnp.moveaxis(across_halves(out_weight), 0, 1)
-    qkv_full = lax.all_gather(qkv_pair, "dl", axis=0, tiled=False)
-    qkv_full = jnp.swapaxes(qkv_full, 0, 1).reshape(-1, local_width)
-    qkv_full, dec_tokens = lax.optimization_barrier((qkv_full, dec_tokens))
-    every_request = lax.all_gather(dec_tokens, (*dp, "mp"), axis=0, tiled=True)
-    every_request, out_pair = lax.optimization_barrier((every_request, out_pair))
+    gathered = jnp.swapaxes(lax.all_gather(qkv_pair, "dl", axis=0, tiled=False), 0, 1)
+    qkv_full = gathered[:, :, :weight_rows].reshape(-1, local_width)
+    every_request = gathered[:, :, weight_rows:].reshape(group_count, dec_rows, width)
+    every_request = lax.all_gather(every_request, "mp", axis=1, tiled=False)
+    every_request = every_request.reshape(-1, width)
+    qkv_full, out_pair = lax.optimization_barrier((qkv_full, out_pair))
     slot_rows = jnp.dot(
         take_table, every_request, preferred_element_type=jnp.float32
     ).astype(jnp.bfloat16)

time: 673 us -> 619 us (0.920)
  blocking collectives: 90.3 us -> 0 us
  local copies, waits for them, and re-layouts: 43.5 us -> 60.6 us
  starting transfers between devices: 33.9 us -> 47.1 us
  waiting for transfers between devices: 347 us -> 357 us
    all_gather x1 -> x0, blocking collectives: 90.3 us -> none  [local(): every_request = lax.all_gather(dec_tokens, (*dp, 'mp'), axis=0, tiled=True)]
    all_to_all x2, starting transfers between devices: 14.2 us -> 27.1 us  [local(): lax.all_to_all(outbound, 'dl', split_axis=0, concat_axis=0, tiled=True)]
    slice x1 -> x5, local copies, waits for them, and re-layouts: 0.26 us -> 11.7 us  [the longest x2 10 us: local(): qkv_full = gathered[:, :, :weight_rows].reshape(-1, local_width)]
    all_gather x0 -> x1, local copies, waits for them, and re-layouts: none -> 9.16 us  [local(): lax.all_gather(qkv_pair, 'dl', axis=0, tiled=False)]
    unnamed x61 -> x60, local copies, waits for them, and re-layouts: 14.1 us -> 14.8 us
  transfers between devices with their start and end apart: 9 -> 9, of which waited for: 6 -> 7; matrix products, arithmetic and copies ran while one was open for 25% -> 29% of each run, Pallas kernels for 0% -> 0%
where the time goes in v6:
time: 619 us; the launch traced here: 615 us
  waiting for transfers between devices  357 us (58%)
  matrix products  111 us (18%)
  local copies, waits for them, and re-layouts  60.6 us (10%)
  starting transfers between devices  47.1 us (8%)
  other arithmetic  24.2 us (4%)
  between operations  14.9 us (2%)
    all_to_all x2, waiting for transfers between devices, local(): lax.all_to_all(outbound, 'dl', split_axis=0, concat_axis=0, tiled=True)  148 us
    all_to_all x2, waiting for transfers between devices, local(): lax.all_to_all(expert_out, 'dl', split_axis=0, concat_axis=0, tiled=True)  146 us
    all_gather x1, waiting for transfers between devices, local(): lax.all_gather(qkv_pair, 'dl', axis=0, tiled=False)  53.4 us
    all_to_all x2, starting transfers between devices, local(): lax.all_to_all(outbound, 'dl', split_axis=0, concat_axis=0, tiled=True)  27.1 us
    sub x1, matrix products, prefill_attention(): expo = jnp.exp(scores - highest)  24.4 us
    dot_general x1, matrix products, prefill_attention(): jnp.einsum('gpck,gkh->cgph', weights, all_values, preferred_element_type=...  18.7 us
    dot_general x2, matrix products, local(): jnp.einsum('snd,df->snf', arrived, full_gu[l], preferred_element_type=jnp...  17.2 us
    dot_general x2, matrix products, local(): jnp.einsum('ecr,ecd->rd', combine_table[picked], returned, preferred_elem...  16 us
  transfers between devices with their start and end apart: 9, of which 7 were waited for; matrix products, arithmetic and copies ran while one was open for 29% of the time, Pallas kernels for 0%

profile of v6, /device:TPU:23, one launch (start us, length us, event | category | flops | bytes accessed | tf_op | source)
XLA Modules:
  0.0 614.6 jit_solution(4387722068715014828)
XLA Ops:
  8.3 6.4 %collective-permute-done = bf16[34,2048]{1,0:T(8,128)(2,1)S(1)} collective-permute-done((bf16[34,2048]{1,0:T(8,128)(2,1)S(1)}, bf16[34,2048]{1,0:T(8,128)(2,1)S(1)}, u32[]{:S(2)}, u32[]{:S(2)}) %collective-permute-start) | collective-permute-done | bytes 139296 | tf_op jit(solution)/shard_map/ppermute | solution.py:116
  24.6 7.4 %all-to-all-start.1 = ((bf16[32,2,48,1024]{3,2,1,0:T(8,128)(2,1)}), bf16[32,2,48,1024]{3,2,1,0:T(8,128)(2,1)}, u32[]{:S(2)}, u32[]{:S(2)}) async-start(bf16[32,2,48,1024]{3,2,1,0:T(8,128)(2,1)} %pad_maximum_fusion), calls=%async_computation.1 | async-start | bytes 12582912 | tf_op jit(solution)/shard_map/all_to_all | solution.py:199
  46.4 4.8 fusion.6
  51.9 53.4 %all-gather.5.cloned.1.call-done = bf16[32,34,2048]{2,1,0:T(8,128)(2,1)} async-done(((bf16[2,34,2048]{2,1,0:T(8,128)(2,1)}), bf16[32,34,2048]{2,1,0:T(8,128)(2,1)}) %all-gather.5.cloned.1.call-update) | async-done | bytes 4456464 | tf_op jit(solution)/shard_map/all_gather | solution.py:160
  105.3 9.2 %copy.116 = bf16[16,2,34,2048]{3,1,0,2:T(2,128)(2,1)} copy(bf16[16,2,34,2048]{3,2,1,0:T(8,128)(2,1)} %bitcast.157) | data formatting | bytes 8912896 | tf_op jit(solution)/shard_map/all_gather | solution.py:160
  114.5 5.6 slice.162
  135.9 5.3 copy.91
  152.9 24.4 %fusion.93 = (f32[8,2,512]{2,1,0:T(2,128)S(1)}, f32[8,2,512,1536]{2,3,1,0:T(8,128)}) fusion(pred[512,1536]{0,1:T(8,128)(4,1)} %fusion.25, bf16[8,512,64]{1,2,0:T(8,128)(2,1)} %maximum_bitcast_fusion.13, bf16[8,1024,64]{1,2,0:T(8,128)(2,1)} %get-tuple-element.14, bf16[512,8,2,32]{0,3,2,1:T(8,128)(2,1)} %get-tuple-element.12, ...), kind=kOutput, calls=%fused_computation.151 | convolution fusion | flops 1666188800 | bytes 53772288 | tf_op jit(solution)/shard_map/sub | solution.py:60
  177.3 18.7 %fusion.43 = bf16[8,64,2,512]{3,1,2,0:T(8,128)(2,1)} fusion(f32[8,2,512,1536]{2,3,1,0:T(8,128)} %get-tuple-element.34, f32[8,2,512]{2,1,0:T(2,128)S(1)} %get-tuple-element.33, bf16[8,512,64]{1,2,0:T(8,128)(2,1)S(1)} %copy-done.11, bf16[8,1024,64]{1,2,0:T(8,128)(2,1)S(1)} %copy-done.8), kind=kOutput, calls=%fused_computation.60 | convolution fusion | flops 1639448576 | bytes 52985856 | tf_op jit(solution)/shard_map/gpck,gkh->cgph/dot_general | solution.py:62
  202.9 6.8 %fusion.22 = bf16[16,172,1024]{2,1,0:T(8,128)(2,1)} fusion(pred[32,172,516]{2,1,0:T(8,128)(4,1)S(1)} %copy-done.3, bf16[516,1024]{1,0:T(8,128)(2,1)S(1)} %get-tuple-element.36, f32[1024]{0:T(1024)S(1)} %copy-done.21, f32[516]{0:T(1024)S(1)} %add_rsqrt_fusion, bf16[4,1024]{1,0:T(4,128)(2,1)S(1)} %copy-done.19, bf16[512,1024]{1,0:T(8,128)(2,1)S(1)} %copy-done.7), kind=kOutput, calls=%fused_computation.30 | convolution fusion | flops 2915799040 | bytes 9568256 | tf_op jit(solution)/shard_map/ecr,rd->ecd/dot_general | solution.py:233
  209.7 22.5 %all-to-all-start.3 = ((bf16[16,172,1024]{2,1,0:T(8,128)(2,1)}), bf16[16,172,1024]{2,1,0:T(8,128)(2,1)}, u32[]{:S(2)}, u32[]{:S(2)}) async-start(bf16[16,172,1024]{2,1,0:T(8,128)(2,1)} %fusion.22), calls=%async_computation.3 | async-start | bytes 11534336 | tf_op jit(solution)/shard_map/all_to_all | solution.py:237
  232.3 8.2 %fusion.19 = bf16[16,172,1024]{2,1,0:T(8,128)(2,1)} fusion(pred[32,172,516]{2,1,0:T(8,128)(4,1)} %fusion.6, bf16[516,1024]{1,0:T(8,128)(2,1)S(1)} %copy-done.26, f32[1024]{0:T(1024)S(1)} %copy-done.21, f32[516]{0:T(1024)S(1)} %add_rsqrt_fusion, bf16[4,1024]{1,0:T(4,128)(2,1)S(1)} %copy-done.19, bf16[512,1024]{1,0:T(8,128)(2,1)S(1)} %copy-done.7), kind=kOutput, calls=%fused_computation.29 | convolution fusion | flops 2915799040 | bytes 9558032 | tf_op jit(solution)/shard_map/ecr,rd->ecd/dot_general | solution.py:233
  240.5 80.3 %all-to-all-done.3 = bf16[16,172,1024]{2,1,0:T(8,128)(2,1)} async-done(((bf16[16,172,1024]{2,1,0:T(8,128)(2,1)}), bf16[16,172,1024]{2,1,0:T(8,128)(2,1)}, u32[]{:S(2)}, u32[]{:S(2)}) %all-to-all-start.3) | async-done | bytes 5636128 | tf_op jit(solution)/shard_map/all_to_all | solution.py:237
  332.2 8.3 %fusion.33 = f32[16,172,1024]{2,1,0:T(8,128)S(1)} fusion(bf16[16,172,1024]{2,1,0:T(8,128)(2,1)} %all-to-all-done.3, bf16[1,2,1024,1024]{3,2,1,0:T(8,128)(2,1)S(1)} %bitcast.159), kind=kOutput, calls=%fused_computation.47 | convolution fusion | flops 5771362304 | bytes 19005440 | tf_op jit(solution)/shard_map/snd,df->snf/dot_general | solution.py:238
  340.5 5.1 convolution_convert_fusion
  345.6 67.8 %all-to-all-done = bf16[16,172,1024]{2,1,0:T(8,128)(2,1)} async-done(((bf16[16,172,1024]{2,1,0:T(8,128)(2,1)}), bf16[16,172,1024]{2,1,0:T(8,128)(2,1)}, u32[]{:S(2)}, u32[]{:S(2)}) %all-to-all-start) | async-done | bytes 5636128 | tf_op jit(solution)/shard_map/all_to_all | solution.py:237
  417.9 8.9 %fusion.34 = f32[16,172,1024]{2,1,0:T(8,128)S(1)} fusion(bf16[16,172,1024]{2,1,0:T(8,128)(2,1)} %all-to-all-done, bf16[1,2,1024,1024]{3,2,1,0:T(8,128)(2,1)} %bitcast.160), kind=kOutput, calls=%fused_computation.50 | convolution fusion | flops 5771362304 | bytes 19136512 | tf_op jit(solution)/shard_map/snd,df->snf/dot_general | solution.py:238
  426.8 5.2 convolution_convert_fusion.1
  432.0 74.1 %all-to-all-done.4 = bf16[16,172,1024]{2,1,0:T(8,128)(2,1)} async-done(((bf16[16,172,1024]{2,1,0:T(8,128)(2,1)}), bf16[16,172,1024]{2,1,0:T(8,128)(2,1)}, u32[]{:S(2)}, u32[]{:S(2)}) %all-to-all-start.4) | async-done | bytes 5636128 | tf_op jit(solution)/shard_map/all_to_all | solution.py:245
  506.1 4.7 all-to-all-start.2
  511.0 5.5 select_convert_fusion
  519.4 7.4 %fusion.15 = f32[516,1024,1]{1,0,2:T(8,128)} fusion(bf16[16,172,1024]{2,1,0:T(8,128)(2,1)} %all-to-all-done.4, bf16[32,172,516]{2,1,0:T(8,128)(2,1)S(1)} %select_convert_fusion), kind=kOutput, calls=%fused_computation.25 | convolution fusion | flops 2908225536 | bytes 11354112 | tf_op jit(solution)/shard_map/ecr,ecd->rd/dot_general | solution.py:247
  526.8 72.2 %all-to-all-done.2 = bf16[16,172,1024]{2,1,0:T(8,128)(2,1)} async-done(((bf16[16,172,1024]{2,1,0:T(8,128)(2,1)}), bf16[16,172,1024]{2,1,0:T(8,128)(2,1)}, u32[]{:S(2)}, u32[]{:S(2)}) %all-to-all-start.2) | async-done | bytes 5636128 | tf_op jit(solution)/shard_map/all_to_all | solution.py:245
  598.9 8.6 %fusion.32 = bf16[516,1024]{1,0:T(8,128)(2,1)} fusion(f32[516,1024,1]{1,0,2:T(8,128)} %fusion.15, bf16[516,1024]{1,0:T(8,128)(2,1)S(1)} %copy-done.27, bf16[16,172,1024]{2,1,0:T(8,128)(2,1)} %all-to-all-done.2, bf16[32,172,516]{2,1,0:T(8,128)(2,1)} %copy-done.1, bf16[4,1024]{1,0:T(4,128)(2,1)S(1)} %copy-done.19, bf16[512,1024]{1,0:T(8,128)(2,1)S(1)} %copy-done.7), kind=kOutput, calls=%fused_computation.43 | convolution fusion | flops 2912980992 | bytes 14671872 | tf_op jit(solution)/shard_map/ecr,ecd->rd/dot_general | solution.py:247
  (136 shorter events, 79.0 us)
Async XLA Ops:
  6.5 98.8 %all-gather.5.cloned.1.call-start = ((), (), s32[]{:S(2)}) async-start(), calls=%async_computation.5 | async-start | bytes 5570560 | tf_op jit(solution)/shard_map/all_gather | solution.py:160
  8.2 6.5 %collective-permute-start = (bf16[34,2048]{1,0:T(8,128)(2,1)S(1)}, bf16[34,2048]{1,0:T(8,128)(2,1)S(1)}, u32[]{:S(2)}, u32[]{:S(2)}) collective-permute-start(bf16[34,2048]{1,0:T(8,128)(2,1)S(1)} %constant_dynamic-update-slice_fusion), channel_id=1, source_target_pairs={{0,16},{16,0},{1,17},{17,1},{2,18},{18,2},{3,19},{19,3},{4,20},{20... | collective-permute-start | bytes 417800 | tf_op jit(solution)/shard_map/ppermute | solution.py:116
  15.6 35.7 %collective-permute-start.1 = (bf16[1024,32]{0,1:T(8,128)(2,1)}, bf16[1024,32]{0,1:T(8,128)(2,1)S(1)}, u32[]{:S(2)}, u32[]{:S(2)}) collective-permute-start(bf16[1024,32]{0,1:T(8,128)(2,1)} %param.25), channel_id=1, source_target_pairs={{0,16},{16,0},{1,17},{17,1},{2,18},{18,2},{3,19},{19,3},{4,20},{20... | collective-permute-start | bytes 196616 | tf_op jit(solution)/shard_map/ppermute | solution.py:116
  24.6 8.2 %copy-start.4 = (bf16[8,1,1024,128]{3,2,1,0:T(8,128)(2,1)S(1)}, bf16[8,1,1024,128]{3,2,1,0:T(8,128)(2,1)}, u32[]{:S(2)}) copy-start(bf16[8,1,1024,128]{3,2,1,0:T(8,128)(2,1)} %param.21) | copy-start | bytes 6291460
  24.6 185.1 %all-to-all-start.1 = ((bf16[32,2,48,1024]{3,2,1,0:T(8,128)(2,1)}), bf16[32,2,48,1024]{3,2,1,0:T(8,128)(2,1)}, u32[]{:S(2)}, u32[]{:S(2)}) async-start(bf16[32,2,48,1024]{3,2,1,0:T(8,128)(2,1)} %pad_maximum_fusion), calls=%async_computation.1 | async-start | bytes 12582912 | tf_op jit(solution)/shard_map/all_to_all | solution.py:199
  32.1 166.3 %all-gather.7.cloned.1.call-start = ((), (), s32[]{:S(2)}) async-start(), calls=%async_computation.6 | async-start | bytes 2228224 | tf_op jit(solution)/shard_map/all_gather | solution.py:179
  35.4 5.7 copy-start
  35.5 10.9 %copy-start.12 = (pred[516,32]{0,1:T(8,128)(4,1)}, pred[516,32]{0,1:T(8,128)(4,1)S(1)}, u32[]{:S(2)}) copy-start(pred[516,32]{0,1:T(8,128)(4,1)S(1)} %fusion.64) | copy-start | bytes 49540
  37.9 8.5 %copy-start.9 = (s32[32,516]{1,0:T(8,128)}, s32[32,516]{1,0:T(8,128)S(1)}, u32[]{:S(2)}) copy-start(s32[32,516]{1,0:T(8,128)S(1)} %fusion.66) | copy-start | bytes 198148
  43.9 7.3 %copy-start.16 = (bf16[1024,32]{0,1:T(8,128)(2,1)S(1)}, bf16[1024,32]{0,1:T(8,128)(2,1)}, u32[]{:S(2)}) copy-start(bf16[1024,32]{0,1:T(8,128)(2,1)} %param.25) | copy-start | bytes 196612
  121.2 5.1 copy-start.7
  121.2 5.4 copy-start.20
  152.9 24.4 %copy-start.8 = (bf16[8,1024,64]{1,2,0:T(8,128)(2,1)S(1)}, bf16[8,1024,64]{1,2,0:T(8,128)(2,1)}, u32[]{:S(2)}) copy-start(bf16[8,1024,64]{1,2,0:T(8,128)(2,1)} %get-tuple-element.13) | copy-start | bytes 3145732
  152.9 24.4 %copy-start.11 = (bf16[8,512,64]{1,2,0:T(8,128)(2,1)S(1)}, bf16[8,512,64]{1,2,0:T(8,128)(2,1)}, u32[]{:S(2)}) copy-start(bf16[8,512,64]{1,2,0:T(8,128)(2,1)} %fusion.65) | copy-start | bytes 1572868
  209.7 22.6 %copy-start.26 = (bf16[516,1024]{1,0:T(8,128)(2,1)S(1)}, bf16[516,1024]{1,0:T(8,128)(2,1)}, u32[]{:S(2)}) copy-start(bf16[516,1024]{1,0:T(8,128)(2,1)} %copy-done.25) | copy-start | bytes 3170308
  209.7 111.0 %all-to-all-start.3 = ((bf16[16,172,1024]{2,1,0:T(8,128)(2,1)}), bf16[16,172,1024]{2,1,0:T(8,128)(2,1)}, u32[]{:S(2)}, u32[]{:S(2)}) async-start(bf16[16,172,1024]{2,1,0:T(8,128)(2,1)} %fusion.22), calls=%async_computation.3 | async-start | bytes 11534336 | tf_op jit(solution)/shard_map/all_to_all | solution.py:237
  320.8 92.7 %all-to-all-start = ((bf16[16,172,1024]{2,1,0:T(8,128)(2,1)}), bf16[16,172,1024]{2,1,0:T(8,128)(2,1)}, u32[]{:S(2)}, u32[]{:S(2)}) async-start(bf16[16,172,1024]{2,1,0:T(8,128)(2,1)} %fusion.19), calls=%async_computation | async-start | bytes 11534336 | tf_op jit(solution)/shard_map/all_to_all | solution.py:237
  413.4 92.7 %all-to-all-start.4 = ((bf16[16,172,1024]{2,1,0:T(8,128)(2,1)}), bf16[16,172,1024]{2,1,0:T(8,128)(2,1)}, u32[]{:S(2)}, u32[]{:S(2)}) async-start(bf16[16,172,1024]{2,1,0:T(8,128)(2,1)} %convolution_convert_fusion), calls=%async_computation.4 | async-start | bytes 11534336 | tf_op jit(solution)/shard_map/all_to_all | solution.py:245
  432.0 78.8 %copy-start.17 = (bf16[516,8]{0,1:T(8,128)(2,1)S(1)}, bf16[516,8]{0,1:T(8,128)(2,1)}, u32[]{:S(2)}) copy-start(bf16[516,8]{0,1:T(8,128)(2,1)} %param.29) | copy-start | bytes 24772
  432.0 78.9 %copy-start.15 = (s32[516,8]{0,1:T(8,128)S(1)}, s32[516,8]{0,1:T(8,128)}, u32[]{:S(2)}) copy-start(s32[516,8]{0,1:T(8,128)} %param.28) | copy-start | bytes 49540
  432.0 79.0 %copy-start.10 = (s32[32,516]{1,0:T(8,128)S(1)}, s32[32,516]{1,0:T(8,128)}, u32[]{:S(2)}) copy-start(s32[32,516]{1,0:T(8,128)} %copy-done.9) | copy-start | bytes 198148
  432.0 79.0 %copy-start.13 = (pred[516,32]{0,1:T(8,128)(4,1)S(1)}, pred[516,32]{0,1:T(8,128)(4,1)}, u32[]{:S(2)}) copy-start(pred[516,32]{0,1:T(8,128)(4,1)} %copy-done.12) | copy-start | bytes 49540
  506.1 92.8 %all-to-all-start.2 = ((bf16[16,172,1024]{2,1,0:T(8,128)(2,1)}), bf16[16,172,1024]{2,1,0:T(8,128)(2,1)}, u32[]{:S(2)}, u32[]{:S(2)}) async-start(bf16[16,172,1024]{2,1,0:T(8,128)(2,1)} %convolution_convert_fusion.1), calls=%async_computation.2 | async-start | bytes 11534336 | tf_op jit(solution)/shard_map/all_to_all | solution.py:245
  519.4 79.5 %copy-start.27 = (bf16[516,1024]{1,0:T(8,128)(2,1)S(1)}, bf16[516,1024]{1,0:T(8,128)(2,1)}, u32[]{:S(2)}) copy-start(bf16[516,1024]{1,0:T(8,128)(2,1)} %copy-done.25) | copy-start | bytes 3170308
  (13 other events, 43.4 us)
Sparse Core Ops, SparseCore 0:
  15.7 89.5 all-gather.4
  147.4 50.9 all-gather.6

commit v7 on v4

--- a/solution.py
+++ b/solution.py
@@ -6,6 +6,7 @@
 EPSILON = 1e-06
 ROTARY_BASE = 10000.0
 SCORE_SCALE = 0.015625
+DL = ("dc", "core")
 
 
 def root_norm(values, gain):
@@ -109,13 +110,16 @@
     return jnp.concatenate([pre_out, dec_out], axis=1).reshape(-1, columns)
 
 
+def pair_over(shard, axis):
+    if lax.axis_size(axis) == 1:
+        return shard[None]
+    other = lax.ppermute(shard, axis, [(0, 1), (1, 0)])
+    first = lax.axis_index(axis) == 0
+    return jnp.stack([jnp.where(first, shard, other), jnp.where(first, other, shard)])
+
+
 def across_halves(shard):
-    halves = lax.axis_size("zh")
-    if halves == 1:
-        return shard[None]
-    other = lax.ppermute(shard, "zh", [(0, 1), (1, 0)])
-    first = lax.axis_index("zh") == 0
-    return jnp.stack([jnp.where(first, shard, other), jnp.where(first, other, shard)])
+    return pair_over(shard, "zh")
 
 
 def local(
@@ -135,12 +139,14 @@
     routes,
     route_gates,
 ):
-    dp = ("zh", "dl")
+    dp = ("zh", *DL)
     halves = lax.axis_size("zh")
-    half_size = lax.axis_size("dl")
+    half_size = lax.axis_size("dc") * lax.axis_size("core")
     group_count = halves * half_size
     part_count = lax.axis_size("mp")
-    group_index = lax.axis_index("zh") * half_size + lax.axis_index("dl")
+    group_index = (
+        lax.axis_index("zh") * lax.axis_size("dc") + lax.axis_index("dc")
+    ) * lax.axis_size("core") + lax.axis_index("core")
     part_index = lax.axis_index("mp")
     pre_rows = pre_tokens.shape[0]
     width = pre_tokens.shape[1]
@@ -182,8 +188,8 @@
     local_width = qkv_weight.shape[1]
     qkv_pair = across_halves(qkv_weight)
     out_pair = jnp.moveaxis(across_halves(out_weight), 0, 1)
-    qkv_full = lax.all_gather(qkv_pair, "dl", axis=0, tiled=False)
-    qkv_full = jnp.swapaxes(qkv_full, 0, 1).reshape(-1, local_width)
+    qkv_full = pair_over(lax.all_gather(qkv_pair, "dc", axis=0, tiled=False), "core")
+    qkv_full = jnp.transpose(qkv_full, (2, 1, 0, 3, 4)).reshape(-1, local_width)
     qkv_full, out_pair = lax.optimization_barrier((qkv_full, out_pair))
     projected = jnp.dot(group_rows, qkv_full, preferred_element_type=jnp.float32)
     local_groups = dec_cache.shape[0]
@@ -191,8 +197,8 @@
     attn_out = group_attention(
         projected, prior_cache[:, 0], dec_cache, dec_lengths, pre_offsets[0], pre_rows, head_dim
     )
-    out_full = lax.all_gather(out_pair, "dl", axis=1, tiled=False)
-    out_full = jnp.swapaxes(out_full, 1, 2).reshape(out_weight.shape[0], -1)
+    out_full = pair_over(lax.all_gather(out_pair, "dc", axis=1, tiled=False), "core")
+    out_full = jnp.transpose(out_full, (1, 3, 2, 0, 4)).reshape(out_weight.shape[0], -1)
     partial_sums = jnp.dot(attn_out, out_full, preferred_element_type=jnp.float32)
     attn_sum = lax.psum_scatter(
         partial_sums.astype(jnp.bfloat16), "mp", scatter_dimension=0, tiled=True
@@ -249,7 +255,7 @@
             "ecr,rd->ecd", table, normed_moe, preferred_element_type=jnp.float32
         ).astype(jnp.bfloat16)
         outbound = outbound.reshape(half_size, -1, width)
-        arrived = lax.all_to_all(outbound, "dl", split_axis=0, concat_axis=0, tiled=True)
+        arrived = lax.all_to_all(outbound, DL, split_axis=0, concat_axis=0, tiled=True)
         both = jnp.einsum(
             "snd,df->snf", arrived, full_gu[l], preferred_element_type=jnp.float32
         )
@@ -257,7 +263,7 @@
         expert_out = jnp.einsum(
             "snf,fd->snd", activation, full_dn[l], preferred_element_type=jnp.float32
         ).astype(jnp.bfloat16)
-        returned = lax.all_to_all(expert_out, "dl", split_axis=0, concat_axis=0, tiled=True)
+        returned = lax.all_to_all(expert_out, DL, split_axis=0, concat_axis=0, tiled=True)
         returned = returned.reshape(-1, capacity, width)
         moe_sum = moe_sum + jnp.einsum(
             "ecr,ecd->rd", combine_table[picked], returned, preferred_element_type=jnp.float32
@@ -268,9 +274,10 @@
 def solution(mesh):
     groups = mesh.shape["dp"]
     halves = 2 if groups % 2 == 0 else 1
-    devices = mesh.devices.reshape(halves, groups // halves, mesh.shape["mp"])
-    split_mesh = jax.sharding.Mesh(devices, ("zh", "dl", "mp"))
-    dp = ("zh", "dl")
+    cores = 2 if groups % (2 * halves) == 0 else 1
+    devices = mesh.devices.reshape(halves, groups // halves // cores, cores, mesh.shape["mp"])
+    split_mesh = jax.sharding.Mesh(devices, ("zh", "dc", "core", "mp"))
+    dp = ("zh", *DL)
     return jax.shard_map(
         local,
         mesh=split_mesh,

time: 593 us -> 618 us (1.042)
  waiting for transfers between devices: 352 us -> 364 us
  starting transfers between devices: 37 us -> 46.8 us
    all_gather x2, waiting for transfers between devices: 7.94 us -> 31.9 us  [the longest x1 20 us: local(): lax.all_gather(qkv_pair, 'dc', axis=0, tiled=False)]
    all_to_all x1, waiting for transfers between devices: 44 us -> 32.4 us  [local(): lax.all_to_all(jnp.concatenate([owner_major(gate_up), owner_major(down_we...]
    ppermute x2 -> x4, starting transfers between devices: 0.36 us -> 6.68 us  [pair_over(): other = lax.ppermute(shard, axis, [(0, 1), (1, 0)])]
    unnamed x59 -> x61, local copies, waits for them, and re-layouts: 15.9 us -> 19.1 us
  transfers between devices with their start and end apart: 10 -> 12, of which waited for: 7 -> 9; matrix products, arithmetic and copies ran while one was open for 28% -> 27% of each run, Pallas kernels for 0% -> 0%
where the time goes in v7:
time: 618 us; the launch traced here: 607 us
  waiting for transfers between devices  364 us (59%)
  matrix products  109 us (18%)
  starting transfers between devices  46.8 us (8%)
  local copies, waits for them, and re-layouts  41.6 us (7%)
  other arithmetic  31.1 us (5%)
  between operations  14.8 us (2%)
    all_to_all x2, waiting for transfers between devices, local(): lax.all_to_all(outbound, DL, split_axis=0, concat_axis=0, tiled=True)  148 us
    all_to_all x2, waiting for transfers between devices, local(): lax.all_to_all(expert_out, DL, split_axis=0, concat_axis=0, tiled=True)  146 us
    all_to_all x1, waiting for transfers between devices, local(): lax.all_to_all(jnp.concatenate([owner_major(gate_up), owner_major(down_we...  32.4 us
    sub x1, matrix products, prefill_attention(): expo = jnp.exp(scores - highest)  24.1 us
    all_gather x1, waiting for transfers between devices, local(): lax.all_gather(qkv_pair, 'dc', axis=0, tiled=False)  20 us
    unnamed x61, local copies, waits for them, and re-layouts  19.1 us
    dot_general x1, matrix products, prefill_attention(): jnp.einsum('gpck,gkh->cgph', weights, all_values, preferred_element_type=...  18.5 us
    dot_general x2, matrix products, local(): jnp.einsum('snd,df->snf', arrived, full_gu[l], preferred_element_type=jnp...  17.2 us
  transfers between devices with their start and end apart: 12, of which 9 were waited for; matrix products, arithmetic and copies ran while one was open for 27% of the time, Pallas kernels for 0%

profile of v7, /device:TPU:23, one launch (start us, length us, event | category | flops | bytes accessed | tf_op | source)
XLA Modules:
  0.0 607.5 jit_solution(14214144945515083284)
XLA Ops:
  16.9 10.1 %all-to-all-start = ((bf16[32,2,512]{2,1,0:T(2,128)(2,1)}), bf16[32,2,512]{2,1,0:T(2,128)(2,1)S(1)}, u32[]{:S(2)}, u32[]{:S(2)}) async-start(bf16[32,2,512]{2,1,0:T(2,128)(2,1)} %reshape.494), calls=%async_computation | async-start | bytes 131072 | tf_op jit(solution)/shard_map/all_to_all | solution.py:169
  46.2 20.0 %all-gather.5.cloned.1.call-done = bf16[16,32,2048]{2,1,0:T(8,128)(2,1)} async-done(((bf16[2,32,2048]{2,1,0:T(8,128)(2,1)}), bf16[16,32,2048]{2,1,0:T(8,128)(2,1)}) %all-gather.5.cloned.1.call-update) | async-done | bytes 2097168 | tf_op jit(solution)/shard_map/all_gather | solution.py:191
  68.2 4.8 fusion.6
  73.7 7.2 %all-to-all-start.2 = ((bf16[32,2,48,1024]{3,2,1,0:T(8,128)(2,1)}), bf16[32,2,48,1024]{3,2,1,0:T(8,128)(2,1)}, u32[]{:S(2)}, u32[]{:S(2)}) async-start(bf16[32,2,48,1024]{3,2,1,0:T(8,128)(2,1)} %pad_maximum_fusion), calls=%async_computation.2 | async-start | bytes 12582912 | tf_op jit(solution)/shard_map/all_to_all | solution.py:220
  94.7 5.5 copy.104
  107.7 24.1 %fusion.95 = (f32[8,2,512]{2,1,0:T(2,128)S(1)}, f32[8,2,512,1536]{2,3,1,0:T(8,128)}) fusion(pred[512,1536]{0,1:T(8,128)(4,1)} %fusion.25, bf16[8,512,64]{1,2,0:T(8,128)(2,1)} %maximum_bitcast_fusion.15, bf16[8,1024,64]{1,2,0:T(8,128)(2,1)} %get-tuple-element.16, bf16[512,8,2,32]{0,3,2,1:T(8,128)(2,1)} %get-tuple-element.14, ...), kind=kOutput, calls=%fused_computation.168 | convolution fusion | flops 1666188800 | bytes 53772288 | tf_op jit(solution)/shard_map/sub | solution.py:61
  131.8 18.5 %fusion.43 = bf16[8,64,2,512]{3,1,2,0:T(8,128)(2,1)} fusion(f32[8,2,512,1536]{2,3,1,0:T(8,128)} %get-tuple-element.38, f32[8,2,512]{2,1,0:T(2,128)S(1)} %get-tuple-element.37, bf16[8,512,64]{1,2,0:T(8,128)(2,1)} %fusion.66, bf16[8,1024,64]{1,2,0:T(8,128)(2,1)S(1)} %copy-done.11), kind=kOutput, calls=%fused_computation.63 | convolution fusion | flops 1639448576 | bytes 52985856 | tf_op jit(solution)/shard_map/gpck,gkh->cgph/dot_general | solution.py:63
  154.1 12.0 %all-gather.7.cloned.1.call-done = bf16[1024,16,32]{0,2,1:T(8,128)(2,1)} async-done(((bf16[1024,2,32]{0,2,1:T(8,128)(2,1)}), bf16[1024,16,32]{0,2,1:T(8,128)(2,1)}) %all-gather.7.cloned.1.call-update) | async-done | bytes 1048592 | tf_op jit(solution)/shard_map/all_gather | solution.py:200
  176.7 7.2 %fusion.22 = bf16[16,172,1024]{2,1,0:T(8,128)(2,1)} fusion(pred[32,172,516]{2,1,0:T(8,128)(4,1)S(1)} %copy-done.6, bf16[516,1024]{1,0:T(8,128)(2,1)S(1)} %get-tuple-element.40, f32[1024]{0:T(1024)S(1)} %copy-done.21, f32[516]{0:T(1024)S(1)} %add_rsqrt_fusion, bf16[4,1024]{1,0:T(4,128)(2,1)S(1)} %convolution_convert_fusion.4, ...), kind=kOutput, calls=%fused_computation.30 | convolution fusion | flops 2915799040 | bytes 9568256 | tf_op jit(solution)/shard_map/ecr,rd->ecd/dot_general | solution.py:254
  183.9 32.4 %all-to-all-done.2 = bf16[32,2,48,1024]{3,2,1,0:T(8,128)(2,1)} async-done(((bf16[32,2,48,1024]{3,2,1,0:T(8,128)(2,1)}), bf16[32,2,48,1024]{3,2,1,0:T(8,128)(2,1)}, u32[]{:S(2)}, u32[]{:S(2)}) %all-to-all-start.2) | async-done | bytes 6291488 | tf_op jit(solution)/shard_map/all_to_all | solution.py:220
  216.3 8.6 %all-to-all-start.4 = ((bf16[16,172,1024]{2,1,0:T(8,128)(2,1)}), bf16[16,172,1024]{2,1,0:T(8,128)(2,1)}, u32[]{:S(2)}, u32[]{:S(2)}) async-start(bf16[16,172,1024]{2,1,0:T(8,128)(2,1)} %fusion.22), calls=%async_computation.4 | async-start | bytes 11534336 | tf_op jit(solution)/shard_map/all_to_all | solution.py:258
  224.9 8.2 %fusion.19 = bf16[16,172,1024]{2,1,0:T(8,128)(2,1)} fusion(pred[32,172,516]{2,1,0:T(8,128)(4,1)} %fusion.6, bf16[516,1024]{1,0:T(8,128)(2,1)S(1)} %copy-done.26, f32[1024]{0:T(1024)S(1)} %copy-done.21, f32[516]{0:T(1024)S(1)} %add_rsqrt_fusion, bf16[4,1024]{1,0:T(4,128)(2,1)S(1)} %convolution_convert_fusion.4, bf16[512,1024]{1,0:T(8,128)(2,1)S(1)} %copy-done.10), kind=kOutput, calls=%fused_computation.29 | convolution fusion | flops 2915799040 | bytes 9558032 | tf_op jit(solution)/shard_map/ecr,rd->ecd/dot_general | solution.py:254
  233.1 80.6 %all-to-all-done.4 = bf16[16,172,1024]{2,1,0:T(8,128)(2,1)} async-done(((bf16[16,172,1024]{2,1,0:T(8,128)(2,1)}), bf16[16,172,1024]{2,1,0:T(8,128)(2,1)}, u32[]{:S(2)}, u32[]{:S(2)}) %all-to-all-start.4) | async-done | bytes 5636128 | tf_op jit(solution)/shard_map/all_to_all | solution.py:258
  325.1 8.3 %fusion.33 = f32[16,172,1024]{2,1,0:T(8,128)S(1)} fusion(bf16[16,172,1024]{2,1,0:T(8,128)(2,1)} %all-to-all-done.4, bf16[1,2,1024,1024]{3,2,1,0:T(8,128)(2,1)S(1)} %bitcast.168), kind=kOutput, calls=%fused_computation.47 | convolution fusion | flops 5771362304 | bytes 19005440 | tf_op jit(solution)/shard_map/snd,df->snf/dot_general | solution.py:259
  333.4 5.1 convolution_convert_fusion
  338.6 67.7 %all-to-all-done.1 = bf16[16,172,1024]{2,1,0:T(8,128)(2,1)} async-done(((bf16[16,172,1024]{2,1,0:T(8,128)(2,1)}), bf16[16,172,1024]{2,1,0:T(8,128)(2,1)}, u32[]{:S(2)}, u32[]{:S(2)}) %all-to-all-start.1) | async-done | bytes 5636128 | tf_op jit(solution)/shard_map/all_to_all | solution.py:258
  406.3 4.7 all-to-all-start.5
  411.0 8.9 %fusion.34 = f32[16,172,1024]{2,1,0:T(8,128)S(1)} fusion(bf16[16,172,1024]{2,1,0:T(8,128)(2,1)} %all-to-all-done.1, bf16[1,2,1024,1024]{3,2,1,0:T(8,128)(2,1)} %bitcast.169), kind=kOutput, calls=%fused_computation.50 | convolution fusion | flops 5771362304 | bytes 19136512 | tf_op jit(solution)/shard_map/snd,df->snf/dot_general | solution.py:259
  419.9 5.2 convolution_convert_fusion.1
  425.0 74.0 %all-to-all-done.5 = bf16[16,172,1024]{2,1,0:T(8,128)(2,1)} async-done(((bf16[16,172,1024]{2,1,0:T(8,128)(2,1)}), bf16[16,172,1024]{2,1,0:T(8,128)(2,1)}, u32[]{:S(2)}, u32[]{:S(2)}) %all-to-all-start.5) | async-done | bytes 5636128 | tf_op jit(solution)/shard_map/all_to_all | solution.py:266
  503.8 5.5 select_convert_fusion
  512.2 7.4 %fusion.15 = f32[516,1024,1]{1,0,2:T(8,128)} fusion(bf16[16,172,1024]{2,1,0:T(8,128)(2,1)} %all-to-all-done.5, bf16[32,172,516]{2,1,0:T(8,128)(2,1)S(1)} %select_convert_fusion), kind=kOutput, calls=%fused_computation.25 | convolution fusion | flops 2908225536 | bytes 11354112 | tf_op jit(solution)/shard_map/ecr,ecd->rd/dot_general | solution.py:268
  519.6 72.1 %all-to-all-done.3 = bf16[16,172,1024]{2,1,0:T(8,128)(2,1)} async-done(((bf16[16,172,1024]{2,1,0:T(8,128)(2,1)}), bf16[16,172,1024]{2,1,0:T(8,128)(2,1)}, u32[]{:S(2)}, u32[]{:S(2)}) %all-to-all-start.3) | async-done | bytes 5636128 | tf_op jit(solution)/shard_map/all_to_all | solution.py:266
  591.8 8.7 %fusion.32 = bf16[516,1024]{1,0:T(8,128)(2,1)} fusion(f32[516,1024,1]{1,0,2:T(8,128)} %fusion.15, bf16[516,1024]{1,0:T(8,128)(2,1)S(1)} %copy-done.27, bf16[16,172,1024]{2,1,0:T(8,128)(2,1)} %all-to-all-done.3, bf16[32,172,516]{2,1,0:T(8,128)(2,1)} %copy-done.4, bf16[4,1024]{1,0:T(4,128)(2,1)S(1)} %convolution_convert_fusion.4, ...), kind=kOutput, calls=%fused_computation.43 | convolution fusion | flops 2912980992 | bytes 14671872 | tf_op jit(solution)/shard_map/ecr,ecd->rd/dot_general | solution.py:268
  (146 shorter events, 85.9 us)
Async XLA Ops:
  6.5 59.6 %all-gather.5.cloned.1.call-start = ((), (), s32[]{:S(2)}) async-start(), calls=%async_computation.6 | async-start | bytes 2359296 | tf_op jit(solution)/shard_map/all_gather | solution.py:191
  6.5 6.6 %collective-permute-start = (bf16[32,2048]{1,0:T(8,128)(2,1)}, bf16[32,2048]{1,0:T(8,128)(2,1)S(1)}, u32[]{:S(2)}, u32[]{:S(2)}) collective-permute-start(bf16[32,2048]{1,0:T(8,128)(2,1)} %param.24), channel_id=1, source_target_pairs={{0,16},{16,0},{1,17},{17,1},{2,18},{18,2},{3,19},{19,3},{4,20},{20... | collective-permute-start | bytes 393224 | tf_op jit(solution)/shard_map/ppermute | solution.py:116
  6.6 66.4 %collective-permute-start.2 = (bf16[1024,32]{0,1:T(8,128)(2,1)}, bf16[1024,32]{0,1:T(8,128)(2,1)S(1)}, u32[]{:S(2)}, u32[]{:S(2)}) collective-permute-start(bf16[1024,32]{0,1:T(8,128)(2,1)} %param.25), channel_id=1, source_target_pairs={{0,16},{16,0},{1,17},{17,1},{2,18},{18,2},{3,19},{19,3},{4,20},{20... | collective-permute-start | bytes 196616 | tf_op jit(solution)/shard_map/ppermute | solution.py:116
  14.1 16.4 %copy-start.16 = (s32[516,8]{0,1:T(8,128)S(1)}, s32[516,8]{0,1:T(8,128)}, u32[]{:S(2)}) copy-start(s32[516,8]{0,1:T(8,128)} %param.28) | copy-start | bytes 49540
  14.9 17.5 %copy-start.22 = (s32[128]{0:T(128)S(1)}, s32[128]{0:T(128)}, u32[]{:S(2)}) copy-start(s32[128]{0:T(128)} %param.17) | copy-start | bytes 1540
  16.9 56.9 %all-to-all-start = ((bf16[32,2,512]{2,1,0:T(2,128)(2,1)}), bf16[32,2,512]{2,1,0:T(2,128)(2,1)S(1)}, u32[]{:S(2)}, u32[]{:S(2)}) async-start(bf16[32,2,512]{2,1,0:T(2,128)(2,1)} %reshape.494), calls=%async_computation | async-start | bytes 131072 | tf_op jit(solution)/shard_map/all_to_all | solution.py:169
  30.6 37.6 %copy-start.14 = (pred[516,32]{0,1:T(8,128)(4,1)}, pred[516,32]{0,1:T(8,128)(4,1)S(1)}, u32[]{:S(2)}) copy-start(pred[516,32]{0,1:T(8,128)(4,1)S(1)} %fusion.65) | copy-start | bytes 49540
  33.2 35.0 %copy-start.12 = (s32[32,516]{1,0:T(8,128)}, s32[32,516]{1,0:T(8,128)S(1)}, u32[]{:S(2)}) copy-start(s32[32,516]{1,0:T(8,128)S(1)} %fusion.67) | copy-start | bytes 198148
  43.8 29.2 %copy-start.18 = (bf16[1024,32]{0,1:T(8,128)(2,1)S(1)}, bf16[1024,32]{0,1:T(8,128)(2,1)}, u32[]{:S(2)}) copy-start(bf16[1024,32]{0,1:T(8,128)(2,1)} %param.25) | copy-start | bytes 196612
  66.1 15.9 %collective-permute-start.1 = (bf16[8,2,32,2048]{3,2,1,0:T(8,128)(2,1)}, bf16[8,2,32,2048]{3,2,1,0:T(8,128)(2,1)}, u32[]{:S(2)}, u32[]{:S(2)}) collective-permute-start(bf16[8,2,32,2048]{3,2,1,0:T(8,128)(2,1)} %bitcast.175), channel_id=1, source_target_pairs={{0,1},{1,0},{2,3},{3,2},{4,5},{5,4},{6,7},{7,6},{8,9},{9,8},{10,11... | collective-permute-start | bytes 6291464 | tf_op jit(solution)/shard_map/ppermute | solution.py:116
  73.7 142.6 %all-to-all-start.2 = ((bf16[32,2,48,1024]{3,2,1,0:T(8,128)(2,1)}), bf16[32,2,48,1024]{3,2,1,0:T(8,128)(2,1)}, u32[]{:S(2)}, u32[]{:S(2)}) async-start(bf16[32,2,48,1024]{3,2,1,0:T(8,128)(2,1)} %pad_maximum_fusion), calls=%async_computation.2 | async-start | bytes 12582912 | tf_op jit(solution)/shard_map/all_to_all | solution.py:220
  81.0 85.0 %all-gather.7.cloned.1.call-start = ((), (), s32[]{:S(2)}) async-start(), calls=%async_computation.7 | async-start | bytes 1179648 | tf_op jit(solution)/shard_map/all_gather | solution.py:200
  107.7 24.1 %copy-start.11 = (bf16[8,1024,64]{1,2,0:T(8,128)(2,1)S(1)}, bf16[8,1024,64]{1,2,0:T(8,128)(2,1)}, u32[]{:S(2)}) copy-start(bf16[8,1024,64]{1,2,0:T(8,128)(2,1)} %get-tuple-element.15) | copy-start | bytes 3145732
  166.0 4.9 collective-permute-start.3
  183.9 41.0 %copy-start.26 = (bf16[516,1024]{1,0:T(8,128)(2,1)S(1)}, bf16[516,1024]{1,0:T(8,128)(2,1)}, u32[]{:S(2)}) copy-start(bf16[516,1024]{1,0:T(8,128)(2,1)} %copy-done.25) | copy-start | bytes 3170308
  216.3 97.4 %all-to-all-start.4 = ((bf16[16,172,1024]{2,1,0:T(8,128)(2,1)}), bf16[16,172,1024]{2,1,0:T(8,128)(2,1)}, u32[]{:S(2)}, u32[]{:S(2)}) async-start(bf16[16,172,1024]{2,1,0:T(8,128)(2,1)} %fusion.22), calls=%async_computation.4 | async-start | bytes 11534336 | tf_op jit(solution)/shard_map/all_to_all | solution.py:258
  313.7 92.6 %all-to-all-start.1 = ((bf16[16,172,1024]{2,1,0:T(8,128)(2,1)}), bf16[16,172,1024]{2,1,0:T(8,128)(2,1)}, u32[]{:S(2)}, u32[]{:S(2)}) async-start(bf16[16,172,1024]{2,1,0:T(8,128)(2,1)} %fusion.19), calls=%async_computation.1 | async-start | bytes 11534336 | tf_op jit(solution)/shard_map/all_to_all | solution.py:258
  406.3 92.8 %all-to-all-start.5 = ((bf16[16,172,1024]{2,1,0:T(8,128)(2,1)}), bf16[16,172,1024]{2,1,0:T(8,128)(2,1)}, u32[]{:S(2)}, u32[]{:S(2)}) async-start(bf16[16,172,1024]{2,1,0:T(8,128)(2,1)} %convolution_convert_fusion), calls=%async_computation.5 | async-start | bytes 11534336 | tf_op jit(solution)/shard_map/all_to_all | solution.py:266
  425.0 78.6 %copy-start.19 = (bf16[516,8]{0,1:T(8,128)(2,1)S(1)}, bf16[516,8]{0,1:T(8,128)(2,1)}, u32[]{:S(2)}) copy-start(bf16[516,8]{0,1:T(8,128)(2,1)} %param.29) | copy-start | bytes 24772
  425.0 78.6 %copy-start.17 = (s32[516,8]{0,1:T(8,128)S(1)}, s32[516,8]{0,1:T(8,128)}, u32[]{:S(2)}) copy-start(s32[516,8]{0,1:T(8,128)} %param.28) | copy-start | bytes 49540
  425.0 78.7 %copy-start.13 = (s32[32,516]{1,0:T(8,128)S(1)}, s32[32,516]{1,0:T(8,128)}, u32[]{:S(2)}) copy-start(s32[32,516]{1,0:T(8,128)} %copy-done.12) | copy-start | bytes 198148
  425.0 78.7 %copy-start.15 = (pred[516,32]{0,1:T(8,128)(4,1)S(1)}, pred[516,32]{0,1:T(8,128)(4,1)}, u32[]{:S(2)}) copy-start(pred[516,32]{0,1:T(8,128)(4,1)} %copy-done.14) | copy-start | bytes 49540
  499.1 92.7 %all-to-all-start.3 = ((bf16[16,172,1024]{2,1,0:T(8,128)(2,1)}), bf16[16,172,1024]{2,1,0:T(8,128)(2,1)}, u32[]{:S(2)}, u32[]{:S(2)}) async-start(bf16[16,172,1024]{2,1,0:T(8,128)(2,1)} %convolution_convert_fusion.1), calls=%async_computation.3 | async-start | bytes 11534336 | tf_op jit(solution)/shard_map/all_to_all | solution.py:266
  512.2 79.6 %copy-start.27 = (bf16[516,1024]{1,0:T(8,128)(2,1)S(1)}, bf16[516,1024]{1,0:T(8,128)(2,1)}, u32[]{:S(2)}) copy-start(bf16[516,1024]{1,0:T(8,128)(2,1)} %copy-done.25) | copy-start | bytes 3170308
  (16 other events, 69.1 us)
Sparse Core Ops, SparseCore 0:
  15.0 51.0 all-gather.4
  107.0 58.9 all-gather.6

commit v8 on v7

--- a/solution.py
+++ b/solution.py
@@ -155,31 +155,17 @@
     bundle = max(1, dec_rows // group_count)
     device = group_index * part_count + part_index
     position = jnp.arange(dec_rows, dtype=jnp.int32)
-    own_deal = lax.dynamic_slice_in_dim(deal_slots, device * dec_rows, dec_rows, 0)
-    target = own_deal // (part_count * dec_rows)
-    group_ids = jnp.arange(group_count, dtype=jnp.int32)
-    lane_ids = jnp.arange(bundle, dtype=jnp.int32)
-    send_table = (
-        (target[None, None, :] == group_ids[:, None, None])
-        & (position[None, None, :] % bundle == lane_ids[None, :, None])
-    ).astype(jnp.bfloat16)
-    outgoing = jnp.einsum(
-        "jbi,id->jbd", send_table, dec_tokens, preferred_element_type=jnp.float32
-    ).astype(jnp.bfloat16)
-    incoming = lax.all_to_all(outgoing, dp, split_axis=0, concat_axis=0, tiled=True)
     slot_ids = device * dec_rows + position
-    request_ids = jnp.arange(deal_slots.shape[0], dtype=jnp.int32)
-    request = jnp.sum(
-        jnp.where(deal_slots[None, :] == slot_ids[:, None], request_ids[None, :], 0), axis=1
-    )
-    source = request // (part_count * dec_rows)
-    lane = request % dec_rows % bundle
-    take_table = (
-        (source[:, None, None] == group_ids[None, :, None])
-        & (lane[:, None, None] == lane_ids[None, None, :])
-    ).astype(jnp.bfloat16)
-    slot_rows = jnp.einsum(
-        "ijb,jbd->id", take_table, incoming, preferred_element_type=jnp.float32
+    take_table = (deal_slots[None, :] == slot_ids[:, None]).astype(jnp.bfloat16)
+    every_request = pair_over(
+        lax.all_gather(pair_over(dec_tokens, "zh"), "dc", axis=0, tiled=False), "core"
+    )
+    every_request = jnp.transpose(every_request, (2, 1, 0, 3, 4)).reshape(
+        group_count, dec_rows, width
+    )
+    every_request = lax.all_gather(every_request, "mp", axis=1, tiled=False).reshape(-1, width)
+    slot_rows = jnp.dot(
+        take_table, every_request, preferred_element_type=jnp.float32
     ).astype(jnp.bfloat16)
     layer_input = jnp.concatenate([pre_tokens, slot_rows], axis=0)
     rows_dev = layer_input.shape[0]

time: 618 us -> 670 us (1.084)
  blocking collectives: 0 us -> 33.6 us
  waiting for transfers between devices: 364 us -> 389 us
  starting transfers between devices: 46.8 us -> 39.1 us
    all_gather x1, waiting for transfers between devices: 20 us -> 92.8 us  [local(): lax.all_gather(qkv_pair, 'dc', axis=0, tiled=False)]
    all_gather x0 -> x1, blocking collectives: none -> 33.6 us  [local(): lax.all_gather(pair_over(dec_tokens, 'zh'), 'dc', axis=0, tiled=False)]
    all_to_all x1, waiting for transfers between devices: 32.4 us -> 0.01 us  [local(): lax.all_to_all(jnp.concatenate([owner_major(gate_up), owner_major(down_we...]
    all_gather x1, waiting for transfers between devices: 12 us -> 0.01 us  [local(): lax.all_gather(out_pair, 'dc', axis=1, tiled=False)]
    all_to_all x1 -> x0, starting transfers between devices: 10.1 us -> none  [local(): lax.all_to_all(outgoing, dp, split_axis=0, concat_axis=0, tiled=True)]
    unnamed x61 -> x69, local copies, waits for them, and re-layouts: 19.1 us -> 17.6 us
  transfers between devices with their start and end apart: 12 -> 13, of which waited for: 9 -> 6; matrix products, arithmetic and copies ran while one was open for 27% -> 25% of each run, Pallas kernels for 0% -> 0%
where the time goes in v8:
time: 670 us; the launch traced here: 658 us
  waiting for transfers between devices  389 us (58%)
  matrix products  110 us (16%)
  local copies, waits for them, and re-layouts  41.1 us (6%)
  starting transfers between devices  39.1 us (6%)
  blocking collectives  33.6 us (5%)
  other arithmetic  30.1 us (4%)
  between operations  14.9 us (2%)
    all_to_all x2, waiting for transfers between devices, local(): lax.all_to_all(outbound, DL, split_axis=0, concat_axis=0, tiled=True)  148 us
    all_to_all x2, waiting for transfers between devices, local(): lax.all_to_all(expert_out, DL, split_axis=0, concat_axis=0, tiled=True)  146 us
    all_gather x1, waiting for transfers between devices, local(): lax.all_gather(qkv_pair, 'dc', axis=0, tiled=False)  92.8 us
    all_gather x1, blocking collectives, local(): lax.all_gather(pair_over(dec_tokens, 'zh'), 'dc', axis=0, tiled=False)  33.6 us
    sub x1, matrix products, prefill_attention(): expo = jnp.exp(scores - highest)  23.7 us
    dot_general x1, matrix products, prefill_attention(): jnp.einsum('gpck,gkh->cgph', weights, all_values, preferred_element_type=...  18.6 us
    unnamed x69, local copies, waits for them, and re-layouts  17.6 us
    dot_general x2, matrix products, local(): jnp.einsum('snd,df->snf', arrived, full_gu[l], preferred_element_type=jnp...  17.2 us
  transfers between devices with their start and end apart: 13, of which 6 were waited for; matrix products, arithmetic and copies ran while one was open for 25% of the time, Pallas kernels for 0%

profile of v8, /device:TPU:23, one launch (start us, length us, event | category | flops | bytes accessed | tf_op | source)
XLA Modules:
  0.0 657.7 jit_solution(14443126380842713387)
XLA Ops:
  14.9 7.3 %all-to-all-start.1 = ((bf16[32,2,48,1024]{3,2,1,0:T(8,128)(2,1)}), bf16[32,2,48,1024]{3,2,1,0:T(8,128)(2,1)}, u32[]{:S(2)}, u32[]{:S(2)}) async-start(bf16[32,2,48,1024]{3,2,1,0:T(8,128)(2,1)} %pad_maximum_fusion), calls=%async_computation.1 | async-start | bytes 12582912 | tf_op jit(solution)/shard_map/all_to_all | solution.py:206
  33.7 4.9 fusion.6
  38.6 92.8 %all-gather.6.cloned.1.call-done = bf16[16,32,2048]{2,1,0:T(8,128)(2,1)} async-done(((bf16[2,32,2048]{2,1,0:T(8,128)(2,1)}), bf16[16,32,2048]{2,1,0:T(8,128)(2,1)}) %all-gather.6.cloned.1.call-update) | async-done | bytes 2097168 | tf_op jit(solution)/shard_map/all_gather | solution.py:177
  135.3 33.6 %all-gather = bf16[16,4,1024]{2,1,0:T(4,128)(2,1)S(1)} all-gather(bf16[2,4,1024]{2,1,0:T(4,128)(2,1)S(1)} %pad_maximum_fusion.8), channel_id=2, replica_groups=mesh['zh'=2,'dc'=8,'core'=2,'mp'=1] {'dc'}, dimensions={0}, use_global_device_ids=true | all-gather | bytes 147456 | tf_op jit(solution)/shard_map/all_gather | solution.py:161
  168.9 4.9 collective-permute-start.1
  190.1 5.4 copy.102
  202.9 23.7 %fusion.93 = (f32[8,2,512]{2,1,0:T(2,128)S(1)}, f32[8,2,512,1536]{2,3,1,0:T(8,128)}) fusion(pred[512,1536]{0,1:T(8,128)(4,1)S(1)} %copy-done.13, bf16[8,512,64]{1,2,0:T(8,128)(2,1)} %maximum_bitcast_fusion.15, bf16[8,1024,64]{1,2,0:T(8,128)(2,1)S(1)} %copy-done.12, bf16[512,8,2,32]{0,3,2,1:T(8,128)(2,1)} %get-tuple-element.14, ...), kind=kOutput, calls=%fused_computation.160 | convolution fusion | flops 1666188800 | bytes 53772288 | tf_op jit(solution)/shard_map/sub | solution.py:61
  226.6 18.6 %fusion.43 = bf16[8,64,2,512]{3,1,2,0:T(8,128)(2,1)} fusion(f32[8,2,512,1536]{2,3,1,0:T(8,128)} %get-tuple-element.42, f32[8,2,512]{2,1,0:T(2,128)S(1)} %get-tuple-element.41, bf16[8,512,64]{1,2,0:T(8,128)(2,1)} %fusion.65, bf16[8,1024,64]{1,2,0:T(8,128)(2,1)S(1)} %copy-done.11), kind=kOutput, calls=%fused_computation.63 | convolution fusion | flops 1639448576 | bytes 52985856 | tf_op jit(solution)/shard_map/gpck,gkh->cgph/dot_general | solution.py:63
  257.9 7.2 %fusion.22 = bf16[16,172,1024]{2,1,0:T(8,128)(2,1)} fusion(pred[32,172,516]{2,1,0:T(8,128)(4,1)S(1)} %copy-done.4, bf16[516,1024]{1,0:T(8,128)(2,1)S(1)} %get-tuple-element.44, f32[1024]{0:T(1024)S(1)} %copy-done.26, f32[516]{0:T(1024)S(1)} %add_rsqrt_fusion, bf16[4,1024]{1,0:T(4,128)(2,1)S(1)} %convolution_convert_fusion.3, ...), kind=kOutput, calls=%fused_computation.30 | convolution fusion | flops 2915799040 | bytes 9568256 | tf_op jit(solution)/shard_map/ecr,rd->ecd/dot_general | solution.py:240
  265.1 10.0 %all-to-all-start.3 = ((bf16[16,172,1024]{2,1,0:T(8,128)(2,1)}), bf16[16,172,1024]{2,1,0:T(8,128)(2,1)}, u32[]{:S(2)}, u32[]{:S(2)}) async-start(bf16[16,172,1024]{2,1,0:T(8,128)(2,1)} %fusion.22), calls=%async_computation.3 | async-start | bytes 11534336 | tf_op jit(solution)/shard_map/all_to_all | solution.py:244
  275.2 8.2 %fusion.19 = bf16[16,172,1024]{2,1,0:T(8,128)(2,1)} fusion(pred[32,172,516]{2,1,0:T(8,128)(4,1)} %fusion.6, bf16[516,1024]{1,0:T(8,128)(2,1)S(1)} %copy-done.31, f32[1024]{0:T(1024)S(1)} %copy-done.26, f32[516]{0:T(1024)S(1)} %add_rsqrt_fusion, bf16[4,1024]{1,0:T(4,128)(2,1)S(1)} %convolution_convert_fusion.3, bf16[512,1024]{1,0:T(8,128)(2,1)S(1)} %copy-done.10), kind=kOutput, calls=%fused_computation.29 | convolution fusion | flops 2915799040 | bytes 9558032 | tf_op jit(solution)/shard_map/ecr,rd->ecd/dot_general | solution.py:240
  283.4 80.5 %all-to-all-done.3 = bf16[16,172,1024]{2,1,0:T(8,128)(2,1)} async-done(((bf16[16,172,1024]{2,1,0:T(8,128)(2,1)}), bf16[16,172,1024]{2,1,0:T(8,128)(2,1)}, u32[]{:S(2)}, u32[]{:S(2)}) %all-to-all-start.3) | async-done | bytes 5636128 | tf_op jit(solution)/shard_map/all_to_all | solution.py:244
  363.9 4.5 all-to-all-start
  375.4 8.3 %fusion.33 = f32[16,172,1024]{2,1,0:T(8,128)S(1)} fusion(bf16[16,172,1024]{2,1,0:T(8,128)(2,1)} %all-to-all-done.3, bf16[1,2,1024,1024]{3,2,1,0:T(8,128)(2,1)S(1)} %bitcast.176), kind=kOutput, calls=%fused_computation.47 | convolution fusion | flops 5771362304 | bytes 19005440 | tf_op jit(solution)/shard_map/snd,df->snf/dot_general | solution.py:245
  383.7 5.1 convolution_convert_fusion
  388.8 67.7 %all-to-all-done = bf16[16,172,1024]{2,1,0:T(8,128)(2,1)} async-done(((bf16[16,172,1024]{2,1,0:T(8,128)(2,1)}), bf16[16,172,1024]{2,1,0:T(8,128)(2,1)}, u32[]{:S(2)}, u32[]{:S(2)}) %all-to-all-start) | async-done | bytes 5636128 | tf_op jit(solution)/shard_map/all_to_all | solution.py:244
  456.5 4.7 all-to-all-start.4
  461.2 8.9 %fusion.34 = f32[16,172,1024]{2,1,0:T(8,128)S(1)} fusion(bf16[16,172,1024]{2,1,0:T(8,128)(2,1)} %all-to-all-done, bf16[1,2,1024,1024]{3,2,1,0:T(8,128)(2,1)} %bitcast.177), kind=kOutput, calls=%fused_computation.50 | convolution fusion | flops 5771362304 | bytes 19136512 | tf_op jit(solution)/shard_map/snd,df->snf/dot_general | solution.py:245
  470.1 5.2 convolution_convert_fusion.1
  475.3 74.0 %all-to-all-done.4 = bf16[16,172,1024]{2,1,0:T(8,128)(2,1)} async-done(((bf16[16,172,1024]{2,1,0:T(8,128)(2,1)}), bf16[16,172,1024]{2,1,0:T(8,128)(2,1)}, u32[]{:S(2)}, u32[]{:S(2)}) %all-to-all-start.4) | async-done | bytes 5636128 | tf_op jit(solution)/shard_map/all_to_all | solution.py:252
  554.0 5.5 select_convert_fusion
  562.4 7.3 %fusion.15 = f32[516,1024,1]{1,0,2:T(8,128)} fusion(bf16[16,172,1024]{2,1,0:T(8,128)(2,1)} %all-to-all-done.4, bf16[32,172,516]{2,1,0:T(8,128)(2,1)S(1)} %select_convert_fusion), kind=kOutput, calls=%fused_computation.25 | convolution fusion | flops 2908225536 | bytes 11354112 | tf_op jit(solution)/shard_map/ecr,ecd->rd/dot_general | solution.py:254
  569.7 72.3 %all-to-all-done.2 = bf16[16,172,1024]{2,1,0:T(8,128)(2,1)} async-done(((bf16[16,172,1024]{2,1,0:T(8,128)(2,1)}), bf16[16,172,1024]{2,1,0:T(8,128)(2,1)}, u32[]{:S(2)}, u32[]{:S(2)}) %all-to-all-start.2) | async-done | bytes 5636128 | tf_op jit(solution)/shard_map/all_to_all | solution.py:252
  642.0 8.6 %fusion.32 = bf16[516,1024]{1,0:T(8,128)(2,1)} fusion(f32[516,1024,1]{1,0,2:T(8,128)} %fusion.15, bf16[516,1024]{1,0:T(8,128)(2,1)S(1)} %copy-done.32, bf16[16,172,1024]{2,1,0:T(8,128)(2,1)} %all-to-all-done.2, bf16[32,172,516]{2,1,0:T(8,128)(2,1)} %copy-done.2, bf16[4,1024]{1,0:T(4,128)(2,1)S(1)} %convolution_convert_fusion.3, ...), kind=kOutput, calls=%fused_computation.43 | convolution fusion | flops 2912980992 | bytes 14671872 | tf_op jit(solution)/shard_map/ecr,ecd->rd/dot_general | solution.py:254
  (157 shorter events, 73.5 us)
Async XLA Ops:
  6.5 21.1 %collective-permute-start.2 = (bf16[32,2048]{1,0:T(8,128)(2,1)}, bf16[32,2048]{1,0:T(8,128)(2,1)S(1)}, u32[]{:S(2)}, u32[]{:S(2)}) collective-permute-start(bf16[32,2048]{1,0:T(8,128)(2,1)} %param.24), channel_id=1, source_target_pairs={{0,16},{16,0},{1,17},{17,1},{2,18},{18,2},{3,19},{19,3},{4,20},{20... | collective-permute-start | bytes 393224 | tf_op jit(solution)/shard_map/ppermute | solution.py:116
  6.6 167.3 %collective-permute-start.4 = (bf16[1024,32]{0,1:T(8,128)(2,1)}, bf16[1024,32]{0,1:T(8,128)(2,1)}, u32[]{:S(2)}, u32[]{:S(2)}) collective-permute-start(bf16[1024,32]{0,1:T(8,128)(2,1)} %param.25), channel_id=1, source_target_pairs={{0,16},{16,0},{1,17},{17,1},{2,18},{18,2},{3,19},{19,3},{4,20},{20... | collective-permute-start | bytes 196616 | tf_op jit(solution)/shard_map/ppermute | solution.py:116
  8.9 126.4 %collective-permute-start = (bf16[4,1024]{1,0:T(4,128)(2,1)}, bf16[4,1024]{1,0:T(4,128)(2,1)S(1)}, u32[]{:S(2)}, u32[]{:S(2)}) collective-permute-start(bf16[4,1024]{1,0:T(4,128)(2,1)} %param.16), channel_id=1, source_target_pairs={{0,16},{16,0},{1,17},{17,1},{2,18},{18,2},{3,19},{19,3},{4,20},{20... | collective-permute-start | bytes 24584 | tf_op jit(solution)/shard_map/ppermute | solution.py:116
  14.9 250.3 %all-to-all-start.1 = ((bf16[32,2,48,1024]{3,2,1,0:T(8,128)(2,1)}), bf16[32,2,48,1024]{3,2,1,0:T(8,128)(2,1)}, u32[]{:S(2)}, u32[]{:S(2)}) async-start(bf16[32,2,48,1024]{3,2,1,0:T(8,128)(2,1)} %pad_maximum_fusion), calls=%async_computation.1 | async-start | bytes 12582912 | tf_op jit(solution)/shard_map/all_to_all | solution.py:206
  22.2 109.2 %all-gather.6.cloned.1.call-start = ((), (), s32[]{:S(2)}) async-start(), calls=%async_computation.5 | async-start | bytes 2359296 | tf_op jit(solution)/shard_map/all_gather | solution.py:177
  22.3 11.4 %copy-start.18 = (pred[516,32]{0,1:T(8,128)(4,1)}, pred[516,32]{0,1:T(8,128)(4,1)S(1)}, u32[]{:S(2)}) copy-start(pred[516,32]{0,1:T(8,128)(4,1)S(1)} %fusion.64) | copy-start | bytes 49540
  28.4 220.6 %all-gather.8.cloned.1.call-start = ((), (), s32[]{:S(2)}) async-start(), calls=%async_computation.6 | async-start | bytes 1179648 | tf_op jit(solution)/shard_map/all_gather | solution.py:186
  31.4 100.5 %copy-start.1 = (bf16[8,4,256,128]{3,2,1,0:T(8,128)(2,1)S(1)}, bf16[8,4,256,128]{3,2,1,0:T(8,128)(2,1)}, u32[]{:S(2)}) copy-start(bf16[8,4,256,128]{3,2,1,0:T(8,128)(2,1)} %param.20) | copy-start | bytes 6291460
  131.4 45.1 %copy-start.28 = (s32[128]{0:T(128)S(1)}, s32[128]{0:T(128)}, u32[]{:S(2)}) copy-start(s32[128]{0:T(128)} %param.17) | copy-start | bytes 1540
  131.4 46.6 %collective-permute-start.3 = (bf16[8,2,32,2048]{3,2,1,0:T(8,128)(2,1)}, bf16[8,2,32,2048]{3,2,1,0:T(8,128)(2,1)}, u32[]{:S(2)}, u32[]{:S(2)}) collective-permute-start(bf16[8,2,32,2048]{3,2,1,0:T(8,128)(2,1)} %bitcast.183), channel_id=1, source_target_pairs={{0,1},{1,0},{2,3},{3,2},{4,5},{5,4},{6,7},{7,6},{8,9},{9,8},{10,11... | collective-permute-start | bytes 6291464 | tf_op jit(solution)/shard_map/ppermute | solution.py:116
  131.9 45.7 %copy-start.9 = (bf16[512,1024]{1,0:T(8,128)(2,1)S(1)}, bf16[512,1024]{1,0:T(8,128)(2,1)}, u32[]{:S(2)}) copy-start(bf16[512,1024]{1,0:T(8,128)(2,1)} %param.15) | copy-start | bytes 3145732
  134.7 43.2 %copy-start.6 = (bf16[16,32,2048]{2,1,0:T(8,128)(2,1)S(1)}, bf16[16,32,2048]{2,1,0:T(8,128)(2,1)}, u32[]{:S(2)}) copy-start(bf16[16,32,2048]{2,1,0:T(8,128)(2,1)} %all-gather.6.cloned.1.call-done) | copy-start | bytes 6291460
  168.9 6.5 collective-permute-start.1
  202.9 23.7 %copy-start.11 = (bf16[8,1024,64]{1,2,0:T(8,128)(2,1)S(1)}, bf16[8,1024,64]{1,2,0:T(8,128)(2,1)}, u32[]{:S(2)}) copy-start(bf16[8,1024,64]{1,2,0:T(8,128)(2,1)} %get-tuple-element.15) | copy-start | bytes 3145732
  249.1 3.1 collective-permute-start.5
  265.1 98.8 %all-to-all-start.3 = ((bf16[16,172,1024]{2,1,0:T(8,128)(2,1)}), bf16[16,172,1024]{2,1,0:T(8,128)(2,1)}, u32[]{:S(2)}, u32[]{:S(2)}) async-start(bf16[16,172,1024]{2,1,0:T(8,128)(2,1)} %fusion.22), calls=%async_computation.3 | async-start | bytes 11534336 | tf_op jit(solution)/shard_map/all_to_all | solution.py:244
  363.9 92.6 %all-to-all-start = ((bf16[16,172,1024]{2,1,0:T(8,128)(2,1)}), bf16[16,172,1024]{2,1,0:T(8,128)(2,1)}, u32[]{:S(2)}, u32[]{:S(2)}) async-start(bf16[16,172,1024]{2,1,0:T(8,128)(2,1)} %fusion.19), calls=%async_computation | async-start | bytes 11534336 | tf_op jit(solution)/shard_map/all_to_all | solution.py:244
  456.5 92.8 %all-to-all-start.4 = ((bf16[16,172,1024]{2,1,0:T(8,128)(2,1)}), bf16[16,172,1024]{2,1,0:T(8,128)(2,1)}, u32[]{:S(2)}, u32[]{:S(2)}) async-start(bf16[16,172,1024]{2,1,0:T(8,128)(2,1)} %convolution_convert_fusion), calls=%async_computation.4 | async-start | bytes 11534336 | tf_op jit(solution)/shard_map/all_to_all | solution.py:252
  475.3 78.6 %copy-start.23 = (bf16[516,8]{0,1:T(8,128)(2,1)S(1)}, bf16[516,8]{0,1:T(8,128)(2,1)}, u32[]{:S(2)}) copy-start(bf16[516,8]{0,1:T(8,128)(2,1)} %param.29) | copy-start | bytes 24772
  475.3 78.6 %copy-start.22 = (s32[516,8]{0,1:T(8,128)S(1)}, s32[516,8]{0,1:T(8,128)}, u32[]{:S(2)}) copy-start(s32[516,8]{0,1:T(8,128)} %param.28) | copy-start | bytes 49540
  475.3 78.7 %copy-start.15 = (s32[32,516]{1,0:T(8,128)S(1)}, s32[32,516]{1,0:T(8,128)}, u32[]{:S(2)}) copy-start(s32[32,516]{1,0:T(8,128)} %copy-done.14) | copy-start | bytes 198148
  475.3 78.7 %copy-start.19 = (pred[516,32]{0,1:T(8,128)(4,1)S(1)}, pred[516,32]{0,1:T(8,128)(4,1)}, u32[]{:S(2)}) copy-start(pred[516,32]{0,1:T(8,128)(4,1)} %copy-done.18) | copy-start | bytes 49540
  549.3 92.7 %all-to-all-start.2 = ((bf16[16,172,1024]{2,1,0:T(8,128)(2,1)}), bf16[16,172,1024]{2,1,0:T(8,128)(2,1)}, u32[]{:S(2)}, u32[]{:S(2)}) async-start(bf16[16,172,1024]{2,1,0:T(8,128)(2,1)} %convolution_convert_fusion.1), calls=%async_computation.2 | async-start | bytes 11534336 | tf_op jit(solution)/shard_map/all_to_all | solution.py:252
  562.4 79.6 %copy-start.32 = (bf16[516,1024]{1,0:T(8,128)(2,1)S(1)}, bf16[516,1024]{1,0:T(8,128)(2,1)}, u32[]{:S(2)}) copy-start(bf16[516,1024]{1,0:T(8,128)(2,1)} %copy-done.30) | copy-start | bytes 3170308
  (22 other events, 74.2 us)
Sparse Core Ops, SparseCore 0:
  28.6 102.7 all-gather.5
  202.2 35.9 all-gather.7

commit v9 on v4

--- a/solution.py
+++ b/solution.py
@@ -116,6 +116,18 @@
     other = lax.ppermute(shard, "zh", [(0, 1), (1, 0)])
     first = lax.axis_index("zh") == 0
     return jnp.stack([jnp.where(first, shard, other), jnp.where(first, other, shard)])
+
+
+def exchange(blocks, axis):
+    size = blocks.shape[0]
+    me = lax.axis_index(axis)
+    arrived = [lax.dynamic_index_in_dim(blocks, me, 0, keepdims=False)]
+    for shift in range(1, size):
+        sent = lax.dynamic_index_in_dim(blocks, (me + shift) % size, 0, keepdims=False)
+        pairs = [(i, (i + shift) % size) for i in range(size)]
+        arrived.append(lax.ppermute(sent, axis, pairs))
+    order = (me - jnp.arange(size, dtype=jnp.int32)) % size
+    return jnp.take(jnp.stack(arrived), order, axis=0)
 
 
 def local(
@@ -249,7 +261,7 @@
             "ecr,rd->ecd", table, normed_moe, preferred_element_type=jnp.float32
         ).astype(jnp.bfloat16)
         outbound = outbound.reshape(half_size, -1, width)
-        arrived = lax.all_to_all(outbound, "dl", split_axis=0, concat_axis=0, tiled=True)
+        arrived = exchange(outbound, "dl")
         both = jnp.einsum(
             "snd,df->snf", arrived, full_gu[l], preferred_element_type=jnp.float32
         )
@@ -257,7 +269,7 @@
         expert_out = jnp.einsum(
             "snf,fd->snd", activation, full_dn[l], preferred_element_type=jnp.float32
         ).astype(jnp.bfloat16)
-        returned = lax.all_to_all(expert_out, "dl", split_axis=0, concat_axis=0, tiled=True)
+        returned = exchange(expert_out, "dl")
         returned = returned.reshape(-1, capacity, width)
         moe_sum = moe_sum + jnp.einsum(
             "ecr,ecd->rd", combine_table[picked], returned, preferred_element_type=jnp.float32

time: 593 us -> 632 us (1.066)
  waiting for transfers between devices: 352 us -> 233 us
  local copies, waits for them, and re-layouts: 42.6 us -> 135 us
  starting transfers between devices: 37 us -> 108 us
  matrix products: 110 us -> 103 us
    all_to_all x4 -> x0, waiting for transfers between devices: 294 us -> none  [the longest x2 148 us: local(): lax.all_to_all(outbound, 'dl', split_axis=0, concat_axis=0, tiled=True)]
    ppermute x0 -> x60, waiting for transfers between devices: none -> 189 us  [exchange(): arrived.append(lax.ppermute(sent, axis, pairs))]
    ppermute x0 -> x60, starting transfers between devices: none -> 91 us  [exchange(): arrived.append(lax.ppermute(sent, axis, pairs))]
    unnamed x59 -> x163, local copies, waits for them, and re-layouts: 15.9 us -> 70.2 us
    gather x0 -> x4, local copies, waits for them, and re-layouts: none -> 24.2 us  [exchange(): return jnp.take(jnp.stack(arrived), order, axis=0)]
    all_to_all x4 -> x0, starting transfers between devices: 20.4 us -> none  [the longest x2 11.2 us: local(): lax.all_to_all(outbound, 'dl', split_axis=0, concat_axis=0, tiled=True)]
    all_to_all x1, waiting for transfers between devices: 44 us -> 33 us  [local(): lax.all_to_all(jnp.concatenate([owner_major(gate_up), owner_major(down_we...]
    squeeze x0 -> x4, local copies, waits for them, and re-layouts: none -> 9.05 us  [exchange(): lax.dynamic_index_in_dim(blocks, (me + shift) % size, 0, keepdims=False)]
  transfers between devices with their start and end apart: 10 -> 66, of which waited for: 7 -> 33; matrix products, arithmetic and copies ran while one was open for 28% -> 39% of each run, Pallas kernels for 0% -> 0%
where the time goes in v9:
time: 632 us; the launch traced here: 627 us
  waiting for transfers between devices  233 us (37%)
  local copies, waits for them, and re-layouts  135 us (21%)
  starting transfers between devices  108 us (17%)
  matrix products  103 us (16%)
  other arithmetic  33 us (5%)
  between operations  15.3 us (2%)
    ppermute x60, waiting for transfers between devices, exchange(): arrived.append(lax.ppermute(sent, axis, pairs))  189 us
    ppermute x60, starting transfers between devices, exchange(): arrived.append(lax.ppermute(sent, axis, pairs))  91 us
    unnamed x163, local copies, waits for them, and re-layouts  70.2 us
    all_to_all x1, waiting for transfers between devices, local(): lax.all_to_all(jnp.concatenate([owner_major(gate_up), owner_major(down_we...  33 us
    gather x4, local copies, waits for them, and re-layouts, exchange(): return jnp.take(jnp.stack(arrived), order, axis=0)  24.2 us
    sub x1, matrix products, prefill_attention(): expo = jnp.exp(scores - highest)  24.1 us
    dot_general x1, matrix products, prefill_attention(): jnp.einsum('gpck,gkh->cgph', weights, all_values, preferred_element_type=...  18.5 us
    dot_general x2, matrix products, local(): jnp.einsum('snd,df->snf', arrived, full_gu[l], preferred_element_type=jnp...  18 us
  transfers between devices with their start and end apart: 66, of which 33 were waited for; matrix products, arithmetic and copies ran while one was open for 39% of the time, Pallas kernels for 0%

profile of v9, /device:TPU:23, one launch (start us, length us, event | category | flops | bytes accessed | tf_op | source)
XLA Modules:
  0.0 627.0 jit_solution(588677806804192392)
XLA Ops:
  16.6 9.7 %all-to-all-start = ((bf16[32,2,512]{2,1,0:T(2,128)(2,1)}), bf16[32,2,512]{2,1,0:T(2,128)(2,1)S(1)}, u32[]{:S(2)}, u32[]{:S(2)}) async-start(bf16[32,2,512]{2,1,0:T(2,128)(2,1)} %reshape.543), calls=%async_computation | async-start | bytes 131072 | tf_op jit(solution)/shard_map/all_to_all | solution.py:175
  50.2 8.2 %select_convert_fusion = bf16[32,172,516]{2,1,0:T(8,128)(2,1)} fusion(bf16[32,516]{1,0:T(8,128)(2,1)S(1)} %bitcast.412, s32[32,516]{1,0:T(8,128)S(1)} %fusion.81, pred[32,516]{1,0:T(8,128)(4,1)S(1)} %bitcast.409), kind=kLoop, calls=%fused_computation.13 | loop fusion | flops 8520192 | bytes 5795712 | tf_op jit(solution)/shard_map/convert_element_type | solution.py:251
  103.2 24.1 %fusion.114 = (f32[8,2,512]{2,1,0:T(2,128)S(1)}, f32[8,2,512,1536]{2,3,1,0:T(8,128)}) fusion(pred[512,1536]{0,1:T(8,128)(4,1)} %fusion.35, bf16[8,512,64]{1,2,0:T(8,128)(2,1)} %maximum_bitcast_fusion.13, bf16[8,1024,64]{1,2,0:T(8,128)(2,1)} %get-tuple-element.79, bf16[512,8,2,32]{0,3,2,1:T(8,128)(2,1)} %get-tuple-element.77, ...), kind=kOutput, calls=%fused_computation.313 | convolution fusion | flops 1666188800 | bytes 53772288 | tf_op jit(solution)/shard_map/sub | solution.py:60
  127.3 18.5 %fusion.57 = bf16[8,64,2,512]{3,1,2,0:T(8,128)(2,1)} fusion(f32[8,2,512,1536]{2,3,1,0:T(8,128)} %get-tuple-element.99, f32[8,2,512]{2,1,0:T(2,128)S(1)} %get-tuple-element.98, bf16[8,512,64]{1,2,0:T(8,128)(2,1)S(1)} %copy-done.9, bf16[8,1024,64]{1,2,0:T(8,128)(2,1)S(1)} %copy-done.8), kind=kOutput, calls=%fused_computation.75 | convolution fusion | flops 1639448576 | bytes 52985856 | tf_op jit(solution)/shard_map/gpck,gkh->cgph/dot_general | solution.py:62
  164.3 6.9 %collective-permute-start.32 = (bf16[172,1024]{1,0:T(8,128)(2,1)}, bf16[172,1024]{1,0:T(8,128)(2,1)}, u32[]{:S(2)}, u32[]{:S(2)}) collective-permute-start(bf16[172,1024]{1,0:T(8,128)(2,1)} %get-tuple-element.40), channel_id=1, source_target_pairs={{0,1},{1,2},{2,3},{3,4},{4,5},{5,6},{6,7},{7,8},{8,9},{9,10},{10,1... | collective-permute-start | bytes 1056776 | tf_op jit(solution)/shard_map/ppermute | solution.py:128
  182.8 33.0 %all-to-all-done.1 = bf16[32,2,48,1024]{3,2,1,0:T(8,128)(2,1)} async-done(((bf16[32,2,48,1024]{3,2,1,0:T(8,128)(2,1)}), bf16[32,2,48,1024]{3,2,1,0:T(8,128)(2,1)}, u32[]{:S(2)}, u32[]{:S(2)}) %all-to-all-start.1) | async-done | bytes 6291488 | tf_op jit(solution)/shard_map/all_to_all | solution.py:226
  230.8 11.5 %collective-permute-done.35 = bf16[172,1024]{1,0:T(8,128)(2,1)} collective-permute-done((bf16[172,1024]{1,0:T(8,128)(2,1)}, bf16[172,1024]{1,0:T(8,128)(2,1)}, u32[]{:S(2)}, u32[]{:S(2)}) %collective-permute-start.35) | collective-permute-done | bytes 352288 | tf_op jit(solution)/shard_map/ppermute | solution.py:128
  258.5 7.0 %collective-permute-done.38 = bf16[172,1024]{1,0:T(8,128)(2,1)S(1)} collective-permute-done((bf16[172,1024]{1,0:T(8,128)(2,1)S(1)}, bf16[172,1024]{1,0:T(8,128)(2,1)S(1)}, u32[]{:S(2)}, u32[]{:S(2)}) %collective-permute-start.38) | collective-permute-done | bytes 352288 | tf_op jit(solution)/shard_map/ppermute | solution.py:128
  266.2 7.0 %collective-permute-done.39 = bf16[172,1024]{1,0:T(8,128)(2,1)S(1)} collective-permute-done((bf16[172,1024]{1,0:T(8,128)(2,1)S(1)}, bf16[172,1024]{1,0:T(8,128)(2,1)S(1)}, u32[]{:S(2)}, u32[]{:S(2)}) %collective-permute-start.39) | collective-permute-done | bytes 352288 | tf_op jit(solution)/shard_map/ppermute | solution.py:128
  284.3 12.5 %collective-permute-start.3 = (bf16[172,1024]{1,0:T(8,128)(2,1)}, bf16[172,1024]{1,0:T(8,128)(2,1)}, u32[]{:S(2)}, u32[]{:S(2)}) collective-permute-start(bf16[172,1024]{1,0:T(8,128)(2,1)} %get-tuple-element.71), channel_id=1, source_target_pairs={{0,2},{1,3},{2,4},{3,5},{4,6},{5,7},{6,8},{7,9},{8,10},{9,11},{10,... | collective-permute-start | bytes 1056776 | tf_op jit(solution)/shard_map/ppermute | solution.py:128
  310.8 9.1 %fusion.17 = f32[16,172,1024]{2,1,0:T(8,128)S(1)} fusion(bf16[16,172,1024]{2,1,0:T(8,128)(2,1)} %gather_fusion.2, pred[16]{0:T(512)(128)(4,1)S(1)} %copy-done.45, bf16[1,2,1024,1024]{3,2,1,0:T(8,128)(2,1)} %bitcast.399), kind=kOutput, calls=%fused_computation.28 | convolution fusion | flops 5774180352 | bytes 19136528 | tf_op jit(solution)/shard_map/snd,df->snf/dot_general | solution.py:265
  374.2 12.3 %collective-permute-done.13 = bf16[172,1024]{1,0:T(8,128)(2,1)S(1)} collective-permute-done((bf16[172,1024]{1,0:T(8,128)(2,1)S(1)}, bf16[172,1024]{1,0:T(8,128)(2,1)S(1)}, u32[]{:S(2)}, u32[]{:S(2)}) %collective-permute-start.13) | collective-permute-done | bytes 352288 | tf_op jit(solution)/shard_map/ppermute | solution.py:128
  388.2 6.3 collective-permute-done.14
  395.2 9.0 %collective-permute-done.15 = bf16[172,1024]{1,0:T(8,128)(2,1)S(1)} collective-permute-done((bf16[172,1024]{1,0:T(8,128)(2,1)S(1)}, bf16[172,1024]{1,0:T(8,128)(2,1)S(1)}, u32[]{:S(2)}, u32[]{:S(2)}) %collective-permute-start.15) | collective-permute-done | bytes 352288 | tf_op jit(solution)/shard_map/ppermute | solution.py:128
  413.9 8.9 %fusion.21 = f32[16,172,1024]{2,1,0:T(8,128)S(1)} fusion(bf16[16,172,1024]{2,1,0:T(8,128)(2,1)} %gather_fusion, pred[16]{0:T(512)(128)(4,1)S(1)} %copy-done.45, bf16[1,2,1024,1024]{3,2,1,0:T(8,128)(2,1)} %bitcast.400), kind=kOutput, calls=%fused_computation.32 | convolution fusion | flops 5774180352 | bytes 19136528 | tf_op jit(solution)/shard_map/snd,df->snf/dot_general | solution.py:265
  458.2 6.7 %collective-permute-start.60 = (bf16[172,1024]{1,0:T(8,128)(2,1)S(1)}, bf16[172,1024]{1,0:T(8,128)(2,1)S(1)}, u32[]{:S(2)}, u32[]{:S(2)}) collective-permute-start(bf16[172,1024]{1,0:T(8,128)(2,1)S(1)} %get-tuple-element.11), channel_id=1, source_target_pairs={{0,14},{1,15},{2,0},{3,1},{4,2},{5,3},{6,4},{7,5},{8,6},{9,7},{10,... | collective-permute-start | bytes 1056776 | tf_op jit(solution)/shard_map/ppermute | solution.py:128
  474.6 9.5 %collective-permute-done.58 = bf16[172,1024]{1,0:T(8,128)(2,1)S(1)} collective-permute-done((bf16[172,1024]{1,0:T(8,128)(2,1)S(1)}, bf16[172,1024]{1,0:T(8,128)(2,1)S(1)}, u32[]{:S(2)}, u32[]{:S(2)}) %collective-permute-start.58) | collective-permute-done | bytes 352288 | tf_op jit(solution)/shard_map/ppermute | solution.py:128
  484.9 8.7 %collective-permute-done.59 = bf16[172,1024]{1,0:T(8,128)(2,1)S(1)} collective-permute-done((bf16[172,1024]{1,0:T(8,128)(2,1)S(1)}, bf16[172,1024]{1,0:T(8,128)(2,1)S(1)}, u32[]{:S(2)}, u32[]{:S(2)}) %collective-permute-start.59) | collective-permute-done | bytes 352288 | tf_op jit(solution)/shard_map/ppermute | solution.py:128
  494.4 6.3 %collective-permute-done.60 = bf16[172,1024]{1,0:T(8,128)(2,1)S(1)} collective-permute-done((bf16[172,1024]{1,0:T(8,128)(2,1)S(1)}, bf16[172,1024]{1,0:T(8,128)(2,1)S(1)}, u32[]{:S(2)}, u32[]{:S(2)}) %collective-permute-start.60) | collective-permute-done | bytes 352288 | tf_op jit(solution)/shard_map/ppermute | solution.py:128
  512.3 23.2 %collective-permute-done.20 = bf16[172,1024]{1,0:T(8,128)(2,1)S(1)} collective-permute-done((bf16[172,1024]{1,0:T(8,128)(2,1)S(1)}, bf16[172,1024]{1,0:T(8,128)(2,1)S(1)}, u32[]{:S(2)}, u32[]{:S(2)}) %collective-permute-start.20) | collective-permute-done | bytes 352288 | tf_op jit(solution)/shard_map/ppermute | solution.py:128
  550.3 9.7 %collective-permute-done.26 = bf16[172,1024]{1,0:T(8,128)(2,1)S(1)} collective-permute-done((bf16[172,1024]{1,0:T(8,128)(2,1)S(1)}, bf16[172,1024]{1,0:T(8,128)(2,1)S(1)}, u32[]{:S(2)}, u32[]{:S(2)}) %collective-permute-start.26) | collective-permute-done | bytes 352288 | tf_op jit(solution)/shard_map/ppermute | solution.py:128
  563.3 22.6 %collective-permute-done.28 = bf16[172,1024]{1,0:T(8,128)(2,1)S(1)} collective-permute-done((bf16[172,1024]{1,0:T(8,128)(2,1)S(1)}, bf16[172,1024]{1,0:T(8,128)(2,1)S(1)}, u32[]{:S(2)}, u32[]{:S(2)}) %collective-permute-start.28) | collective-permute-done | bytes 352288 | tf_op jit(solution)/shard_map/ppermute | solution.py:128
  606.2 6.6 %fusion.19 = f32[516,1024,1]{1,0,2:T(8,128)S(1)} fusion(bf16[16,172,1024]{2,1,0:T(8,128)(2,1)} %gather_fusion.1, pred[16]{0:T(512)(128)(4,1)S(1)} %copy-done.45, bf16[32,172,516]{2,1,0:T(8,128)(2,1)} %select_convert_fusion), kind=kOutput, calls=%fused_computation.30 | convolution fusion | flops 2911043584 | bytes 11485200 | tf_op jit(solution)/shard_map/ecr,ecd->rd/dot_general | solution.py:274
  612.9 7.1 %fusion.46 = bf16[516,1024]{1,0:T(8,128)(2,1)} fusion(f32[516,1024,1]{1,0,2:T(8,128)S(1)} %fusion.19, bf16[516,1024]{1,0:T(8,128)(2,1)S(1)} %copy-done.48, bf16[16,172,1024]{2,1,0:T(8,128)(2,1)} %gather_fusion.3, pred[16]{0:T(512)(128)(4,1)S(1)} %copy-done.46, bf16[32,172,516]{2,1,0:T(8,128)(2,1)S(1)} %bitcast.396, ...), kind=kOutput, calls=%fused_computation.60 | convolution fusion | flops 2915799040 | bytes 14549504 | tf_op jit(solution)/shard_map/ecr,ecd->rd/dot_general | solution.py:274
  (368 shorter events, 327.4 us)
Async XLA Ops:
  6.5 65.0 %all-gather.5.cloned.1.call-start = ((), (), s32[]{:S(2)}) async-start(), calls=%async_computation.2 | async-start | bytes 4456448 | tf_op jit(solution)/shard_map/all_gather | solution.py:197
  16.6 47.9 %all-to-all-start = ((bf16[32,2,512]{2,1,0:T(2,128)(2,1)}), bf16[32,2,512]{2,1,0:T(2,128)(2,1)S(1)}, u32[]{:S(2)}, u32[]{:S(2)}) async-start(bf16[32,2,512]{2,1,0:T(2,128)(2,1)} %reshape.543), calls=%async_computation | async-start | bytes 131072 | tf_op jit(solution)/shard_map/all_to_all | solution.py:175
  64.5 151.2 %all-to-all-start.1 = ((bf16[32,2,48,1024]{3,2,1,0:T(8,128)(2,1)}), bf16[32,2,48,1024]{3,2,1,0:T(8,128)(2,1)}, u32[]{:S(2)}, u32[]{:S(2)}) async-start(bf16[32,2,48,1024]{3,2,1,0:T(8,128)(2,1)} %pad_maximum_fusion), calls=%async_computation.1 | async-start | bytes 12582912 | tf_op jit(solution)/shard_map/all_to_all | solution.py:226
  70.8 80.4 %all-gather.7.cloned.1.call-start = ((), (), s32[]{:S(2)}) async-start(), calls=%async_computation.3 | async-start | bytes 2228224 | tf_op jit(solution)/shard_map/all_gather | solution.py:206
  164.3 58.6 %collective-permute-start.32 = (bf16[172,1024]{1,0:T(8,128)(2,1)}, bf16[172,1024]{1,0:T(8,128)(2,1)}, u32[]{:S(2)}, u32[]{:S(2)}) collective-permute-start(bf16[172,1024]{1,0:T(8,128)(2,1)} %get-tuple-element.40), channel_id=1, source_target_pairs={{0,1},{1,2},{2,3},{3,4},{4,5},{5,6},{6,7},{7,8},{8,9},{9,10},{10,1... | collective-permute-start | bytes 1056776 | tf_op jit(solution)/shard_map/ppermute | solution.py:128
  171.2 53.7 %collective-permute-start.33 = (bf16[172,1024]{1,0:T(8,128)(2,1)}, bf16[172,1024]{1,0:T(8,128)(2,1)}, u32[]{:S(2)}, u32[]{:S(2)}) collective-permute-start(bf16[172,1024]{1,0:T(8,128)(2,1)} %get-tuple-element.39), channel_id=1, source_target_pairs={{0,2},{1,3},{2,4},{3,5},{4,6},{5,7},{6,8},{7,9},{8,10},{9,11},{10,... | collective-permute-start | bytes 1056776 | tf_op jit(solution)/shard_map/ppermute | solution.py:128
  171.2 55.5 %collective-permute-start.34 = (bf16[172,1024]{1,0:T(8,128)(2,1)}, bf16[172,1024]{1,0:T(8,128)(2,1)}, u32[]{:S(2)}, u32[]{:S(2)}) collective-permute-start(bf16[172,1024]{1,0:T(8,128)(2,1)} %get-tuple-element.38), channel_id=1, source_target_pairs={{0,3},{1,4},{2,5},{3,6},{4,7},{5,8},{6,9},{7,10},{8,11},{9,12},{10... | collective-permute-start | bytes 1056776 | tf_op jit(solution)/shard_map/ppermute | solution.py:128
  174.8 67.5 %collective-permute-start.35 = (bf16[172,1024]{1,0:T(8,128)(2,1)}, bf16[172,1024]{1,0:T(8,128)(2,1)}, u32[]{:S(2)}, u32[]{:S(2)}) collective-permute-start(bf16[172,1024]{1,0:T(8,128)(2,1)} %get-tuple-element.37), channel_id=1, source_target_pairs={{0,4},{1,5},{2,6},{3,7},{4,8},{5,9},{6,10},{7,11},{8,12},{9,13},{1... | collective-permute-start | bytes 1056776 | tf_op jit(solution)/shard_map/ppermute | solution.py:128
  174.8 75.3 %collective-permute-start.36 = (bf16[172,1024]{1,0:T(8,128)(2,1)}, bf16[172,1024]{1,0:T(8,128)(2,1)}, u32[]{:S(2)}, u32[]{:S(2)}) collective-permute-start(bf16[172,1024]{1,0:T(8,128)(2,1)} %get-tuple-element.36), channel_id=1, source_target_pairs={{0,5},{1,6},{2,7},{3,8},{4,9},{5,10},{6,11},{7,12},{8,13},{9,14},{... | collective-permute-start | bytes 1056776 | tf_op jit(solution)/shard_map/ppermute | solution.py:128
  224.9 40.5 %collective-permute-start.38 = (bf16[172,1024]{1,0:T(8,128)(2,1)S(1)}, bf16[172,1024]{1,0:T(8,128)(2,1)S(1)}, u32[]{:S(2)}, u32[]{:S(2)}) collective-permute-start(bf16[172,1024]{1,0:T(8,128)(2,1)S(1)} %copy-done.34), channel_id=1, source_target_pairs={{0,7},{1,8},{2,9},{3,10},{4,11},{5,12},{6,13},{7,14},{8,15},{9,0},... | collective-permute-start | bytes 1056776 | tf_op jit(solution)/shard_map/ppermute | solution.py:128
  226.7 46.4 %collective-permute-start.39 = (bf16[172,1024]{1,0:T(8,128)(2,1)S(1)}, bf16[172,1024]{1,0:T(8,128)(2,1)S(1)}, u32[]{:S(2)}, u32[]{:S(2)}) collective-permute-start(bf16[172,1024]{1,0:T(8,128)(2,1)S(1)} %copy-done.33), channel_id=1, source_target_pairs={{0,8},{1,9},{2,10},{3,11},{4,12},{5,13},{6,14},{7,15},{8,0},{9,1},... | collective-permute-start | bytes 1056776 | tf_op jit(solution)/shard_map/ppermute | solution.py:128
  275.9 50.2 %collective-permute-start.2 = (bf16[172,1024]{1,0:T(8,128)(2,1)}, bf16[172,1024]{1,0:T(8,128)(2,1)}, u32[]{:S(2)}, u32[]{:S(2)}) collective-permute-start(bf16[172,1024]{1,0:T(8,128)(2,1)} %get-tuple-element.72), channel_id=1, source_target_pairs={{0,1},{1,2},{2,3},{3,4},{4,5},{5,6},{6,7},{7,8},{8,9},{9,10},{10,1... | collective-permute-start | bytes 1056776 | tf_op jit(solution)/shard_map/ppermute | solution.py:128
  284.3 43.7 %collective-permute-start.3 = (bf16[172,1024]{1,0:T(8,128)(2,1)}, bf16[172,1024]{1,0:T(8,128)(2,1)}, u32[]{:S(2)}, u32[]{:S(2)}) collective-permute-start(bf16[172,1024]{1,0:T(8,128)(2,1)} %get-tuple-element.71), channel_id=1, source_target_pairs={{0,2},{1,3},{2,4},{3,5},{4,6},{5,7},{6,8},{7,9},{8,10},{9,11},{10,... | collective-permute-start | bytes 1056776 | tf_op jit(solution)/shard_map/ppermute | solution.py:128
  344.8 41.8 %collective-permute-start.13 = (bf16[172,1024]{1,0:T(8,128)(2,1)S(1)}, bf16[172,1024]{1,0:T(8,128)(2,1)S(1)}, u32[]{:S(2)}, u32[]{:S(2)}) collective-permute-start(bf16[172,1024]{1,0:T(8,128)(2,1)S(1)} %copy-done.13), channel_id=1, source_target_pairs={{0,12},{1,13},{2,14},{3,15},{4,0},{5,1},{6,2},{7,3},{8,4},{9,5},{1... | collective-permute-start | bytes 1056776 | tf_op jit(solution)/shard_map/ppermute | solution.py:128
  354.7 39.8 %collective-permute-start.14 = (bf16[172,1024]{1,0:T(8,128)(2,1)S(1)}, bf16[172,1024]{1,0:T(8,128)(2,1)S(1)}, u32[]{:S(2)}, u32[]{:S(2)}) collective-permute-start(bf16[172,1024]{1,0:T(8,128)(2,1)S(1)} %copy-done.11), channel_id=1, source_target_pairs={{0,13},{1,14},{2,15},{3,0},{4,1},{5,2},{6,3},{7,4},{8,5},{9,6},{10... | collective-permute-start | bytes 1056776 | tf_op jit(solution)/shard_map/ppermute | solution.py:128
  357.7 46.5 %collective-permute-start.15 = (bf16[172,1024]{1,0:T(8,128)(2,1)S(1)}, bf16[172,1024]{1,0:T(8,128)(2,1)S(1)}, u32[]{:S(2)}, u32[]{:S(2)}) collective-permute-start(bf16[172,1024]{1,0:T(8,128)(2,1)S(1)} %get-tuple-element.59), channel_id=1, source_target_pairs={{0,14},{1,15},{2,0},{3,1},{4,2},{5,3},{6,4},{7,5},{8,6},{9,7},{10,... | collective-permute-start | bytes 1056776 | tf_op jit(solution)/shard_map/ppermute | solution.py:128
  373.5 54.6 %collective-permute-start.47 = (bf16[172,1024]{1,0:T(8,128)(2,1)}, bf16[172,1024]{1,0:T(8,128)(2,1)}, u32[]{:S(2)}, u32[]{:S(2)}) collective-permute-start(bf16[172,1024]{1,0:T(8,128)(2,1)} %get-tuple-element.24), channel_id=1, source_target_pairs={{0,1},{1,2},{2,3},{3,4},{4,5},{5,6},{6,7},{7,8},{8,9},{9,10},{10,1... | collective-permute-start | bytes 1056776 | tf_op jit(solution)/shard_map/ppermute | solution.py:128
  386.6 43.6 %collective-permute-start.48 = (bf16[172,1024]{1,0:T(8,128)(2,1)}, bf16[172,1024]{1,0:T(8,128)(2,1)}, u32[]{:S(2)}, u32[]{:S(2)}) collective-permute-start(bf16[172,1024]{1,0:T(8,128)(2,1)} %get-tuple-element.23), channel_id=1, source_target_pairs={{0,2},{1,3},{2,4},{3,5},{4,6},{5,7},{6,8},{7,9},{8,10},{9,11},{10,... | collective-permute-start | bytes 1056776 | tf_op jit(solution)/shard_map/ppermute | solution.py:128
  444.4 39.8 %collective-permute-start.58 = (bf16[172,1024]{1,0:T(8,128)(2,1)S(1)}, bf16[172,1024]{1,0:T(8,128)(2,1)S(1)}, u32[]{:S(2)}, u32[]{:S(2)}) collective-permute-start(bf16[172,1024]{1,0:T(8,128)(2,1)S(1)} %copy-done.12), channel_id=1, source_target_pairs={{0,12},{1,13},{2,14},{3,15},{4,0},{5,1},{6,2},{7,3},{8,4},{9,5},{1... | collective-permute-start | bytes 1056776 | tf_op jit(solution)/shard_map/ppermute | solution.py:128
  452.5 41.1 %collective-permute-start.59 = (bf16[172,1024]{1,0:T(8,128)(2,1)S(1)}, bf16[172,1024]{1,0:T(8,128)(2,1)S(1)}, u32[]{:S(2)}, u32[]{:S(2)}) collective-permute-start(bf16[172,1024]{1,0:T(8,128)(2,1)S(1)} %copy-done.10), channel_id=1, source_target_pairs={{0,13},{1,14},{2,15},{3,0},{4,1},{5,2},{6,3},{7,4},{8,5},{9,6},{10... | collective-permute-start | bytes 1056776 | tf_op jit(solution)/shard_map/ppermute | solution.py:128
  458.2 42.5 %collective-permute-start.60 = (bf16[172,1024]{1,0:T(8,128)(2,1)S(1)}, bf16[172,1024]{1,0:T(8,128)(2,1)S(1)}, u32[]{:S(2)}, u32[]{:S(2)}) collective-permute-start(bf16[172,1024]{1,0:T(8,128)(2,1)S(1)} %get-tuple-element.11), channel_id=1, source_target_pairs={{0,14},{1,15},{2,0},{3,1},{4,2},{5,3},{6,4},{7,5},{8,6},{9,7},{10,... | collective-permute-start | bytes 1056776 | tf_op jit(solution)/shard_map/ppermute | solution.py:128
  540.7 45.2 %collective-permute-start.28 = (bf16[172,1024]{1,0:T(8,128)(2,1)S(1)}, bf16[172,1024]{1,0:T(8,128)(2,1)S(1)}, u32[]{:S(2)}, u32[]{:S(2)}) collective-permute-start(bf16[172,1024]{1,0:T(8,128)(2,1)S(1)} %get-tuple-element.45), channel_id=1, source_target_pairs={{0,12},{1,13},{2,14},{3,15},{4,0},{5,1},{6,2},{7,3},{8,4},{9,5},{1... | collective-permute-start | bytes 1056776 | tf_op jit(solution)/shard_map/ppermute | solution.py:128
  545.3 46.4 %collective-permute-start.29 = (bf16[172,1024]{1,0:T(8,128)(2,1)S(1)}, bf16[172,1024]{1,0:T(8,128)(2,1)S(1)}, u32[]{:S(2)}, u32[]{:S(2)}) collective-permute-start(bf16[172,1024]{1,0:T(8,128)(2,1)S(1)} %get-tuple-element.44), channel_id=1, source_target_pairs={{0,13},{1,14},{2,15},{3,0},{4,1},{5,2},{6,3},{7,4},{8,5},{9,6},{10... | collective-permute-start | bytes 1056776 | tf_op jit(solution)/shard_map/ppermute | solution.py:128
  547.1 51.3 %collective-permute-start.30 = (bf16[172,1024]{1,0:T(8,128)(2,1)S(1)}, bf16[172,1024]{1,0:T(8,128)(2,1)S(1)}, u32[]{:S(2)}, u32[]{:S(2)}) collective-permute-start(bf16[172,1024]{1,0:T(8,128)(2,1)S(1)} %get-tuple-element.43), channel_id=1, source_target_pairs={{0,14},{1,15},{2,0},{3,1},{4,2},{5,3},{6,4},{7,5},{8,6},{9,7},{10,... | collective-permute-start | bytes 1056776 | tf_op jit(solution)/shard_map/ppermute | solution.py:128
  (93 other events, 2030.4 us)
Sparse Core Ops, SparseCore 0:
  14.0 39.4 all-gather.4
  99.7 51.4 all-gather.6

commit v10 on v7

--- a/solution.py
+++ b/solution.py
@@ -188,8 +188,8 @@
     local_width = qkv_weight.shape[1]
     qkv_pair = across_halves(qkv_weight)
     out_pair = jnp.moveaxis(across_halves(out_weight), 0, 1)
-    qkv_full = pair_over(lax.all_gather(qkv_pair, "dc", axis=0, tiled=False), "core")
-    qkv_full = jnp.transpose(qkv_full, (2, 1, 0, 3, 4)).reshape(-1, local_width)
+    qkv_full = lax.all_gather(qkv_pair, DL, axis=0, tiled=False)
+    qkv_full = jnp.swapaxes(qkv_full, 0, 1).reshape(-1, local_width)
     qkv_full, out_pair = lax.optimization_barrier((qkv_full, out_pair))
     projected = jnp.dot(group_rows, qkv_full, preferred_element_type=jnp.float32)
     local_groups = dec_cache.shape[0]

time: 618 us -> 596 us (0.964)
  waiting for transfers between devices: 364 us -> 347 us
    all_gather x1, waiting for transfers between devices: 20 us -> 0.02 us  [local(): qkv_full = lax.all_gather(qkv_pair, DL, axis=0, tiled=False)]
  transfers between devices with their start and end apart: 12 -> 11, of which waited for: 9 -> 8; matrix products, arithmetic and copies ran while one was open for 27% -> 28% of each run, Pallas kernels for 0% -> 0%
where the time goes in v10:
time: 596 us; the launch traced here: 586 us
  waiting for transfers between devices  347 us (58%)
  matrix products  109 us (18%)
  local copies, waits for them, and re-layouts  43.4 us (7%)
  starting transfers between devices  43.3 us (7%)
  other arithmetic  28.2 us (5%)
  between operations  14.8 us (2%)
    all_to_all x2, waiting for transfers between devices, local(): lax.all_to_all(outbound, DL, split_axis=0, concat_axis=0, tiled=True)  148 us
    all_to_all x2, waiting for transfers between devices, local(): lax.all_to_all(expert_out, DL, split_axis=0, concat_axis=0, tiled=True)  146 us
    all_to_all x1, waiting for transfers between devices, local(): lax.all_to_all(jnp.concatenate([owner_major(gate_up), owner_major(down_we...  33.2 us
    sub x1, matrix products, prefill_attention(): expo = jnp.exp(scores - highest)  24.1 us
    unnamed x61, local copies, waits for them, and re-layouts  18.9 us
    dot_general x1, matrix products, prefill_attention(): jnp.einsum('gpck,gkh->cgph', weights, all_values, preferred_element_type=...  18.5 us
    dot_general x2, matrix products, local(): jnp.einsum('snd,df->snf', arrived, full_gu[l], preferred_element_type=jnp...  17.2 us
    dot_general x2, matrix products, local(): jnp.einsum('ecr,ecd->rd', combine_table[picked], returned, preferred_elem...  16.1 us
  transfers between devices with their start and end apart: 11, of which 8 were waited for; matrix products, arithmetic and copies ran while one was open for 28% of the time, Pallas kernels for 0%

profile of v10, /device:TPU:23, one launch (start us, length us, event | category | flops | bytes accessed | tf_op | source)
XLA Modules:
  0.0 586.1 jit_solution(14205967225550856117)
XLA Ops:
  6.6 5.4 collective-permute-done
  16.5 9.7 %all-to-all-start = ((bf16[32,2,512]{2,1,0:T(2,128)(2,1)}), bf16[32,2,512]{2,1,0:T(2,128)(2,1)S(1)}, u32[]{:S(2)}, u32[]{:S(2)}) async-start(bf16[32,2,512]{2,1,0:T(2,128)(2,1)} %reshape.494), calls=%async_computation | async-start | bytes 131072 | tf_op jit(solution)/shard_map/all_to_all | solution.py:169
  45.7 4.8 fusion.6
  51.3 6.2 %all-to-all-start.2 = ((bf16[32,2,48,1024]{3,2,1,0:T(8,128)(2,1)}), bf16[32,2,48,1024]{3,2,1,0:T(8,128)(2,1)}, u32[]{:S(2)}, u32[]{:S(2)}) async-start(bf16[32,2,48,1024]{3,2,1,0:T(8,128)(2,1)} %pad_maximum_fusion), calls=%async_computation.2 | async-start | bytes 12582912 | tf_op jit(solution)/shard_map/all_to_all | solution.py:220
  70.3 5.4 copy.103
  83.2 24.1 %fusion.95 = (f32[8,2,512]{2,1,0:T(2,128)S(1)}, f32[8,2,512,1536]{2,3,1,0:T(8,128)}) fusion(pred[512,1536]{0,1:T(8,128)(4,1)} %fusion.25, bf16[8,512,64]{1,2,0:T(8,128)(2,1)} %maximum_bitcast_fusion.14, bf16[8,1024,64]{1,2,0:T(8,128)(2,1)} %get-tuple-element.14, bf16[512,8,2,32]{0,3,2,1:T(8,128)(2,1)} %get-tuple-element.12, ...), kind=kOutput, calls=%fused_computation.165 | convolution fusion | flops 1666188800 | bytes 53772288 | tf_op jit(solution)/shard_map/sub | solution.py:61
  107.3 18.5 %fusion.43 = bf16[8,64,2,512]{3,1,2,0:T(8,128)(2,1)} fusion(f32[8,2,512,1536]{2,3,1,0:T(8,128)} %get-tuple-element.36, f32[8,2,512]{2,1,0:T(2,128)S(1)} %get-tuple-element.35, bf16[8,512,64]{1,2,0:T(8,128)(2,1)} %fusion.66, bf16[8,1024,64]{1,2,0:T(8,128)(2,1)S(1)} %copy-done.11), kind=kOutput, calls=%fused_computation.60 | convolution fusion | flops 1639448576 | bytes 52985856 | tf_op jit(solution)/shard_map/gpck,gkh->cgph/dot_general | solution.py:63
  129.6 12.4 %all-gather.7.cloned.1.call-done = bf16[1024,16,32]{0,2,1:T(8,128)(2,1)} async-done(((bf16[1024,2,32]{0,2,1:T(8,128)(2,1)}), bf16[1024,16,32]{0,2,1:T(8,128)(2,1)}) %all-gather.7.cloned.1.call-update) | async-done | bytes 1048592 | tf_op jit(solution)/shard_map/all_gather | solution.py:200
  152.7 7.2 %fusion.22 = bf16[16,172,1024]{2,1,0:T(8,128)(2,1)} fusion(pred[32,172,516]{2,1,0:T(8,128)(4,1)S(1)} %copy-done.6, bf16[516,1024]{1,0:T(8,128)(2,1)S(1)} %get-tuple-element.38, f32[1024]{0:T(1024)S(1)} %copy-done.21, f32[516]{0:T(1024)S(1)} %add_rsqrt_fusion, bf16[4,1024]{1,0:T(4,128)(2,1)S(1)} %convolution_convert_fusion.4, ...), kind=kOutput, calls=%fused_computation.29 | convolution fusion | flops 2915799040 | bytes 9568256 | tf_op jit(solution)/shard_map/ecr,rd->ecd/dot_general | solution.py:254
  159.9 33.2 %all-to-all-done.2 = bf16[32,2,48,1024]{3,2,1,0:T(8,128)(2,1)} async-done(((bf16[32,2,48,1024]{3,2,1,0:T(8,128)(2,1)}), bf16[32,2,48,1024]{3,2,1,0:T(8,128)(2,1)}, u32[]{:S(2)}, u32[]{:S(2)}) %all-to-all-start.2) | async-done | bytes 6291488 | tf_op jit(solution)/shard_map/all_to_all | solution.py:220
  193.1 10.5 %all-to-all-start.4 = ((bf16[16,172,1024]{2,1,0:T(8,128)(2,1)}), bf16[16,172,1024]{2,1,0:T(8,128)(2,1)}, u32[]{:S(2)}, u32[]{:S(2)}) async-start(bf16[16,172,1024]{2,1,0:T(8,128)(2,1)} %fusion.22), calls=%async_computation.4 | async-start | bytes 11534336 | tf_op jit(solution)/shard_map/all_to_all | solution.py:258
  203.6 8.2 %fusion.19 = bf16[16,172,1024]{2,1,0:T(8,128)(2,1)} fusion(pred[32,172,516]{2,1,0:T(8,128)(4,1)} %fusion.6, bf16[516,1024]{1,0:T(8,128)(2,1)S(1)} %copy-done.26, f32[1024]{0:T(1024)S(1)} %copy-done.21, f32[516]{0:T(1024)S(1)} %add_rsqrt_fusion, bf16[4,1024]{1,0:T(4,128)(2,1)S(1)} %convolution_convert_fusion.4, bf16[512,1024]{1,0:T(8,128)(2,1)S(1)} %copy-done.10), kind=kOutput, calls=%fused_computation.28 | convolution fusion | flops 2915799040 | bytes 9558032 | tf_op jit(solution)/shard_map/ecr,rd->ecd/dot_general | solution.py:254
  211.8 80.5 %all-to-all-done.4 = bf16[16,172,1024]{2,1,0:T(8,128)(2,1)} async-done(((bf16[16,172,1024]{2,1,0:T(8,128)(2,1)}), bf16[16,172,1024]{2,1,0:T(8,128)(2,1)}, u32[]{:S(2)}, u32[]{:S(2)}) %all-to-all-start.4) | async-done | bytes 5636128 | tf_op jit(solution)/shard_map/all_to_all | solution.py:258
  303.8 8.3 %fusion.33 = f32[16,172,1024]{2,1,0:T(8,128)S(1)} fusion(bf16[16,172,1024]{2,1,0:T(8,128)(2,1)} %all-to-all-done.4, bf16[1,2,1024,1024]{3,2,1,0:T(8,128)(2,1)S(1)} %bitcast.165), kind=kOutput, calls=%fused_computation.46 | convolution fusion | flops 5771362304 | bytes 19005440 | tf_op jit(solution)/shard_map/snd,df->snf/dot_general | solution.py:259
  312.1 5.1 convolution_convert_fusion
  317.2 67.7 %all-to-all-done.1 = bf16[16,172,1024]{2,1,0:T(8,128)(2,1)} async-done(((bf16[16,172,1024]{2,1,0:T(8,128)(2,1)}), bf16[16,172,1024]{2,1,0:T(8,128)(2,1)}, u32[]{:S(2)}, u32[]{:S(2)}) %all-to-all-start.1) | async-done | bytes 5636128 | tf_op jit(solution)/shard_map/all_to_all | solution.py:258
  384.9 4.7 all-to-all-start.5
  389.6 8.9 %fusion.34 = f32[16,172,1024]{2,1,0:T(8,128)S(1)} fusion(bf16[16,172,1024]{2,1,0:T(8,128)(2,1)} %all-to-all-done.1, bf16[1,2,1024,1024]{3,2,1,0:T(8,128)(2,1)} %bitcast.166), kind=kOutput, calls=%fused_computation.49 | convolution fusion | flops 5771362304 | bytes 19136512 | tf_op jit(solution)/shard_map/snd,df->snf/dot_general | solution.py:259
  398.5 5.2 convolution_convert_fusion.1
  403.7 74.1 %all-to-all-done.5 = bf16[16,172,1024]{2,1,0:T(8,128)(2,1)} async-done(((bf16[16,172,1024]{2,1,0:T(8,128)(2,1)}), bf16[16,172,1024]{2,1,0:T(8,128)(2,1)}, u32[]{:S(2)}, u32[]{:S(2)}) %all-to-all-start.5) | async-done | bytes 5636128 | tf_op jit(solution)/shard_map/all_to_all | solution.py:266
  482.4 5.5 select_convert_fusion
  490.9 7.4 %fusion.15 = f32[516,1024,1]{1,0,2:T(8,128)} fusion(bf16[16,172,1024]{2,1,0:T(8,128)(2,1)} %all-to-all-done.5, bf16[32,172,516]{2,1,0:T(8,128)(2,1)S(1)} %select_convert_fusion), kind=kOutput, calls=%fused_computation.24 | convolution fusion | flops 2908225536 | bytes 11354112 | tf_op jit(solution)/shard_map/ecr,ecd->rd/dot_general | solution.py:268
  498.3 72.1 %all-to-all-done.3 = bf16[16,172,1024]{2,1,0:T(8,128)(2,1)} async-done(((bf16[16,172,1024]{2,1,0:T(8,128)(2,1)}), bf16[16,172,1024]{2,1,0:T(8,128)(2,1)}, u32[]{:S(2)}, u32[]{:S(2)}) %all-to-all-start.3) | async-done | bytes 5636128 | tf_op jit(solution)/shard_map/all_to_all | solution.py:266
  570.4 8.7 %fusion.32 = bf16[516,1024]{1,0:T(8,128)(2,1)} fusion(f32[516,1024,1]{1,0,2:T(8,128)} %fusion.15, bf16[516,1024]{1,0:T(8,128)(2,1)S(1)} %copy-done.27, bf16[16,172,1024]{2,1,0:T(8,128)(2,1)} %all-to-all-done.3, bf16[32,172,516]{2,1,0:T(8,128)(2,1)} %copy-done.4, bf16[4,1024]{1,0:T(4,128)(2,1)S(1)} %convolution_convert_fusion.4, ...), kind=kOutput, calls=%fused_computation.42 | convolution fusion | flops 2912980992 | bytes 14671872 | tf_op jit(solution)/shard_map/ecr,ecd->rd/dot_general | solution.py:268
  (142 shorter events, 77.4 us)
Async XLA Ops:
  6.5 52.1 %all-gather.5.cloned.1.call-start = ((), (), s32[]{:S(2)}) async-start(), calls=%async_computation.6 | async-start | bytes 4456448 | tf_op jit(solution)/shard_map/all_gather | solution.py:191
  6.5 5.5 collective-permute-start
  6.6 23.5 %copy-start.23 = (s32[4]{0:T(128)S(1)}, s32[4]{0:T(128)}, u32[]{:S(2)}) copy-start(s32[4]{0:T(128)} %param.18) | copy-start | bytes 52
  6.6 23.5 %copy-start.16 = (s32[516,8]{0,1:T(8,128)S(1)}, s32[516,8]{0,1:T(8,128)}, u32[]{:S(2)}) copy-start(s32[516,8]{0,1:T(8,128)} %param.28) | copy-start | bytes 49540
  13.0 19.0 %copy-start.22 = (s32[128]{0:T(128)S(1)}, s32[128]{0:T(128)}, u32[]{:S(2)}) copy-start(s32[128]{0:T(128)} %param.17) | copy-start | bytes 1540
  16.5 34.8 %all-to-all-start = ((bf16[32,2,512]{2,1,0:T(2,128)(2,1)}), bf16[32,2,512]{2,1,0:T(2,128)(2,1)S(1)}, u32[]{:S(2)}, u32[]{:S(2)}) async-start(bf16[32,2,512]{2,1,0:T(2,128)(2,1)} %reshape.494), calls=%async_computation | async-start | bytes 131072 | tf_op jit(solution)/shard_map/all_to_all | solution.py:169
  26.2 24.4 %collective-permute-start.1 = (bf16[1024,32]{0,1:T(8,128)(2,1)}, bf16[1024,32]{0,1:T(8,128)(2,1)S(1)}, u32[]{:S(2)}, u32[]{:S(2)}) collective-permute-start(bf16[1024,32]{0,1:T(8,128)(2,1)} %param.25), channel_id=1, source_target_pairs={{0,16},{16,0},{1,17},{17,1},{2,18},{18,2},{3,19},{19,3},{4,20},{20... | collective-permute-start | bytes 196616 | tf_op jit(solution)/shard_map/ppermute | solution.py:116
  30.2 15.6 %copy-start.14 = (pred[516,32]{0,1:T(8,128)(4,1)}, pred[516,32]{0,1:T(8,128)(4,1)S(1)}, u32[]{:S(2)}) copy-start(pred[516,32]{0,1:T(8,128)(4,1)S(1)} %fusion.65) | copy-start | bytes 49540
  32.8 12.9 %copy-start.12 = (s32[32,516]{1,0:T(8,128)}, s32[32,516]{1,0:T(8,128)S(1)}, u32[]{:S(2)}) copy-start(s32[32,516]{1,0:T(8,128)S(1)} %fusion.67) | copy-start | bytes 198148
  51.3 141.8 %all-to-all-start.2 = ((bf16[32,2,48,1024]{3,2,1,0:T(8,128)(2,1)}), bf16[32,2,48,1024]{3,2,1,0:T(8,128)(2,1)}, u32[]{:S(2)}, u32[]{:S(2)}) async-start(bf16[32,2,48,1024]{3,2,1,0:T(8,128)(2,1)} %pad_maximum_fusion), calls=%async_computation.2 | async-start | bytes 12582912 | tf_op jit(solution)/shard_map/all_to_all | solution.py:220
  57.5 84.4 %all-gather.7.cloned.1.call-start = ((), (), s32[]{:S(2)}) async-start(), calls=%async_computation.7 | async-start | bytes 1179648 | tf_op jit(solution)/shard_map/all_gather | solution.py:200
  83.2 24.1 %copy-start.11 = (bf16[8,1024,64]{1,2,0:T(8,128)(2,1)S(1)}, bf16[8,1024,64]{1,2,0:T(8,128)(2,1)}, u32[]{:S(2)}) copy-start(bf16[8,1024,64]{1,2,0:T(8,128)(2,1)} %get-tuple-element.13) | copy-start | bytes 3145732
  141.9 4.9 collective-permute-start.2
  159.9 43.7 %copy-start.26 = (bf16[516,1024]{1,0:T(8,128)(2,1)S(1)}, bf16[516,1024]{1,0:T(8,128)(2,1)}, u32[]{:S(2)}) copy-start(bf16[516,1024]{1,0:T(8,128)(2,1)} %copy-done.25) | copy-start | bytes 3170308
  193.1 99.2 %all-to-all-start.4 = ((bf16[16,172,1024]{2,1,0:T(8,128)(2,1)}), bf16[16,172,1024]{2,1,0:T(8,128)(2,1)}, u32[]{:S(2)}, u32[]{:S(2)}) async-start(bf16[16,172,1024]{2,1,0:T(8,128)(2,1)} %fusion.22), calls=%async_computation.4 | async-start | bytes 11534336 | tf_op jit(solution)/shard_map/all_to_all | solution.py:258
  292.3 92.6 %all-to-all-start.1 = ((bf16[16,172,1024]{2,1,0:T(8,128)(2,1)}), bf16[16,172,1024]{2,1,0:T(8,128)(2,1)}, u32[]{:S(2)}, u32[]{:S(2)}) async-start(bf16[16,172,1024]{2,1,0:T(8,128)(2,1)} %fusion.19), calls=%async_computation.1 | async-start | bytes 11534336 | tf_op jit(solution)/shard_map/all_to_all | solution.py:258
  384.9 92.8 %all-to-all-start.5 = ((bf16[16,172,1024]{2,1,0:T(8,128)(2,1)}), bf16[16,172,1024]{2,1,0:T(8,128)(2,1)}, u32[]{:S(2)}, u32[]{:S(2)}) async-start(bf16[16,172,1024]{2,1,0:T(8,128)(2,1)} %convolution_convert_fusion), calls=%async_computation.5 | async-start | bytes 11534336 | tf_op jit(solution)/shard_map/all_to_all | solution.py:266
  403.7 78.6 %copy-start.19 = (bf16[516,8]{0,1:T(8,128)(2,1)S(1)}, bf16[516,8]{0,1:T(8,128)(2,1)}, u32[]{:S(2)}) copy-start(bf16[516,8]{0,1:T(8,128)(2,1)} %param.29) | copy-start | bytes 24772
  403.7 78.6 %copy-start.17 = (s32[516,8]{0,1:T(8,128)S(1)}, s32[516,8]{0,1:T(8,128)}, u32[]{:S(2)}) copy-start(s32[516,8]{0,1:T(8,128)} %param.28) | copy-start | bytes 49540
  403.7 78.7 %copy-start.13 = (s32[32,516]{1,0:T(8,128)S(1)}, s32[32,516]{1,0:T(8,128)}, u32[]{:S(2)}) copy-start(s32[32,516]{1,0:T(8,128)} %copy-done.12) | copy-start | bytes 198148
  403.7 78.7 %copy-start.15 = (pred[516,32]{0,1:T(8,128)(4,1)S(1)}, pred[516,32]{0,1:T(8,128)(4,1)}, u32[]{:S(2)}) copy-start(pred[516,32]{0,1:T(8,128)(4,1)} %copy-done.14) | copy-start | bytes 49540
  477.7 92.7 %all-to-all-start.3 = ((bf16[16,172,1024]{2,1,0:T(8,128)(2,1)}), bf16[16,172,1024]{2,1,0:T(8,128)(2,1)}, u32[]{:S(2)}, u32[]{:S(2)}) async-start(bf16[16,172,1024]{2,1,0:T(8,128)(2,1)} %convolution_convert_fusion.1), calls=%async_computation.3 | async-start | bytes 11534336 | tf_op jit(solution)/shard_map/all_to_all | solution.py:266
  490.9 79.6 %copy-start.27 = (bf16[516,1024]{1,0:T(8,128)(2,1)S(1)}, bf16[516,1024]{1,0:T(8,128)(2,1)}, u32[]{:S(2)}) copy-start(bf16[516,1024]{1,0:T(8,128)(2,1)} %copy-done.25) | copy-start | bytes 3170308
  570.4 8.7 %copy-start.1 = (bf16[4,1024]{1,0:T(4,128)(2,1)S(1)}, bf16[4,1024]{1,0:T(4,128)(2,1)}, u32[]{:S(2)}) copy-start(bf16[4,1024]{1,0:T(4,128)(2,1)} %param.16) | copy-start | bytes 24580
  (15 other events, 51.7 us)
Sparse Core Ops, SparseCore 0:
  13.9 39.5 all-gather.4
  82.5 59.3 all-gather.6

commit v11 on v4

--- a/solution.py
+++ b/solution.py
@@ -175,6 +175,21 @@
     slot_rows = jnp.einsum(
         "ijb,jbd->id", take_table, incoming, preferred_element_type=jnp.float32
     ).astype(jnp.bfloat16)
+    expert_count = gate_up.shape[0]
+    local_experts = max(1, expert_count // half_size)
+    copies = max(1, half_size // expert_count)
+
+    def owner_major(weights):
+        per_half = jnp.repeat(weights, copies, axis=0).reshape(
+            (half_size, local_experts) + weights.shape[1:]
+        )
+        both = jnp.broadcast_to(per_half[None], (halves,) + per_half.shape)
+        return both.reshape((group_count, local_experts) + weights.shape[1:])
+
+    weight_rows = jnp.concatenate([owner_major(gate_up), owner_major(down_weight)], axis=2)
+    slot_rows, weight_rows, routes, prior_cache, dec_cache = lax.optimization_barrier(
+        (slot_rows, weight_rows, routes, prior_cache, dec_cache)
+    )
     layer_input = jnp.concatenate([pre_tokens, slot_rows], axis=0)
     rows_dev = layer_input.shape[0]
     normed = root_norm(layer_input.astype(jnp.float32), attn_gain).astype(jnp.bfloat16)
@@ -199,22 +214,8 @@
     ).astype(jnp.float32)
     residual = layer_input.astype(jnp.float32) + attn_sum
     normed_moe = root_norm(residual, moe_gain).astype(jnp.bfloat16)
-    expert_count = gate_up.shape[0]
-    local_experts = max(1, expert_count // half_size)
-    copies = max(1, half_size // expert_count)
-
-    def owner_major(weights):
-        per_half = jnp.repeat(weights, copies, axis=0).reshape(
-            (half_size, local_experts) + weights.shape[1:]
-        )
-        both = jnp.broadcast_to(per_half[None], (halves,) + per_half.shape)
-        return both.reshape((group_count, local_experts) + weights.shape[1:])
-
     gu_rows = gate_up.shape[1]
-    owned = lax.all_to_all(
-        jnp.concatenate([owner_major(gate_up), owner_major(down_weight)], axis=2),
-        dp, split_axis=0, concat_axis=0, tiled=True,
-    )
+    owned = lax.all_to_all(weight_rows, dp, split_axis=0, concat_axis=0, tiled=True)
     owned_gu = jnp.moveaxis(owned[:, :, :gu_rows], 0, 1).reshape(
         (1, local_experts, -1) + gate_up.shape[2:]
     )

time: 593 us -> 586 us (0.988)
  waiting for transfers between devices: 352 us -> 346 us
    optimization_barrier x0 -> x2, local copies, waits for them, and re-layouts: none -> 6.94 us  [local(): lax.optimization_barrier((slot_rows, weight_rows, routes, prior_cache, de...]
    unnamed x59 -> x52, local copies, waits for them, and re-layouts: 15.9 us -> 12.2 us
  transfers between devices with their start and end apart: 10 -> 10, of which waited for: 7 -> 7; matrix products, arithmetic and copies ran while one was open for 28% -> 29% of each run, Pallas kernels for 0% -> 0%
where the time goes in v11:
time: 586 us; the launch traced here: 579 us
  waiting for transfers between devices  346 us (59%)
  matrix products  110 us (19%)
  local copies, waits for them, and re-layouts  42.8 us (7%)
  starting transfers between devices  36.7 us (6%)
  other arithmetic  28.5 us (5%)
  between operations  14.8 us (3%)
    all_to_all x2, waiting for transfers between devices, local(): lax.all_to_all(outbound, 'dl', split_axis=0, concat_axis=0, tiled=True)  148 us
    all_to_all x2, waiting for transfers between devices, local(): lax.all_to_all(expert_out, 'dl', split_axis=0, concat_axis=0, tiled=True)  146 us
    all_to_all x1, waiting for transfers between devices, local(): lax.all_to_all(weight_rows, dp, split_axis=0, concat_axis=0, tiled=True)  43.2 us
    sub x1, matrix products, prefill_attention(): expo = jnp.exp(scores - highest)  24.2 us
    dot_general x1, matrix products, prefill_attention(): jnp.einsum('gpck,gkh->cgph', weights, all_values, preferred_element_type=...  18.4 us
    dot_general x2, matrix products, local(): jnp.einsum('snd,df->snf', arrived, full_gu[l], preferred_element_type=jnp...  17.2 us
    dot_general x2, matrix products, local(): jnp.einsum('ecr,ecd->rd', combine_table[picked], returned, preferred_elem...  16.1 us
    dot_general x2, matrix products, local(): jnp.einsum('ecr,rd->ecd', table, normed_moe, preferred_element_type=jnp.f...  15.4 us
  transfers between devices with their start and end apart: 10, of which 7 were waited for; matrix products, arithmetic and copies ran while one was open for 29% of the time, Pallas kernels for 0%

profile of v11, /device:TPU:23, one launch (start us, length us, event | category | flops | bytes accessed | tf_op | source)
XLA Modules:
  0.0 578.6 jit_solution(6677935186480384568)
XLA Ops:
  6.6 5.4 collective-permute-done
  16.5 9.7 %all-to-all-start = ((bf16[32,2,512]{2,1,0:T(2,128)(2,1)}), bf16[32,2,512]{2,1,0:T(2,128)(2,1)S(1)}, u32[]{:S(2)}, u32[]{:S(2)}) async-start(bf16[32,2,512]{2,1,0:T(2,128)(2,1)} %reshape.494), calls=%async_computation | async-start | bytes 131072 | tf_op jit(solution)/shard_map/all_to_all | solution.py:163
  47.8 6.1 %all-to-all-start.2 = ((bf16[32,2,48,1024]{3,2,1,0:T(8,128)(2,1)}), bf16[32,2,48,1024]{3,2,1,0:T(8,128)(2,1)}, u32[]{:S(2)}, u32[]{:S(2)}) async-start(bf16[32,2,48,1024]{3,2,1,0:T(8,128)(2,1)} %pad_maximum_fusion), calls=%async_computation.2 | async-start | bytes 12582912 | tf_op jit(solution)/shard_map/all_to_all | solution.py:218
  56.2 4.8 fusion.6
  70.7 5.6 copy.102
  88.9 24.2 %fusion.82 = (f32[8,2,512]{2,1,0:T(2,128)S(1)}, f32[8,2,512,1536]{2,3,1,0:T(8,128)}) fusion(pred[512,1536]{0,1:T(8,128)(4,1)} %fusion.25, bf16[8,512,64]{1,2,0:T(8,128)(2,1)} %maximum_bitcast_fusion.13, bf16[8,1024,64]{1,2,0:T(8,128)(2,1)} %get-tuple-element.24, bf16[512,8,2,32]{0,3,2,1:T(8,128)(2,1)} %get-tuple-element.22, ...), kind=kOutput, calls=%fused_computation.159 | convolution fusion | flops 1666188800 | bytes 53772288 | tf_op jit(solution)/shard_map/sub | solution.py:60
  113.2 18.4 %fusion.39 = bf16[8,64,2,512]{3,1,2,0:T(8,128)(2,1)} fusion(f32[8,2,512,1536]{2,3,1,0:T(8,128)} %get-tuple-element.42, f32[8,2,512]{2,1,0:T(2,128)S(1)} %get-tuple-element.41, bf16[8,512,64]{1,2,0:T(8,128)(2,1)S(1)} %copy-done.10, bf16[8,1024,64]{1,2,0:T(8,128)(2,1)S(1)} %copy-done.7), kind=kOutput, calls=%fused_computation.55 | convolution fusion | flops 1639448576 | bytes 52985856 | tf_op jit(solution)/shard_map/gpck,gkh->cgph/dot_general | solution.py:62
  139.1 7.3 %fusion.22 = bf16[16,172,1024]{2,1,0:T(8,128)(2,1)} fusion(pred[32,172,516]{2,1,0:T(8,128)(4,1)S(1)} %copy-done.4, bf16[516,1024]{1,0:T(8,128)(2,1)S(1)} %get-tuple-element.44, f32[1024]{0:T(1024)S(1)} %copy-done.19, f32[516]{0:T(1024)S(1)} %add_rsqrt_fusion, bf16[4,1024]{1,0:T(4,128)(2,1)S(1)} %convolution_convert_fusion.4, bf16[512,1024]{1,0:T(8,128)(2,1)S(1)} %copy-done.6), kind=kOutput, calls=%fused_computation.29 | convolution fusion | flops 2915799040 | bytes 9568256 | tf_op jit(solution)/shard_map/ecr,rd->ecd/dot_general | solution.py:249
  146.3 43.2 %all-to-all-done.2 = bf16[32,2,48,1024]{3,2,1,0:T(8,128)(2,1)} async-done(((bf16[32,2,48,1024]{3,2,1,0:T(8,128)(2,1)}), bf16[32,2,48,1024]{3,2,1,0:T(8,128)(2,1)}, u32[]{:S(2)}, u32[]{:S(2)}) %all-to-all-start.2) | async-done | bytes 6291488 | tf_op jit(solution)/shard_map/all_to_all | solution.py:218
  189.5 6.6 %all-to-all-start.4 = ((bf16[16,172,1024]{2,1,0:T(8,128)(2,1)}), bf16[16,172,1024]{2,1,0:T(8,128)(2,1)}, u32[]{:S(2)}, u32[]{:S(2)}) async-start(bf16[16,172,1024]{2,1,0:T(8,128)(2,1)} %fusion.22), calls=%async_computation.4 | async-start | bytes 11534336 | tf_op jit(solution)/shard_map/all_to_all | solution.py:253
  196.1 8.2 %fusion.19 = bf16[16,172,1024]{2,1,0:T(8,128)(2,1)} fusion(pred[32,172,516]{2,1,0:T(8,128)(4,1)} %fusion.6, bf16[516,1024]{1,0:T(8,128)(2,1)S(1)} %copy-done.22, f32[1024]{0:T(1024)S(1)} %copy-done.19, f32[516]{0:T(1024)S(1)} %add_rsqrt_fusion, bf16[4,1024]{1,0:T(4,128)(2,1)S(1)} %convolution_convert_fusion.4, bf16[512,1024]{1,0:T(8,128)(2,1)S(1)} %copy-done.6), kind=kOutput, calls=%fused_computation.28 | convolution fusion | flops 2915799040 | bytes 9558032 | tf_op jit(solution)/shard_map/ecr,rd->ecd/dot_general | solution.py:249
  204.3 80.5 %all-to-all-done.4 = bf16[16,172,1024]{2,1,0:T(8,128)(2,1)} async-done(((bf16[16,172,1024]{2,1,0:T(8,128)(2,1)}), bf16[16,172,1024]{2,1,0:T(8,128)(2,1)}, u32[]{:S(2)}, u32[]{:S(2)}) %all-to-all-start.4) | async-done | bytes 5636128 | tf_op jit(solution)/shard_map/all_to_all | solution.py:253
  296.2 8.3 %fusion.33 = f32[16,172,1024]{2,1,0:T(8,128)S(1)} fusion(bf16[16,172,1024]{2,1,0:T(8,128)(2,1)} %all-to-all-done.4, bf16[1,2,1024,1024]{3,2,1,0:T(8,128)(2,1)S(1)} %bitcast.161), kind=kOutput, calls=%fused_computation.46 | convolution fusion | flops 5771362304 | bytes 19005440 | tf_op jit(solution)/shard_map/snd,df->snf/dot_general | solution.py:254
  304.5 5.1 convolution_convert_fusion
  309.6 67.8 %all-to-all-done.1 = bf16[16,172,1024]{2,1,0:T(8,128)(2,1)} async-done(((bf16[16,172,1024]{2,1,0:T(8,128)(2,1)}), bf16[16,172,1024]{2,1,0:T(8,128)(2,1)}, u32[]{:S(2)}, u32[]{:S(2)}) %all-to-all-start.1) | async-done | bytes 5636128 | tf_op jit(solution)/shard_map/all_to_all | solution.py:253
  377.4 4.7 all-to-all-start.5
  382.1 8.9 %fusion.34 = f32[16,172,1024]{2,1,0:T(8,128)S(1)} fusion(bf16[16,172,1024]{2,1,0:T(8,128)(2,1)} %all-to-all-done.1, bf16[1,2,1024,1024]{3,2,1,0:T(8,128)(2,1)} %bitcast.162), kind=kOutput, calls=%fused_computation.49 | convolution fusion | flops 5771362304 | bytes 19136512 | tf_op jit(solution)/shard_map/snd,df->snf/dot_general | solution.py:254
  391.0 5.2 convolution_convert_fusion.1
  396.2 74.0 %all-to-all-done.5 = bf16[16,172,1024]{2,1,0:T(8,128)(2,1)} async-done(((bf16[16,172,1024]{2,1,0:T(8,128)(2,1)}), bf16[16,172,1024]{2,1,0:T(8,128)(2,1)}, u32[]{:S(2)}, u32[]{:S(2)}) %all-to-all-start.5) | async-done | bytes 5636128 | tf_op jit(solution)/shard_map/all_to_all | solution.py:261
  470.2 4.5 all-to-all-start.3
  474.9 5.5 select_convert_fusion
  483.3 7.4 %fusion.15 = f32[516,1024,1]{1,0,2:T(8,128)} fusion(bf16[16,172,1024]{2,1,0:T(8,128)(2,1)} %all-to-all-done.5, bf16[32,172,516]{2,1,0:T(8,128)(2,1)S(1)} %select_convert_fusion), kind=kOutput, calls=%fused_computation.24 | convolution fusion | flops 2908225536 | bytes 11354112 | tf_op jit(solution)/shard_map/ecr,ecd->rd/dot_general | solution.py:263
  490.7 72.2 %all-to-all-done.3 = bf16[16,172,1024]{2,1,0:T(8,128)(2,1)} async-done(((bf16[16,172,1024]{2,1,0:T(8,128)(2,1)}), bf16[16,172,1024]{2,1,0:T(8,128)(2,1)}, u32[]{:S(2)}, u32[]{:S(2)}) %all-to-all-start.3) | async-done | bytes 5636128 | tf_op jit(solution)/shard_map/all_to_all | solution.py:261
  562.9 8.7 %fusion.32 = bf16[516,1024]{1,0:T(8,128)(2,1)} fusion(f32[516,1024,1]{1,0,2:T(8,128)} %fusion.15, bf16[516,1024]{1,0:T(8,128)(2,1)S(1)} %copy-done.23, bf16[16,172,1024]{2,1,0:T(8,128)(2,1)} %all-to-all-done.3, bf16[32,172,516]{2,1,0:T(8,128)(2,1)} %copy-done.2, bf16[4,1024]{1,0:T(4,128)(2,1)S(1)} %convolution_convert_fusion.4, ...), kind=kOutput, calls=%fused_computation.42 | convolution fusion | flops 2912980992 | bytes 14671872 | tf_op jit(solution)/shard_map/ecr,ecd->rd/dot_general | solution.py:263
  (130 shorter events, 71.6 us)
Async XLA Ops:
  6.5 7.9 %copy-start = (bf16[4,1024]{1,0:T(4,128)(2,1)S(1)}, bf16[4,1024]{1,0:T(4,128)(2,1)}, u32[]{:S(2)}) copy-start(bf16[4,1024]{1,0:T(4,128)(2,1)} %param.16) | copy-start | bytes 24580
  6.5 54.5 %all-gather.5.cloned.1.call-start = ((), (), s32[]{:S(2)}) async-start(), calls=%async_computation.6 | async-start | bytes 4456448 | tf_op jit(solution)/shard_map/all_gather | solution.py:200
  6.5 5.5 collective-permute-start
  16.5 22.3 %all-to-all-start = ((bf16[32,2,512]{2,1,0:T(2,128)(2,1)}), bf16[32,2,512]{2,1,0:T(2,128)(2,1)S(1)}, u32[]{:S(2)}, u32[]{:S(2)}) async-start(bf16[32,2,512]{2,1,0:T(2,128)(2,1)} %reshape.494), calls=%async_computation | async-start | bytes 131072 | tf_op jit(solution)/shard_map/all_to_all | solution.py:163
  26.2 11.9 %collective-permute-start.1 = (bf16[1024,32]{0,1:T(8,128)(2,1)}, bf16[1024,32]{0,1:T(8,128)(2,1)S(1)}, u32[]{:S(2)}, u32[]{:S(2)}) collective-permute-start(bf16[1024,32]{0,1:T(8,128)(2,1)} %param.25), channel_id=1, source_target_pairs={{0,16},{16,0},{1,17},{17,1},{2,18},{18,2},{3,19},{19,3},{4,20},{20... | collective-permute-start | bytes 196616 | tf_op jit(solution)/shard_map/ppermute | solution.py:116
  32.5 5.6 copy-start.16
  46.1 10.2 %copy-start.11 = (pred[516,32]{0,1:T(8,128)(4,1)}, pred[516,32]{0,1:T(8,128)(4,1)S(1)}, u32[]{:S(2)}) copy-start(pred[516,32]{0,1:T(8,128)(4,1)S(1)} %fusion.53) | copy-start | bytes 49540
  47.8 6.4 %copy-start.6 = (bf16[512,1024]{1,0:T(8,128)(2,1)S(1)}, bf16[512,1024]{1,0:T(8,128)(2,1)}, u32[]{:S(2)}) copy-start(bf16[512,1024]{1,0:T(8,128)(2,1)} %param.15) | copy-start | bytes 3145732
  47.8 141.7 %all-to-all-start.2 = ((bf16[32,2,48,1024]{3,2,1,0:T(8,128)(2,1)}), bf16[32,2,48,1024]{3,2,1,0:T(8,128)(2,1)}, u32[]{:S(2)}, u32[]{:S(2)}) async-start(bf16[32,2,48,1024]{3,2,1,0:T(8,128)(2,1)} %pad_maximum_fusion), calls=%async_computation.2 | async-start | bytes 12582912 | tf_op jit(solution)/shard_map/all_to_all | solution.py:218
  53.9 80.6 %all-gather.7.cloned.1.call-start = ((), (), s32[]{:S(2)}) async-start(), calls=%async_computation.7 | async-start | bytes 2228224 | tf_op jit(solution)/shard_map/all_gather | solution.py:209
  88.9 24.2 %copy-start.7 = (bf16[8,1024,64]{1,2,0:T(8,128)(2,1)S(1)}, bf16[8,1024,64]{1,2,0:T(8,128)(2,1)}, u32[]{:S(2)}) copy-start(bf16[8,1024,64]{1,2,0:T(8,128)(2,1)} %get-tuple-element.23) | copy-start | bytes 3145732
  88.9 24.2 %copy-start.10 = (bf16[8,512,64]{1,2,0:T(8,128)(2,1)S(1)}, bf16[8,512,64]{1,2,0:T(8,128)(2,1)}, u32[]{:S(2)}) copy-start(bf16[8,512,64]{1,2,0:T(8,128)(2,1)} %fusion.54) | copy-start | bytes 1572868
  131.6 4.7 copy-start.20
  146.3 49.8 %copy-start.22 = (bf16[516,1024]{1,0:T(8,128)(2,1)S(1)}, bf16[516,1024]{1,0:T(8,128)(2,1)}, u32[]{:S(2)}) copy-start(bf16[516,1024]{1,0:T(8,128)(2,1)} %copy-done.21) | copy-start | bytes 3170308
  189.5 95.2 %all-to-all-start.4 = ((bf16[16,172,1024]{2,1,0:T(8,128)(2,1)}), bf16[16,172,1024]{2,1,0:T(8,128)(2,1)}, u32[]{:S(2)}, u32[]{:S(2)}) async-start(bf16[16,172,1024]{2,1,0:T(8,128)(2,1)} %fusion.22), calls=%async_computation.4 | async-start | bytes 11534336 | tf_op jit(solution)/shard_map/all_to_all | solution.py:253
  284.7 92.7 %all-to-all-start.1 = ((bf16[16,172,1024]{2,1,0:T(8,128)(2,1)}), bf16[16,172,1024]{2,1,0:T(8,128)(2,1)}, u32[]{:S(2)}, u32[]{:S(2)}) async-start(bf16[16,172,1024]{2,1,0:T(8,128)(2,1)} %fusion.19), calls=%async_computation.1 | async-start | bytes 11534336 | tf_op jit(solution)/shard_map/all_to_all | solution.py:253
  377.4 92.8 %all-to-all-start.5 = ((bf16[16,172,1024]{2,1,0:T(8,128)(2,1)}), bf16[16,172,1024]{2,1,0:T(8,128)(2,1)}, u32[]{:S(2)}, u32[]{:S(2)}) async-start(bf16[16,172,1024]{2,1,0:T(8,128)(2,1)} %convolution_convert_fusion), calls=%async_computation.5 | async-start | bytes 11534336 | tf_op jit(solution)/shard_map/all_to_all | solution.py:261
  396.1 78.6 %copy-start.17 = (bf16[516,8]{0,1:T(8,128)(2,1)S(1)}, bf16[516,8]{0,1:T(8,128)(2,1)}, u32[]{:S(2)}) copy-start(bf16[516,8]{0,1:T(8,128)(2,1)} %param.29) | copy-start | bytes 24772
  396.1 78.6 %copy-start.15 = (s32[516,8]{0,1:T(8,128)S(1)}, s32[516,8]{0,1:T(8,128)}, u32[]{:S(2)}) copy-start(s32[516,8]{0,1:T(8,128)} %param.28) | copy-start | bytes 49540
  396.1 78.7 %copy-start.9 = (s32[32,516]{1,0:T(8,128)S(1)}, s32[32,516]{1,0:T(8,128)}, u32[]{:S(2)}) copy-start(s32[32,516]{1,0:T(8,128)} %copy-done.8) | copy-start | bytes 198148
  396.1 78.7 %copy-start.12 = (pred[516,32]{0,1:T(8,128)(4,1)S(1)}, pred[516,32]{0,1:T(8,128)(4,1)}, u32[]{:S(2)}) copy-start(pred[516,32]{0,1:T(8,128)(4,1)} %copy-done.11) | copy-start | bytes 49540
  470.2 92.7 %all-to-all-start.3 = ((bf16[16,172,1024]{2,1,0:T(8,128)(2,1)}), bf16[16,172,1024]{2,1,0:T(8,128)(2,1)}, u32[]{:S(2)}, u32[]{:S(2)}) async-start(bf16[16,172,1024]{2,1,0:T(8,128)(2,1)} %convolution_convert_fusion.1), calls=%async_computation.3 | async-start | bytes 11534336 | tf_op jit(solution)/shard_map/all_to_all | solution.py:261
  483.3 79.6 %copy-start.23 = (bf16[516,1024]{1,0:T(8,128)(2,1)S(1)}, bf16[516,1024]{1,0:T(8,128)(2,1)}, u32[]{:S(2)}) copy-start(bf16[516,1024]{1,0:T(8,128)(2,1)} %copy-done.21) | copy-start | bytes 3170308
  562.9 8.7 %copy-start.1 = (bf16[4,1024]{1,0:T(4,128)(2,1)S(1)}, bf16[4,1024]{1,0:T(4,128)(2,1)}, u32[]{:S(2)}) copy-start(bf16[4,1024]{1,0:T(4,128)(2,1)} %param.16) | copy-start | bytes 24580
  (10 other events, 28.0 us)
Sparse Core Ops, SparseCore 0:
  13.9 39.4 all-gather.4
  83.4 51.0 all-gather.6

commit v12 on v11

--- a/solution.py
+++ b/solution.py
@@ -187,9 +187,10 @@
         return both.reshape((group_count, local_experts) + weights.shape[1:])
 
     weight_rows = jnp.concatenate([owner_major(gate_up), owner_major(down_weight)], axis=2)
-    slot_rows, weight_rows, routes, prior_cache, dec_cache = lax.optimization_barrier(
-        (slot_rows, weight_rows, routes, prior_cache, dec_cache)
-    )
+    weight_rows, routes, prior_cache, dec_cache = lax.optimization_barrier(
+        (weight_rows, routes, prior_cache, dec_cache)
+    )
+    slot_rows, weight_rows = lax.optimization_barrier((slot_rows, weight_rows))
     layer_input = jnp.concatenate([pre_tokens, slot_rows], axis=0)
     rows_dev = layer_input.shape[0]
     normed = root_norm(layer_input.astype(jnp.float32), attn_gain).astype(jnp.bfloat16)

time: 586 us -> 591 us (level)
  waiting for transfers between devices: 346 us -> 352 us
    unnamed x52 -> x56, local copies, waits for them, and re-layouts: 12.2 us -> 12.2 us
  transfers between devices with their start and end apart: 10 -> 10, of which waited for: 7 -> 7; matrix products, arithmetic and copies ran while one was open for 29% -> 28% of each run, Pallas kernels for 0% -> 0%
where the time goes in v12:
time: 591 us; the launch traced here: 582 us
  waiting for transfers between devices  352 us (60%)
  matrix products  110 us (19%)
  local copies, waits for them, and re-layouts  41.3 us (7%)
  starting transfers between devices  37 us (6%)
  other arithmetic  26.6 us (5%)
  between operations  14.8 us (3%)
    all_to_all x2, waiting for transfers between devices, local(): lax.all_to_all(outbound, 'dl', split_axis=0, concat_axis=0, tiled=True)  148 us
    all_to_all x2, waiting for transfers between devices, local(): lax.all_to_all(expert_out, 'dl', split_axis=0, concat_axis=0, tiled=True)  146 us
    all_to_all x1, waiting for transfers between devices, local(): lax.all_to_all(weight_rows, dp, split_axis=0, concat_axis=0, tiled=True)  44 us
    sub x1, matrix products, prefill_attention(): expo = jnp.exp(scores - highest)  24.2 us
    dot_general x1, matrix products, prefill_attention(): jnp.einsum('gpck,gkh->cgph', weights, all_values, preferred_element_type=...  18.5 us
    dot_general x2, matrix products, local(): jnp.einsum('snd,df->snf', arrived, full_gu[l], preferred_element_type=jnp...  17.2 us
    dot_general x2, matrix products, local(): jnp.einsum('ecr,ecd->rd', combine_table[picked], returned, preferred_elem...  16.1 us
    dot_general x2, matrix products, local(): jnp.einsum('ecr,rd->ecd', table, normed_moe, preferred_element_type=jnp.f...  15.4 us
  transfers between devices with their start and end apart: 10, of which 7 were waited for; matrix products, arithmetic and copies ran while one was open for 28% of the time, Pallas kernels for 0%

profile of v12, /device:TPU:23, one launch (start us, length us, event | category | flops | bytes accessed | tf_op | source)
XLA Modules:
  0.0 582.0 jit_solution(4786358333359672636)
XLA Ops:
  6.6 5.4 collective-permute-done
  16.5 9.7 %all-to-all-start = ((bf16[32,2,512]{2,1,0:T(2,128)(2,1)}), bf16[32,2,512]{2,1,0:T(2,128)(2,1)S(1)}, u32[]{:S(2)}, u32[]{:S(2)}) async-start(bf16[32,2,512]{2,1,0:T(2,128)(2,1)} %reshape.494), calls=%async_computation | async-start | bytes 131072 | tf_op jit(solution)/shard_map/all_to_all | solution.py:163
  42.7 4.8 fusion.6
  51.1 6.2 %all-to-all-start.2 = ((bf16[32,2,48,1024]{3,2,1,0:T(8,128)(2,1)}), bf16[32,2,48,1024]{3,2,1,0:T(8,128)(2,1)}, u32[]{:S(2)}, u32[]{:S(2)}) async-start(bf16[32,2,48,1024]{3,2,1,0:T(8,128)(2,1)} %pad_maximum_fusion), calls=%async_computation.2 | async-start | bytes 12582912 | tf_op jit(solution)/shard_map/all_to_all | solution.py:219
  67.5 5.5 copy.102
  86.4 24.2 %fusion.82 = (f32[8,2,512]{2,1,0:T(2,128)S(1)}, f32[8,2,512,1536]{2,3,1,0:T(8,128)}) fusion(pred[512,1536]{0,1:T(8,128)(4,1)} %fusion.25, bf16[8,512,64]{1,2,0:T(8,128)(2,1)} %maximum_bitcast_fusion.13, bf16[8,1024,64]{1,2,0:T(8,128)(2,1)} %get-tuple-element.26, bf16[512,8,2,32]{0,3,2,1:T(8,128)(2,1)} %get-tuple-element.24, ...), kind=kOutput, calls=%fused_computation.159 | convolution fusion | flops 1666188800 | bytes 53772288 | tf_op jit(solution)/shard_map/sub | solution.py:60
  110.6 18.5 %fusion.39 = bf16[8,64,2,512]{3,1,2,0:T(8,128)(2,1)} fusion(f32[8,2,512,1536]{2,3,1,0:T(8,128)} %get-tuple-element.44, f32[8,2,512]{2,1,0:T(2,128)S(1)} %get-tuple-element.43, bf16[8,512,64]{1,2,0:T(8,128)(2,1)S(1)} %copy-done.11, bf16[8,1024,64]{1,2,0:T(8,128)(2,1)S(1)} %copy-done.8), kind=kOutput, calls=%fused_computation.55 | convolution fusion | flops 1639448576 | bytes 52985856 | tf_op jit(solution)/shard_map/gpck,gkh->cgph/dot_general | solution.py:62
  129.1 7.9 %all-gather.7.cloned.1.call-done = bf16[1024,32,32]{0,2,1:T(8,128)(2,1)} async-done(((bf16[1024,2,32]{0,2,1:T(8,128)(2,1)}), bf16[1024,32,32]{0,2,1:T(8,128)(2,1)}) %all-gather.7.cloned.1.call-update) | async-done | bytes 2097168 | tf_op jit(solution)/shard_map/all_gather | solution.py:210
  141.5 7.2 %fusion.22 = bf16[16,172,1024]{2,1,0:T(8,128)(2,1)} fusion(pred[32,172,516]{2,1,0:T(8,128)(4,1)S(1)} %copy-done.4, bf16[516,1024]{1,0:T(8,128)(2,1)S(1)} %get-tuple-element.46, f32[1024]{0:T(1024)S(1)} %copy-done.19, f32[516]{0:T(1024)S(1)} %add_rsqrt_fusion, bf16[4,1024]{1,0:T(4,128)(2,1)S(1)} %convolution_convert_fusion.4, bf16[512,1024]{1,0:T(8,128)(2,1)S(1)} %copy-done.7), kind=kOutput, calls=%fused_computation.29 | convolution fusion | flops 2915799040 | bytes 9568256 | tf_op jit(solution)/shard_map/ecr,rd->ecd/dot_general | solution.py:250
  148.7 44.0 %all-to-all-done.2 = bf16[32,2,48,1024]{3,2,1,0:T(8,128)(2,1)} async-done(((bf16[32,2,48,1024]{3,2,1,0:T(8,128)(2,1)}), bf16[32,2,48,1024]{3,2,1,0:T(8,128)(2,1)}, u32[]{:S(2)}, u32[]{:S(2)}) %all-to-all-start.2) | async-done | bytes 6291488 | tf_op jit(solution)/shard_map/all_to_all | solution.py:219
  192.7 6.8 %all-to-all-start.4 = ((bf16[16,172,1024]{2,1,0:T(8,128)(2,1)}), bf16[16,172,1024]{2,1,0:T(8,128)(2,1)}, u32[]{:S(2)}, u32[]{:S(2)}) async-start(bf16[16,172,1024]{2,1,0:T(8,128)(2,1)} %fusion.22), calls=%async_computation.4 | async-start | bytes 11534336 | tf_op jit(solution)/shard_map/all_to_all | solution.py:254
  199.5 8.2 %fusion.19 = bf16[16,172,1024]{2,1,0:T(8,128)(2,1)} fusion(pred[32,172,516]{2,1,0:T(8,128)(4,1)} %fusion.6, bf16[516,1024]{1,0:T(8,128)(2,1)S(1)} %copy-done.24, f32[1024]{0:T(1024)S(1)} %copy-done.19, f32[516]{0:T(1024)S(1)} %add_rsqrt_fusion, bf16[4,1024]{1,0:T(4,128)(2,1)S(1)} %convolution_convert_fusion.4, bf16[512,1024]{1,0:T(8,128)(2,1)S(1)} %copy-done.7), kind=kOutput, calls=%fused_computation.28 | convolution fusion | flops 2915799040 | bytes 9558032 | tf_op jit(solution)/shard_map/ecr,rd->ecd/dot_general | solution.py:250
  207.7 80.5 %all-to-all-done.4 = bf16[16,172,1024]{2,1,0:T(8,128)(2,1)} async-done(((bf16[16,172,1024]{2,1,0:T(8,128)(2,1)}), bf16[16,172,1024]{2,1,0:T(8,128)(2,1)}, u32[]{:S(2)}, u32[]{:S(2)}) %all-to-all-start.4) | async-done | bytes 5636128 | tf_op jit(solution)/shard_map/all_to_all | solution.py:254
  299.6 8.3 %fusion.33 = f32[16,172,1024]{2,1,0:T(8,128)S(1)} fusion(bf16[16,172,1024]{2,1,0:T(8,128)(2,1)} %all-to-all-done.4, bf16[1,2,1024,1024]{3,2,1,0:T(8,128)(2,1)S(1)} %bitcast.161), kind=kOutput, calls=%fused_computation.46 | convolution fusion | flops 5771362304 | bytes 19005440 | tf_op jit(solution)/shard_map/snd,df->snf/dot_general | solution.py:255
  307.9 5.1 convolution_convert_fusion
  313.0 67.8 %all-to-all-done.1 = bf16[16,172,1024]{2,1,0:T(8,128)(2,1)} async-done(((bf16[16,172,1024]{2,1,0:T(8,128)(2,1)}), bf16[16,172,1024]{2,1,0:T(8,128)(2,1)}, u32[]{:S(2)}, u32[]{:S(2)}) %all-to-all-start.1) | async-done | bytes 5636128 | tf_op jit(solution)/shard_map/all_to_all | solution.py:254
  380.8 4.7 all-to-all-start.5
  385.5 8.9 %fusion.34 = f32[16,172,1024]{2,1,0:T(8,128)S(1)} fusion(bf16[16,172,1024]{2,1,0:T(8,128)(2,1)} %all-to-all-done.1, bf16[1,2,1024,1024]{3,2,1,0:T(8,128)(2,1)} %bitcast.162), kind=kOutput, calls=%fused_computation.49 | convolution fusion | flops 5771362304 | bytes 19136512 | tf_op jit(solution)/shard_map/snd,df->snf/dot_general | solution.py:255
  394.4 5.1 convolution_convert_fusion.1
  399.6 74.1 %all-to-all-done.5 = bf16[16,172,1024]{2,1,0:T(8,128)(2,1)} async-done(((bf16[16,172,1024]{2,1,0:T(8,128)(2,1)}), bf16[16,172,1024]{2,1,0:T(8,128)(2,1)}, u32[]{:S(2)}, u32[]{:S(2)}) %all-to-all-start.5) | async-done | bytes 5636128 | tf_op jit(solution)/shard_map/all_to_all | solution.py:262
  478.3 5.5 select_convert_fusion
  486.7 7.4 %fusion.15 = f32[516,1024,1]{1,0,2:T(8,128)} fusion(bf16[16,172,1024]{2,1,0:T(8,128)(2,1)} %all-to-all-done.5, bf16[32,172,516]{2,1,0:T(8,128)(2,1)S(1)} %select_convert_fusion), kind=kOutput, calls=%fused_computation.24 | convolution fusion | flops 2908225536 | bytes 11354112 | tf_op jit(solution)/shard_map/ecr,ecd->rd/dot_general | solution.py:264
  494.1 72.2 %all-to-all-done.3 = bf16[16,172,1024]{2,1,0:T(8,128)(2,1)} async-done(((bf16[16,172,1024]{2,1,0:T(8,128)(2,1)}), bf16[16,172,1024]{2,1,0:T(8,128)(2,1)}, u32[]{:S(2)}, u32[]{:S(2)}) %all-to-all-start.3) | async-done | bytes 5636128 | tf_op jit(solution)/shard_map/all_to_all | solution.py:262
  566.3 8.7 %fusion.32 = bf16[516,1024]{1,0:T(8,128)(2,1)} fusion(f32[516,1024,1]{1,0,2:T(8,128)} %fusion.15, bf16[516,1024]{1,0:T(8,128)(2,1)S(1)} %copy-done.25, bf16[16,172,1024]{2,1,0:T(8,128)(2,1)} %all-to-all-done.3, bf16[32,172,516]{2,1,0:T(8,128)(2,1)} %copy-done.2, bf16[4,1024]{1,0:T(4,128)(2,1)S(1)} %convolution_convert_fusion.4, ...), kind=kOutput, calls=%fused_computation.42 | convolution fusion | flops 2912980992 | bytes 14671872 | tf_op jit(solution)/shard_map/ecr,ecd->rd/dot_general | solution.py:264
  (134 shorter events, 70.6 us)
Async XLA Ops:
  6.5 8.0 %copy-start = (bf16[4,1024]{1,0:T(4,128)(2,1)S(1)}, bf16[4,1024]{1,0:T(4,128)(2,1)}, u32[]{:S(2)}) copy-start(bf16[4,1024]{1,0:T(4,128)(2,1)} %param.16) | copy-start | bytes 24580
  6.5 51.3 %all-gather.5.cloned.1.call-start = ((), (), s32[]{:S(2)}) async-start(), calls=%async_computation.6 | async-start | bytes 4456448 | tf_op jit(solution)/shard_map/all_gather | solution.py:201
  6.5 5.5 collective-permute-start
  16.5 34.4 %all-to-all-start = ((bf16[32,2,512]{2,1,0:T(2,128)(2,1)}), bf16[32,2,512]{2,1,0:T(2,128)(2,1)S(1)}, u32[]{:S(2)}, u32[]{:S(2)}) async-start(bf16[32,2,512]{2,1,0:T(2,128)(2,1)} %reshape.494), calls=%async_computation | async-start | bytes 131072 | tf_op jit(solution)/shard_map/all_to_all | solution.py:163
  26.2 24.0 %collective-permute-start.1 = (bf16[1024,32]{0,1:T(8,128)(2,1)}, bf16[1024,32]{0,1:T(8,128)(2,1)S(1)}, u32[]{:S(2)}, u32[]{:S(2)}) collective-permute-start(bf16[1024,32]{0,1:T(8,128)(2,1)} %param.25), channel_id=1, source_target_pairs={{0,16},{16,0},{1,17},{17,1},{2,18},{18,2},{3,19},{19,3},{4,20},{20... | collective-permute-start | bytes 196616 | tf_op jit(solution)/shard_map/ppermute | solution.py:116
  36.1 11.4 %copy-start.12 = (pred[516,32]{0,1:T(8,128)(4,1)}, pred[516,32]{0,1:T(8,128)(4,1)S(1)}, u32[]{:S(2)}) copy-start(pred[516,32]{0,1:T(8,128)(4,1)S(1)} %fusion.53) | copy-start | bytes 49540
  38.8 8.8 %copy-start.9 = (s32[32,516]{1,0:T(8,128)}, s32[32,516]{1,0:T(8,128)S(1)}, u32[]{:S(2)}) copy-start(s32[32,516]{1,0:T(8,128)S(1)} %fusion.55) | copy-start | bytes 198148
  42.7 7.5 %copy-start.16 = (bf16[1024,32]{0,1:T(8,128)(2,1)S(1)}, bf16[1024,32]{0,1:T(8,128)(2,1)}, u32[]{:S(2)}) copy-start(bf16[1024,32]{0,1:T(8,128)(2,1)} %param.25) | copy-start | bytes 196612
  51.1 141.6 %all-to-all-start.2 = ((bf16[32,2,48,1024]{3,2,1,0:T(8,128)(2,1)}), bf16[32,2,48,1024]{3,2,1,0:T(8,128)(2,1)}, u32[]{:S(2)}, u32[]{:S(2)}) async-start(bf16[32,2,48,1024]{3,2,1,0:T(8,128)(2,1)} %pad_maximum_fusion), calls=%async_computation.2 | async-start | bytes 12582912 | tf_op jit(solution)/shard_map/all_to_all | solution.py:219
  57.3 79.7 %all-gather.7.cloned.1.call-start = ((), (), s32[]{:S(2)}) async-start(), calls=%async_computation.7 | async-start | bytes 2228224 | tf_op jit(solution)/shard_map/all_gather | solution.py:210
  86.4 24.2 %copy-start.8 = (bf16[8,1024,64]{1,2,0:T(8,128)(2,1)S(1)}, bf16[8,1024,64]{1,2,0:T(8,128)(2,1)}, u32[]{:S(2)}) copy-start(bf16[8,1024,64]{1,2,0:T(8,128)(2,1)} %get-tuple-element.25) | copy-start | bytes 3145732
  86.4 24.2 %copy-start.11 = (bf16[8,512,64]{1,2,0:T(8,128)(2,1)S(1)}, bf16[8,512,64]{1,2,0:T(8,128)(2,1)}, u32[]{:S(2)}) copy-start(bf16[8,512,64]{1,2,0:T(8,128)(2,1)} %fusion.54) | copy-start | bytes 1572868
  129.1 9.7 %copy-start.22 = (bf16[8,64,2,512]{3,1,2,0:T(8,128)(2,1)S(1)}, bf16[8,64,2,512]{3,1,2,0:T(8,128)(2,1)}, u32[]{:S(2)}) copy-start(bf16[8,64,2,512]{3,1,2,0:T(8,128)(2,1)} %fusion.39) | copy-start | bytes 3145732
  148.7 50.8 %copy-start.24 = (bf16[516,1024]{1,0:T(8,128)(2,1)S(1)}, bf16[516,1024]{1,0:T(8,128)(2,1)}, u32[]{:S(2)}) copy-start(bf16[516,1024]{1,0:T(8,128)(2,1)} %copy-done.23) | copy-start | bytes 3170308
  192.7 95.4 %all-to-all-start.4 = ((bf16[16,172,1024]{2,1,0:T(8,128)(2,1)}), bf16[16,172,1024]{2,1,0:T(8,128)(2,1)}, u32[]{:S(2)}, u32[]{:S(2)}) async-start(bf16[16,172,1024]{2,1,0:T(8,128)(2,1)} %fusion.22), calls=%async_computation.4 | async-start | bytes 11534336 | tf_op jit(solution)/shard_map/all_to_all | solution.py:254
  288.2 92.7 %all-to-all-start.1 = ((bf16[16,172,1024]{2,1,0:T(8,128)(2,1)}), bf16[16,172,1024]{2,1,0:T(8,128)(2,1)}, u32[]{:S(2)}, u32[]{:S(2)}) async-start(bf16[16,172,1024]{2,1,0:T(8,128)(2,1)} %fusion.19), calls=%async_computation.1 | async-start | bytes 11534336 | tf_op jit(solution)/shard_map/all_to_all | solution.py:254
  380.8 92.8 %all-to-all-start.5 = ((bf16[16,172,1024]{2,1,0:T(8,128)(2,1)}), bf16[16,172,1024]{2,1,0:T(8,128)(2,1)}, u32[]{:S(2)}, u32[]{:S(2)}) async-start(bf16[16,172,1024]{2,1,0:T(8,128)(2,1)} %convolution_convert_fusion), calls=%async_computation.5 | async-start | bytes 11534336 | tf_op jit(solution)/shard_map/all_to_all | solution.py:262
  399.5 78.6 %copy-start.17 = (bf16[516,8]{0,1:T(8,128)(2,1)S(1)}, bf16[516,8]{0,1:T(8,128)(2,1)}, u32[]{:S(2)}) copy-start(bf16[516,8]{0,1:T(8,128)(2,1)} %param.29) | copy-start | bytes 24772
  399.6 78.6 %copy-start.15 = (s32[516,8]{0,1:T(8,128)S(1)}, s32[516,8]{0,1:T(8,128)}, u32[]{:S(2)}) copy-start(s32[516,8]{0,1:T(8,128)} %param.28) | copy-start | bytes 49540
  399.6 78.7 %copy-start.10 = (s32[32,516]{1,0:T(8,128)S(1)}, s32[32,516]{1,0:T(8,128)}, u32[]{:S(2)}) copy-start(s32[32,516]{1,0:T(8,128)} %copy-done.9) | copy-start | bytes 198148
  399.6 78.7 %copy-start.13 = (pred[516,32]{0,1:T(8,128)(4,1)S(1)}, pred[516,32]{0,1:T(8,128)(4,1)}, u32[]{:S(2)}) copy-start(pred[516,32]{0,1:T(8,128)(4,1)} %copy-done.12) | copy-start | bytes 49540
  473.6 92.7 %all-to-all-start.3 = ((bf16[16,172,1024]{2,1,0:T(8,128)(2,1)}), bf16[16,172,1024]{2,1,0:T(8,128)(2,1)}, u32[]{:S(2)}, u32[]{:S(2)}) async-start(bf16[16,172,1024]{2,1,0:T(8,128)(2,1)} %convolution_convert_fusion.1), calls=%async_computation.3 | async-start | bytes 11534336 | tf_op jit(solution)/shard_map/all_to_all | solution.py:262
  486.7 79.6 %copy-start.25 = (bf16[516,1024]{1,0:T(8,128)(2,1)S(1)}, bf16[516,1024]{1,0:T(8,128)(2,1)}, u32[]{:S(2)}) copy-start(bf16[516,1024]{1,0:T(8,128)(2,1)} %copy-done.23) | copy-start | bytes 3170308
  566.3 8.7 %copy-start.1 = (bf16[4,1024]{1,0:T(4,128)(2,1)S(1)}, bf16[4,1024]{1,0:T(4,128)(2,1)}, u32[]{:S(2)}) copy-start(bf16[4,1024]{1,0:T(4,128)(2,1)} %param.16) | copy-start | bytes 24580
  (12 other events, 43.9 us)
Sparse Core Ops, SparseCore 0:
  13.9 39.4 all-gather.4
  80.9 56.0 all-gather.6
